TPU v7x, 256 devices: a whole 4x4x8 slice. The times are simulated.
256 devices in a mesh: row: 8 (over z_lo, y), col: 32 (over z_hi, x, core).
Axes of the slice: x: 4, y: 4, z: 8 (z_hi: 4, z_lo: 2; z = z_hi * 2 + z_lo), core: 2. Of those that a mesh axis runs over, the one named last changes fastest.
Arguments:
- strip: float32 [12, 2048, 2, 1024], P(None, 'col', None, 'row'), may hold values from -6 to 6
- lower: float32 [12, 2048, 2, 1024], P(None, 'col', None, 'row'), may hold values from -1.6 to 1.6, as said below
Outputs:
- reduced: float32 [12, 2048, 2, 1024], P(None, 'col', None, 'row')
Inputs may be any that keep to these rules, and one draw needn't show every extreme that they name: `lower`: in the first 2048 rows the diagonal lies between 0.8 and 1.6 and entries above it are zero.
All inputs are finite; a program needn't handle non-finite values.
Results may differ from a plain program's by a relative error of at most 0.00013.
Values sent between devices are 32-bit elements; how exact they have to be, the bound alone decides.
No kernel may reach another device: no remote copies, remote signals or barrier semaphores. Data moves between devices by JAX's collectives and lax.ppermute only.
A program may use at most 64 MiB of HBM per device.

v0:
```python
import jax
import jax.numpy as jnp
from jax import lax
from jax.sharding import PartitionSpec as P

highest = lax.Precision.HIGHEST


def spread(array, axis, root):
    mine = lax.axis_index(axis) == root
    return lax.psum(jnp.where(mine, array, jnp.zeros_like(array)), axis)


def times_rows(coeff, right_side):
    return jnp.dot(coeff, right_side, precision=highest, preferred_element_type=jnp.float32)


def times_rows_turned(coeff, right_turned):
    return lax.dot_general(
        coeff,
        right_turned,
        (((1,), (1,)), ((), ())),
        precision=highest,
        preferred_element_type=jnp.float32,
    )


def local(strip, lower):
    rounds = strip.shape[0]
    strip_width = strip.shape[1]
    row_run = strip.shape[3]
    row_count = lax.axis_size("row")
    block_size = row_run * row_count
    cols_here = rounds * strip_width
    trail_count = cols_here - strip_width
    local_strip = strip.reshape(cols_here, 2, row_run)
    left_part = local_strip[:, 0, :]
    right_part = local_strip[:, 1, :]
    gathered = lax.all_gather(lower[0], "col", axis=0, tiled=True)
    first_cols = gathered[:block_size, 0, :]
    cross_cols = gathered[block_size:, 0, :]
    second_cols = gathered[block_size:, 1, :]
    inverse_all = lax.all_gather(second_cols, "row", axis=1, tiled=True)
    mixed_cols = jnp.dot(
        inverse_all, cross_cols, precision=highest, preferred_element_type=jnp.float32
    )
    upper_half = lax.psum_scatter(
        times_rows_turned(first_cols, left_part), "row", scatter_dimension=0, tiled=True
    )
    carried = lax.psum_scatter(
        times_rows(cross_cols, upper_half), "row", scatter_dimension=0, tiled=True
    )
    remainder = right_part.T - carried
    lower_half = lax.psum_scatter(
        times_rows(second_cols, remainder), "row", scatter_dimension=0, tiled=True
    )
    solved = jnp.stack([upper_half.T, lower_half.T], axis=1)
    lead_rows = solved[:strip_width].reshape(strip_width, 2 * row_run)
    tail_rows = solved[strip_width:].reshape(trail_count, 2 * row_run)
    col_position = lax.axis_index("col")
    offset = col_position * strip_width
    part_block = offset // block_size
    inside = offset % block_size
    root_row = inside // row_run
    shift_in = inside % row_run
    zero_index = jnp.zeros((), jnp.int32)
    mirror_piece = lax.dynamic_slice(
        gathered, (zero_index, part_block, shift_in), (2 * block_size, 1, strip_width)
    )
    mirror_piece = mirror_piece.reshape(2 * block_size, strip_width)
    mirrored = spread(mirror_piece, "row", root_row)
    first_flag = (part_block == 0).astype(jnp.float32)
    second_flag = 1.0 - first_flag
    row_position = lax.axis_index("row")
    first_rows = lax.dynamic_slice_in_dim(mirrored, row_position * row_run, row_run, 0)
    partial_mix = jnp.dot(
        mixed_cols, first_rows, precision=highest, preferred_element_type=jnp.float32
    )
    chained = lax.psum(partial_mix, "row")
    coeff_whole = jnp.concatenate(
        [
            first_flag * mirrored[:block_size],
            second_flag * mirrored[block_size:] - first_flag * chained,
        ],
        axis=0,
    )
    solved_lead = lax.psum_scatter(
        times_rows(coeff_whole, lead_rows), "col", scatter_dimension=0, tiled=True
    )
    everything = lax.all_gather(solved_lead, "col", axis=0, tiled=True)
    left_rows = lower[1:].reshape(trail_count, 2 * row_run)
    grouped = everything.reshape(2, row_count, row_run, 2 * row_run).transpose(1, 0, 2, 3)
    swapped = lax.all_to_all(grouped, "row", split_axis=0, concat_axis=0, tiled=True)
    turned_block = swapped.reshape(row_count, 2, row_run, 2, row_run).transpose(0, 3, 4, 1, 2)
    turned_block = turned_block.reshape(row_count * 2 * row_run, 2 * row_run)
    summed = lax.psum_scatter(
        times_rows_turned(turned_block, left_rows), "row", scatter_dimension=0, tiled=True
    )
    update = summed.T
    reduced = jnp.concatenate([solved_lead, tail_rows - update], axis=0)
    return reduced.reshape(rounds, strip_width, 2, row_run)


def solution(mesh):
    in_specs = (P(None, "col", None, "row"), P(None, "col", None, "row"))
    out_specs = P(None, "col", None, "row")
    return jax.shard_map(local, mesh=mesh, in_specs=in_specs, out_specs=out_specs, check_vma=False)
```

profile of v0, /device:TPU:1, one launch (start us, length us, event | category | flops | bytes accessed | tf_op | source)
XLA Modules:
  0.0 760.2 jit_solution(14494232658817926773)
XLA Ops:
  6.5 1.5 slice_bitcast_fusion.3
  8.0 0.0 all-gather.8.cloned.1.call-update
  8.0 0.0 reduce-scatter.6.cloned.1.call-start
  8.1 1.2 copy.10
  9.3 59.5 %all-gather.8.cloned.1.call-done = f32[1,2048,2,128]{3,2,0,1:T(2,128)} async-done(((f32[1,64,2,128]{3,2,0,1:T(2,128)}), f32[1,2048,2,128]{3,2,0,1:T(2,128)}) %all-gather.8.cloned.1.call-update) | async-done | bytes 2097168 | tf_op jit(solution)/shard_map/all_gather | solution.py:39
  68.8 4.1 fusion.20
  73.0 4.3 fusion.14
  77.3 0.0 reduce-scatter.6.cloned.1.call-update
  77.3 0.0 all-gather.10.cloned.1.call-start
  77.4 0.7 all-gather.10.cloned.1.call-update
  78.0 0.0 all-reduce.3.cloned.1.call-start
  78.2 3.5 constant_dynamic-slice_fusion
  81.7 0.6 copy.19
  82.3 0.9 select_bitcast_fusion
  83.2 0.0 all-reduce.3.cloned.1.call-update
  83.2 0.0 reduce-scatter.8.cloned.1.call-start
  83.3 35.7 %reduce-scatter.6.cloned.1.call-done = f32[128,768]{1,0:T(8,128)} async-done(((f32[1024,768]{1,0:T(8,128)}), f32[128,768]{1,0:T(8,128)}) %reduce-scatter.6.cloned.1.call-update) | async-done | bytes 393232 | tf_op jit(solution)/shard_map/reduce_scatter | solution.py:47
  118.9 5.3 convolution_bitcast_fusion.1
  124.3 0.0 all-reduce.5.cloned.1.call-start
  124.3 97.1 %all-gather.10.cloned.1.call-done = f32[1024,1,1024]{2,1,0:T(1,128)} async-done(((f32[1024,1,128]{2,1,0:T(1,128)}), f32[1024,1,1024]{2,1,0:T(1,128)}) %all-gather.10.cloned.1.call-update) | async-done | bytes 4194320 | tf_op jit(solution)/shard_map/all_gather | solution.py:43
  221.5 5.7 fusion
  227.2 74.9 %all-reduce.3.cloned.1.call-done = f32[2048,64]{0,1:T(8,128)} async-done(((f32[2048,64]{0,1:T(8,128)}), f32[2048,64]{0,1:T(8,128)}) %all-reduce.3.cloned.1.call-update) | async-done | bytes 524304 | tf_op jit(solution)/shard_map/psum | solution.py:11
  302.1 2.2 fusion.16
  304.3 0.2 reduce-scatter.10.cloned.1.call-start
  304.5 49.9 %reduce-scatter.8.cloned.1.call-done = f32[128,768]{0,1:T(8,128)} async-done(((f32[1024,768]{0,1:T(8,128)}), f32[128,768]{0,1:T(8,128)}) %reduce-scatter.8.cloned.1.call-update) | async-done | bytes 393232 | tf_op jit(solution)/shard_map/reduce_scatter | solution.py:50
  354.4 5.3 convolution_bitcast_fusion
  359.8 0.0 reduce-scatter.12.cloned.1.call-start
  359.8 74.5 %all-reduce.5.cloned.1.call-done = f32[1024,64]{0,1:T(8,128)} async-done(((f32[1024,64]{0,1:T(8,128)}), f32[1024,64]{0,1:T(8,128)}) %all-reduce.5.cloned.1.call-update) | async-done | bytes 262160 | tf_op jit(solution)/shard_map/psum | solution.py:79
  434.3 1.0 slice_multiply_fusion.1
  435.3 50.9 %reduce-scatter.10.cloned.1.call-done = f32[128,768]{1,0:T(8,128)} async-done(((f32[1024,768]{1,0:T(8,128)}), f32[128,768]{1,0:T(8,128)}) %reduce-scatter.10.cloned.1.call-update) | async-done | bytes 393232 | tf_op jit(solution)/shard_map/reduce_scatter | solution.py:54
  486.2 0.8 pad_maximum_fusion.2
  487.0 3.2 fusion.8
  490.2 0.0 all-gather.6.cloned.1.call-start
  490.3 92.9 %reduce-scatter.12.cloned.1.call-done = f32[64,256]{1,0:T(8,128)} async-done(((f32[2048,256]{1,0:T(8,128)}), f32[64,256]{1,0:T(8,128)}) %reduce-scatter.12.cloned.1.call-update) | async-done | bytes 65552 | tf_op jit(solution)/shard_map/reduce_scatter | solution.py:87
  583.2 57.3 %all-gather.6.cloned.1.call-done = f32[2048,256]{1,0:T(8,128)} async-done(((f32[64,256]{1,0:T(8,128)}), f32[2048,256]{1,0:T(8,128)}) %all-gather.6.cloned.1.call-update) | async-done | bytes 2097168 | tf_op jit(solution)/shard_map/all_gather | solution.py:90
  640.5 3.1 copy.35
  643.6 4.3 all-to-all-start
  648.0 0.0 reduce-scatter.14.cloned.1.call-start
  648.0 26.2 %all-to-all-done = f32[8,2,128,256]{3,2,1,0:T(8,128)} async-done(((f32[8,2,128,256]{3,2,1,0:T(8,128)}), f32[8,2,128,256]{3,2,1,0:T(8,128)}, u32[]{:S(2)}, u32[]{:S(2)}) %all-to-all-start) | async-done | bytes 2097184 | tf_op jit(solution)/shard_map/all_to_all | solution.py:93
  674.2 2.8 copy.16
  677.1 6.8 fusion.3
  683.9 1.0 copy-done.2
  684.8 0.3 pad_maximum_fusion
  685.1 0.2 copy.14
  685.4 65.5 %reduce-scatter.14.cloned.1.call-done = f32[256,704]{0,1:T(8,128)} async-done(((f32[2048,704]{0,1:T(8,128)}), f32[256,704]{0,1:T(8,128)}) %reduce-scatter.14.cloned.1.call-update) | async-done | bytes 720912 | tf_op jit(solution)/shard_map/reduce_scatter | solution.py:96
  750.9 1.2 bitcast_subtract_fusion
  752.1 0.1 pad_maximum_fusion.1
  752.1 1.3 reshape.35
  (18 shorter events, 0.1 us)
Async XLA Ops:
  6.5 62.3 %all-gather.8.cloned.1.call-start = ((), (), s32[]{:S(2)}) async-start(), calls=%async_computation.14 | async-start | bytes 2162688 | tf_op jit(solution)/shard_map/all_gather | solution.py:39
  8.0 110.9 %reduce-scatter.6.cloned.1.call-start = ((), (), s32[]{:S(2)}) async-start(), calls=%async_computation.8 | async-start | bytes 3538944 | tf_op jit(solution)/shard_map/reduce_scatter | solution.py:47
  77.3 144.2 %all-gather.10.cloned.1.call-start = ((), (), s32[]{:S(2)}) async-start(), calls=%async_computation.15 | async-start | bytes 4718592 | tf_op jit(solution)/shard_map/all_gather | solution.py:43
  78.0 224.0 %all-reduce.3.cloned.1.call-start = ((), (), s32[]{:S(2)}) async-start(), calls=%async_computation.6 | async-start | bytes 1048576 | tf_op jit(solution)/shard_map/psum | solution.py:11
  83.2 271.2 %reduce-scatter.8.cloned.1.call-start = ((), (), s32[]{:S(2)}) async-start(), calls=%async_computation.9 | async-start | bytes 3538944 | tf_op jit(solution)/shard_map/reduce_scatter | solution.py:50
  124.3 310.0 %all-reduce.5.cloned.1.call-start = ((), (), s32[]{:S(2)}) async-start(), calls=%async_computation.7 | async-start | bytes 524288 | tf_op jit(solution)/shard_map/psum | solution.py:79
  124.3 230.0 %copy-start = (f32[1024,1,128]{2,1,0:T(1,128)S(1)}, f32[1024,1,128]{2,1,0:T(1,128)}, u32[]{:S(2)}) copy-start(f32[1024,1,128]{2,1,0:T(1,128)} %get-tuple-element.6) | copy-start | bytes 1572868
  304.3 181.9 %reduce-scatter.10.cloned.1.call-start = ((), (), s32[]{:S(2)}) async-start(), calls=%async_computation.10 | async-start | bytes 3538944 | tf_op jit(solution)/shard_map/reduce_scatter | solution.py:54
  354.4 79.9 %copy-start.3 = (f32[2048,64]{0,1:T(8,128)S(1)}, f32[2048,64]{0,1:T(8,128)}, u32[]{:S(2)}) copy-start(f32[2048,64]{0,1:T(8,128)} %all-reduce.3.cloned.1.call-done) | copy-start | bytes 1572868
  359.7 126.5 %copy-start.1 = (f32[128,768]{1,0:T(8,128)S(1)}, f32[128,768]{1,0:T(8,128)}, u32[]{:S(2)}) copy-start(f32[128,768]{1,0:T(8,128)} %reduce-scatter.6.cloned.1.call-done) | copy-start | bytes 1179652
  359.8 223.5 %reduce-scatter.12.cloned.1.call-start = ((), (), s32[]{:S(2)}) async-start(), calls=%async_computation.11 | async-start | bytes 2162688 | tf_op jit(solution)/shard_map/reduce_scatter | solution.py:87
  490.2 150.3 %all-gather.6.cloned.1.call-start = ((), (), s32[]{:S(2)}) async-start(), calls=%async_computation.12 | async-start | bytes 2162688 | tf_op jit(solution)/shard_map/all_gather | solution.py:90
  643.6 30.6 %all-to-all-start = ((f32[8,2,128,256]{3,2,1,0:T(8,128)}), f32[8,2,128,256]{3,2,1,0:T(8,128)}, u32[]{:S(2)}, u32[]{:S(2)}) async-start(f32[8,2,128,256]{3,2,1,0:T(8,128)} %bitcast.59), calls=%async_computation.4 | async-start | bytes 4194304 | tf_op jit(solution)/shard_map/all_to_all | solution.py:93
  648.0 29.1 %slice-start = ((f32[12,64,2,128]{3,2,1,0:T(2,128)}), f32[11,64,2,128]{3,2,1,0:T(2,128)S(1)}, s32[]{:S(2)}) async-start(f32[12,64,2,128]{3,2,1,0:T(2,128)} %param.3), calls=%async_computation.16 | async-start | bytes 1441792 | tf_op jit(solution)/shard_map/slice | solution.py:91
  648.0 102.9 %reduce-scatter.14.cloned.1.call-start = ((), (), s32[]{:S(2)}) async-start(), calls=%async_computation.13 | async-start | bytes 6488064 | tf_op jit(solution)/shard_map/reduce_scatter | solution.py:96
  683.8 1.0 copy-start.2
  684.8 67.2 %copy-start.4 = (f32[64,256]{1,0:T(8,128)S(1)}, f32[64,256]{1,0:T(8,128)}, u32[]{:S(2)}) copy-start(f32[64,256]{1,0:T(8,128)} %reduce-scatter.12.cloned.1.call-done) | copy-start | bytes 196612
Sparse Core Ops, SparseCore 0:
  9.9 58.8 all-gather.7
  77.4 41.4 reduce-scatter.5
  120.6 100.7 all-gather.9
  224.0 78.0 all-reduce.2
  304.7 49.6 reduce-scatter.7
  357.0 77.2 all-reduce.4
  436.8 49.2 reduce-scatter.9
  490.4 92.8 reduce-scatter.11
  585.8 54.6 all-gather.5
  684.0 66.8 reduce-scatter.13
where the time goes:
time: 761 us; the launch traced here: 760 us
  waiting for transfers between devices  685 us (90%)
  matrix products  32.9 us (4%)
  local copies, waits for them, and re-layouts  19.4 us (3%)
  between operations  13.7 us (2%)
    all_gather x1, waiting for transfers between devices, local(): inverse_all = lax.all_gather(second_cols, 'row', axis=1, tiled=True)  97.1 us
    reduce_scatter x1, waiting for transfers between devices, local(): lax.psum_scatter(times_rows(coeff_whole, lead_rows), 'col', scatter_dimen...  92.9 us
    psum x1, waiting for transfers between devices, spread(): return lax.psum(jnp.where(mine, array, jnp.zeros_like(array)), axis)  74.9 us
    psum x1, waiting for transfers between devices, local(): chained = lax.psum(partial_mix, 'row')  74.5 us
    reduce_scatter x1, waiting for transfers between devices, local(): lax.psum_scatter(times_rows_turned(turned_block, left_rows), 'row', scatt...  65.5 us
    all_gather x1, waiting for transfers between devices, local(): gathered = lax.all_gather(lower[0], 'col', axis=0, tiled=True)  59.5 us
    all_gather x1, waiting for transfers between devices, local(): everything = lax.all_gather(solved_lead, 'col', axis=0, tiled=True)  57.3 us
    reduce_scatter x1, waiting for transfers between devices, local(): lax.psum_scatter(times_rows(second_cols, remainder), 'row', scatter_dimen...  50.9 us
  transfers between devices with their start and end apart: 11, of which 11 were waited for; matrix products, arithmetic and copies ran while one was open for 3% of the time, Pallas kernels for 0%

commit v1 on v0

v1 whole, which is shorter than its diff:
```python
import jax
import jax.numpy as jnp
from jax import lax
from jax.sharding import PartitionSpec as P

highest = lax.Precision.HIGHEST


def times_rows(coeff, right_side):
    return jnp.dot(coeff, right_side, precision=highest, preferred_element_type=jnp.float32)


def times_rows_turned(coeff, right_turned):
    return lax.dot_general(
        coeff,
        right_turned,
        (((1,), (1,)), ((), ())),
        precision=highest,
        preferred_element_type=jnp.float32,
    )


def local(strip, lower):
    rounds = strip.shape[0]
    strip_width = strip.shape[1]
    row_run = strip.shape[3]
    row_count = lax.axis_size("row")
    col_count = lax.axis_size("col")
    block_size = row_run * row_count
    cols_here = rounds * strip_width
    trail_count = cols_here - strip_width
    share = block_size // col_count
    local_strip = strip.reshape(cols_here, 2, row_run)
    left_part = local_strip[:, 0, :]
    right_part = local_strip[:, 1, :]
    gathered = lax.all_gather(lower[0], "col", axis=0, tiled=True)
    first_cols = gathered[:block_size, 0, :]
    cross_cols = gathered[block_size:, 0, :]
    second_cols = gathered[block_size:, 1, :]

    col_position = lax.axis_index("col")
    start = col_position * share
    top_rows = lax.dynamic_slice_in_dim(gathered, start, share, 0)
    bottom_rows = lax.dynamic_slice_in_dim(gathered, block_size + start, share, 0)
    picked = jnp.concatenate([top_rows, bottom_rows], axis=0)
    picked_rows = lax.all_gather(picked, "row", axis=2, tiled=True)
    first_rows = picked_rows[:share, 0, :]
    cross_rows = picked_rows[share:, 0, :]
    second_rows = picked_rows[share:, 1, :]

    upper_half = lax.psum_scatter(
        times_rows_turned(first_cols, left_part), "row", scatter_dimension=0, tiled=True
    )
    carried = lax.psum_scatter(
        times_rows(cross_cols, upper_half), "row", scatter_dimension=0, tiled=True
    )
    remainder = right_part.T - carried
    lower_half = lax.psum_scatter(
        times_rows(second_cols, remainder), "row", scatter_dimension=0, tiled=True
    )
    solved = jnp.stack([upper_half.T, lower_half.T], axis=1)
    lead_rows = solved[:strip_width]
    tail_rows = solved[strip_width:].reshape(trail_count, 2 * row_run)

    lead_all = lax.all_gather(lead_rows, "col", axis=0, tiled=True)
    lead_all = lead_all.reshape(2 * block_size, 2 * row_run)
    first_piece = times_rows(first_rows, lead_all[:block_size])
    first_block = lax.all_gather(first_piece, "col", axis=0, tiled=True)
    lead_second = lax.dynamic_slice_in_dim(lead_all, block_size + start, share, 0)
    diff_piece = lead_second - times_rows(cross_rows, first_block)
    diff_block = lax.all_gather(diff_piece, "col", axis=0, tiled=True)
    second_piece = times_rows(second_rows, diff_block)
    second_block = lax.all_gather(second_piece, "col", axis=0, tiled=True)
    everything = jnp.concatenate([first_block, second_block], axis=0)
    solved_lead = lax.dynamic_slice_in_dim(everything, col_position * strip_width, strip_width, 0)

    left_rows = lower[1:].reshape(trail_count, 2 * row_run)
    grouped = everything.reshape(2, row_count, row_run, 2 * row_run).transpose(1, 0, 2, 3)
    swapped = lax.all_to_all(grouped, "row", split_axis=0, concat_axis=0, tiled=True)
    turned_block = swapped.reshape(row_count, 2, row_run, 2, row_run).transpose(0, 3, 4, 1, 2)
    turned_block = turned_block.reshape(row_count * 2 * row_run, 2 * row_run)
    summed = lax.psum_scatter(
        times_rows_turned(turned_block, left_rows), "row", scatter_dimension=0, tiled=True
    )
    update = summed.T
    reduced = jnp.concatenate([solved_lead, tail_rows - update], axis=0)
    return reduced.reshape(rounds, strip_width, 2, row_run)


def solution(mesh):
    in_specs = (P(None, "col", None, "row"), P(None, "col", None, "row"))
    out_specs = P(None, "col", None, "row")
    return jax.shard_map(local, mesh=mesh, in_specs=in_specs, out_specs=out_specs, check_vma=False)
```

time: 761 us -> 563 us (0.74)
  waiting for transfers between devices: 685 us -> 476 us
  blocking collectives: 0 us -> 16.4 us
    psum x2 -> x0, waiting for transfers between devices: 149 us -> none  [the longest x1 74.9 us: spread(): return lax.psum(jnp.where(mine, array, jnp.zeros_like(array)), axis)]
    reduce_scatter x1 -> x0, waiting for transfers between devices: 92.9 us -> none  [local(): lax.psum_scatter(times_rows(coeff_whole, lead_rows), 'col', scatter_dimen...]
    all_gather x2 -> x4, waiting for transfers between devices: 154 us -> 188 us  [the longest x1 49.6 us: local(): diff_block = lax.all_gather(diff_piece, 'col', axis=0, tiled=True)]
    all_gather x0 -> x1, blocking collectives: none -> 16.4 us  [local(): picked_rows = lax.all_gather(picked, 'row', axis=2, tiled=True)]
    dot_general x2 -> x0, matrix products: 7.9 us -> none  [the longest x1 5.73 us: local(): jnp.dot(inverse_all, cross_cols, precision=highest, preferred_element_typ...]
    dot_general x3 -> x5, matrix products: 13.9 us -> 17.6 us  [times_rows(): jnp.dot(coeff, right_side, precision=highest, preferred_element_type=jnp....]
  transfers between devices with their start and end apart: 11 -> 10, of which waited for: 11 -> 10; matrix products, arithmetic and copies ran while one was open for 3% -> 1% of each run, Pallas kernels for 0% -> 0%
where the time goes in v1:
time: 563 us
  waiting for transfers between devices  476 us (85%)
  matrix products  28.5 us (5%)
  local copies, waits for them, and re-layouts  20.7 us (4%)
  blocking collectives  16.4 us (3%)
  between operations  13.3 us (2%)
    reduce_scatter x1, waiting for transfers between devices, local(): lax.psum_scatter(times_rows_turned(turned_block, left_rows), 'row', scatt...  64.9 us
    all_gather x1, waiting for transfers between devices, local(): gathered = lax.all_gather(lower[0], 'col', axis=0, tiled=True)  59.5 us
    all_gather x1, waiting for transfers between devices, local(): diff_block = lax.all_gather(diff_piece, 'col', axis=0, tiled=True)  49.6 us
    all_gather x1, waiting for transfers between devices, local(): second_block = lax.all_gather(second_piece, 'col', axis=0, tiled=True)  49.5 us
    reduce_scatter x1, waiting for transfers between devices, local(): lax.psum_scatter(times_rows(second_cols, remainder), 'row', scatter_dimen...  48.3 us
    reduce_scatter x1, waiting for transfers between devices, local(): lax.psum_scatter(times_rows(cross_cols, upper_half), 'row', scatter_dimen...  48.2 us
    all_gather x1, waiting for transfers between devices, local(): first_block = lax.all_gather(first_piece, 'col', axis=0, tiled=True)  47.4 us
    reduce_scatter x1, waiting for transfers between devices, local(): lax.psum_scatter(times_rows_turned(first_cols, left_part), 'row', scatter...  41.6 us
  transfers between devices with their start and end apart: 10, of which 10 were waited for; matrix products, arithmetic and copies ran while one was open for 1% of the time, Pallas kernels for 0%

profile of v1, /device:TPU:1, one launch (start us, length us, event | category | flops | bytes accessed | tf_op | source)
XLA Modules:
  0.0 562.7 jit_solution(11136738738206330280)
XLA Ops:
  6.5 1.5 slice_bitcast_fusion.3
  8.0 0.0 reduce-scatter.5.cloned.1.call-start
  8.1 1.2 copy.9
  9.3 59.5 %all-gather.15.cloned.1.call-done = f32[1,2048,2,128]{3,2,0,1:T(2,128)} async-done(((f32[1,64,2,128]{3,2,0,1:T(2,128)}), f32[1,2048,2,128]{3,2,0,1:T(2,128)}) %all-gather.15.cloned.1.call-update) | async-done | bytes 2097168 | tf_op jit(solution)/shard_map/all_gather | solution.py:36
  68.8 3.2 fusion.18
  72.1 4.3 fusion.10
  76.4 0.0 reduce-scatter.7.cloned.1.call-start
  76.4 41.6 %reduce-scatter.5.cloned.1.call-done = f32[128,768]{1,0:T(8,128)} async-done(((f32[1024,768]{1,0:T(8,128)}), f32[128,768]{1,0:T(8,128)}) %reduce-scatter.5.cloned.1.call-update) | async-done | bytes 393232 | tf_op jit(solution)/shard_map/reduce_scatter | solution.py:51
  118.0 5.3 convolution_bitcast_fusion.1
  123.3 0.0 reduce-scatter.9.cloned.1.call-start
  123.4 48.2 %reduce-scatter.7.cloned.1.call-done = f32[128,768]{0,1:T(8,128)} async-done(((f32[1024,768]{0,1:T(8,128)}), f32[128,768]{0,1:T(8,128)}) %reduce-scatter.7.cloned.1.call-update) | async-done | bytes 393232 | tf_op jit(solution)/shard_map/reduce_scatter | solution.py:54
  171.6 5.3 convolution_bitcast_fusion
  176.9 0.0 all-gather.7.cloned.1.call-start
  177.0 48.3 %reduce-scatter.9.cloned.1.call-done = f32[128,768]{1,0:T(8,128)} async-done(((f32[1024,768]{1,0:T(8,128)}), f32[128,768]{1,0:T(8,128)}) %reduce-scatter.9.cloned.1.call-update) | async-done | bytes 393232 | tf_op jit(solution)/shard_map/reduce_scatter | solution.py:58
  225.2 0.8 pad_maximum_fusion.2
  226.1 0.7 copy.11
  226.8 0.0 all-gather.9.cloned.1.call-start
  226.9 0.8 dynamic-slice_bitcast_fusion.1
  227.7 16.4 %all_gather.19 = f32[64,2,1024]{2,1,0:T(2,128)S(1)} all-gather(f32[64,2,128]{2,1,0:T(2,128)S(1)} %pad_maximum_fusion.3), channel_id=1, replica_groups=mesh['row'=8,'col'=32] {'row'}, dimensions={2}, use_global_device_ids=true | all-gather | bytes 589824 | tf_op jit(solution)/shard_map/all_gather | solution.py:46
  244.1 1.0 fusion.19
  245.1 41.1 %all-gather.7.cloned.1.call-done = f32[2048,2,128]{2,1,0:T(2,128)} async-done(((f32[64,2,128]{2,1,0:T(2,128)}), f32[2048,2,128]{2,1,0:T(2,128)}) %all-gather.7.cloned.1.call-update) | async-done | bytes 2097168 | tf_op jit(solution)/shard_map/all_gather | solution.py:65
  286.2 1.2 slice-done
  287.4 2.1 fusion.3
  289.5 0.2 all-gather.11.cloned.1.call-start
  289.8 1.5 copy.51
  291.3 47.4 %all-gather.9.cloned.1.call-done = f32[1024,256]{1,0:T(8,128)} async-done(((f32[32,256]{1,0:T(8,128)}), f32[1024,256]{1,0:T(8,128)}) %all-gather.9.cloned.1.call-update) | async-done | bytes 1048592 | tf_op jit(solution)/shard_map/all_gather | solution.py:68
  338.7 2.5 convolution_subtract_fusion
  341.3 0.0 all-gather.13.cloned.1.call-start
  341.3 49.6 %all-gather.11.cloned.1.call-done = f32[1024,256]{1,0:T(8,128)} async-done(((f32[32,256]{1,0:T(8,128)}), f32[1024,256]{1,0:T(8,128)}) %all-gather.11.cloned.1.call-update) | async-done | bytes 1048592 | tf_op jit(solution)/shard_map/all_gather | solution.py:71
  390.9 2.4 fusion.13
  393.4 0.1 constant_dynamic-update-slice_fusion.1
  393.4 49.5 %all-gather.13.cloned.1.call-done = f32[1024,256]{1,0:T(8,128)} async-done(((f32[32,256]{1,0:T(8,128)}), f32[1024,256]{1,0:T(8,128)}) %all-gather.13.cloned.1.call-update) | async-done | bytes 1048592 | tf_op jit(solution)/shard_map/all_gather | solution.py:73
  443.0 1.3 constant_dynamic-update-slice_fusion
  444.3 1.7 copy.52
  445.9 0.3 copy-done
  446.2 4.3 all-to-all-start
  450.6 0.0 reduce-scatter.11.cloned.1.call-start
  450.7 26.2 %all-to-all-done = f32[8,2,128,256]{3,2,1,0:T(8,128)} async-done(((f32[8,2,128,256]{3,2,1,0:T(8,128)}), f32[8,2,128,256]{3,2,1,0:T(8,128)}, u32[]{:S(2)}, u32[]{:S(2)}) %all-to-all-start) | async-done | bytes 2097184 | tf_op jit(solution)/shard_map/all_to_all | solution.py:79
  476.8 2.8 copy.16
  479.7 6.7 %fusion = f32[2048,704]{0,1:T(8,128)} fusion(f32[256,8,2,128]{3,2,1,0:T(2,128)S(1)} %bitcast.74, f32[88,8,2,128]{3,2,1,0:T(2,128)S(1)} %bitcast.83), kind=kOutput, calls=%fused_computation | convolution fusion | flops 4429185024 | bytes 8585216 | tf_op jit(solution)/shard_map/dot_general | solution.py:14
  486.4 1.0 copy-done.4
  487.3 0.3 pad_maximum_fusion
  487.6 0.2 copy.14
  487.9 0.9 constant_dynamic-slice_fusion
  488.7 64.9 %reduce-scatter.11.cloned.1.call-done = f32[256,704]{0,1:T(8,128)} async-done(((f32[2048,704]{0,1:T(8,128)}), f32[256,704]{0,1:T(8,128)}) %reduce-scatter.11.cloned.1.call-update) | async-done | bytes 720912 | tf_op jit(solution)/shard_map/reduce_scatter | solution.py:82
  553.6 1.2 bitcast_subtract_fusion
  554.8 0.1 pad_maximum_fusion.1
  554.9 1.3 reshape.32
  (26 shorter events, 0.2 us)
Async XLA Ops:
  6.5 62.3 %all-gather.15.cloned.1.call-start = ((), (), s32[]{:S(2)}) async-start(), calls=%async_computation.13 | async-start | bytes 2162688 | tf_op jit(solution)/shard_map/all_gather | solution.py:36
  8.0 110.0 %reduce-scatter.5.cloned.1.call-start = ((), (), s32[]{:S(2)}) async-start(), calls=%async_computation.5 | async-start | bytes 3538944 | tf_op jit(solution)/shard_map/reduce_scatter | solution.py:51
  76.4 95.3 %reduce-scatter.7.cloned.1.call-start = ((), (), s32[]{:S(2)}) async-start(), calls=%async_computation.6 | async-start | bytes 3538944 | tf_op jit(solution)/shard_map/reduce_scatter | solution.py:54
  123.3 101.9 %reduce-scatter.9.cloned.1.call-start = ((), (), s32[]{:S(2)}) async-start(), calls=%async_computation.7 | async-start | bytes 3538944 | tf_op jit(solution)/shard_map/reduce_scatter | solution.py:58
  176.9 48.4 %copy-start.3 = (f32[128,768]{1,0:T(8,128)S(1)}, f32[128,768]{1,0:T(8,128)}, u32[]{:S(2)}) copy-start(f32[128,768]{1,0:T(8,128)} %reduce-scatter.5.cloned.1.call-done) | copy-start | bytes 1179652
  176.9 109.3 %all-gather.7.cloned.1.call-start = ((), (), s32[]{:S(2)}) async-start(), calls=%async_computation.8 | async-start | bytes 2162688 | tf_op jit(solution)/shard_map/all_gather | solution.py:65
  226.8 111.9 %all-gather.9.cloned.1.call-start = ((), (), s32[]{:S(2)}) async-start(), calls=%async_computation.9 | async-start | bytes 1081344 | tf_op jit(solution)/shard_map/all_gather | solution.py:68
  286.2 1.2 slice-start
  286.2 3.6 copy-start.1
  289.5 101.4 %all-gather.11.cloned.1.call-start = ((), (), s32[]{:S(2)}) async-start(), calls=%async_computation.10 | async-start | bytes 1081344 | tf_op jit(solution)/shard_map/all_gather | solution.py:71
  289.8 49.0 %copy-start.6 = (f32[32,1,1024]{2,1,0:T(1,128)S(1)}, f32[32,1,1024]{2,1,0:T(1,128)}, u32[]{:S(2)}) copy-start(f32[32,1,1024]{2,1,0:T(1,128)} %get-tuple-element.11) | copy-start | bytes 393220
  289.8 101.1 %copy-start.5 = (f32[32,1,1024]{2,1,0:T(1,128)S(1)}, f32[32,1,1024]{2,1,0:T(1,128)}, u32[]{:S(2)}) copy-start(f32[32,1,1024]{2,1,0:T(1,128)} %get-tuple-element.10) | copy-start | bytes 393220
  338.7 54.6 %copy-start.2 = (f32[1024,256]{1,0:T(8,128)S(1)}, f32[1024,256]{1,0:T(8,128)}, u32[]{:S(2)}) copy-start(f32[1024,256]{1,0:T(8,128)} %all-gather.9.cloned.1.call-done) | copy-start | bytes 3145732
  341.3 101.7 %all-gather.13.cloned.1.call-start = ((), (), s32[]{:S(2)}) async-start(), calls=%async_computation.11 | async-start | bytes 1081344 | tf_op jit(solution)/shard_map/all_gather | solution.py:73
  444.3 2.0 copy-start
  446.2 30.6 %all-to-all-start = ((f32[8,2,128,256]{3,2,1,0:T(8,128)}), f32[8,2,128,256]{3,2,1,0:T(8,128)}, u32[]{:S(2)}, u32[]{:S(2)}) async-start(f32[8,2,128,256]{3,2,1,0:T(8,128)} %bitcast.73), calls=%async_computation.3 | async-start | bytes 4194304 | tf_op jit(solution)/shard_map/all_to_all | solution.py:79
  450.6 103.0 %reduce-scatter.11.cloned.1.call-start = ((), (), s32[]{:S(2)}) async-start(), calls=%async_computation.12 | async-start | bytes 6488064 | tf_op jit(solution)/shard_map/reduce_scatter | solution.py:82
  450.6 29.0 %slice-start.1 = ((f32[12,64,2,128]{3,2,1,0:T(2,128)}), f32[11,64,2,128]{3,2,1,0:T(2,128)S(1)}, s32[]{:S(2)}) async-start(f32[12,64,2,128]{3,2,1,0:T(2,128)} %param.3), calls=%async_computation.15 | async-start | bytes 1441792 | tf_op jit(solution)/shard_map/slice | solution.py:77
  486.3 1.0 copy-start.4
Sparse Core Ops, SparseCore 0:
  9.9 58.8 all-gather.14
  76.5 41.5 reduce-scatter.4
  123.5 48.1 reduce-scatter.6
  177.0 48.1 reduce-scatter.8
  227.6 58.4 all-gather.6
  289.6 49.0 all-gather.8
  341.4 49.4 all-gather.10
  393.5 49.4 all-gather.12
  486.5 67.0 reduce-scatter.10

commit v2 on v1

--- a/solution.py
+++ b/solution.py
@@ -45,7 +45,6 @@
     picked = jnp.concatenate([top_rows, bottom_rows], axis=0)
     picked_rows = lax.all_gather(picked, "row", axis=2, tiled=True)
     first_rows = picked_rows[:share, 0, :]
-    cross_rows = picked_rows[share:, 0, :]
     second_rows = picked_rows[share:, 1, :]
 
     upper_half = lax.psum_scatter(
@@ -62,16 +61,18 @@
     lead_rows = solved[:strip_width]
     tail_rows = solved[strip_width:].reshape(trail_count, 2 * row_run)
 
+    cross_mix = lax.all_gather(times_rows(second_rows, cross_cols), "row", axis=1, tiled=True)
+    chained = lax.all_gather(times_rows(cross_mix, first_cols), "row", axis=1, tiled=True)
+
     lead_all = lax.all_gather(lead_rows, "col", axis=0, tiled=True)
     lead_all = lead_all.reshape(2 * block_size, 2 * row_run)
-    first_piece = times_rows(first_rows, lead_all[:block_size])
-    first_block = lax.all_gather(first_piece, "col", axis=0, tiled=True)
-    lead_second = lax.dynamic_slice_in_dim(lead_all, block_size + start, share, 0)
-    diff_piece = lead_second - times_rows(cross_rows, first_block)
-    diff_block = lax.all_gather(diff_piece, "col", axis=0, tiled=True)
-    second_piece = times_rows(second_rows, diff_block)
-    second_block = lax.all_gather(second_piece, "col", axis=0, tiled=True)
-    everything = jnp.concatenate([first_block, second_block], axis=0)
+    lead_first = lead_all[:block_size]
+    first_piece = times_rows(first_rows, lead_first)
+    second_piece = times_rows(second_rows, lead_all[block_size:]) - times_rows(chained, lead_first)
+    pieces = jnp.concatenate([first_piece, second_piece], axis=0)
+    everything = lax.all_gather(pieces, "col", axis=0, tiled=True)
+    everything = everything.reshape(col_count, 2, share, 2 * row_run).transpose(1, 0, 2, 3)
+    everything = everything.reshape(2 * block_size, 2 * row_run)
     solved_lead = lax.dynamic_slice_in_dim(everything, col_position * strip_width, strip_width, 0)
 
     left_rows = lower[1:].reshape(trail_count, 2 * row_run)

time: 563 us -> 491 us (0.87)
  waiting for transfers between devices: 476 us -> 362 us
  blocking collectives: 16.4 us -> 62.5 us
    all_gather x3 -> x1, waiting for transfers between devices: 147 us -> 73.5 us  [local(): everything = lax.all_gather(pieces, 'col', axis=0, tiled=True)]
    all_gather x0 -> x2, blocking collectives: none -> 46.2 us  [the longest x1 24.2 us: local(): lax.all_gather(times_rows(cross_mix, first_cols), 'row', axis=1, tiled=True)]
    all_gather x1, waiting for transfers between devices: 41.1 us -> 0.01 us  [local(): lead_all = lax.all_gather(lead_rows, 'col', axis=0, tiled=True)]
    dot_general x5 -> x7, matrix products: 17.6 us -> 13.1 us  [times_rows(): jnp.dot(coeff, right_side, precision=highest, preferred_element_type=jnp....]
  transfers between devices with their start and end apart: 10 -> 8, of which waited for: 10 -> 7; matrix products, arithmetic and copies ran while one was open for 1% -> 1% of each run, Pallas kernels for 0% -> 0%
where the time goes in v2:
time: 491 us; the launch traced here: 490 us
  waiting for transfers between devices  362 us (74%)
  blocking collectives  62.5 us (13%)
  matrix products  24.2 us (5%)
  local copies, waits for them, and re-layouts  20 us (4%)
  between operations  13.6 us (3%)
    all_gather x1, waiting for transfers between devices, local(): everything = lax.all_gather(pieces, 'col', axis=0, tiled=True)  73.5 us
    reduce_scatter x1, waiting for transfers between devices, local(): lax.psum_scatter(times_rows_turned(turned_block, left_rows), 'row', scatt...  64.6 us
    all_gather x1, waiting for transfers between devices, local(): gathered = lax.all_gather(lower[0], 'col', axis=0, tiled=True)  59.5 us
    reduce_scatter x1, waiting for transfers between devices, local(): lax.psum_scatter(times_rows(second_cols, remainder), 'row', scatter_dimen...  48.3 us
    reduce_scatter x1, waiting for transfers between devices, local(): lax.psum_scatter(times_rows(cross_cols, upper_half), 'row', scatter_dimen...  48.2 us
    reduce_scatter x1, waiting for transfers between devices, local(): lax.psum_scatter(times_rows_turned(first_cols, left_part), 'row', scatter...  41.6 us
    all_to_all x1, waiting for transfers between devices, local(): lax.all_to_all(grouped, 'row', split_axis=0, concat_axis=0, tiled=True)  26.2 us
    all_gather x1, blocking collectives, local(): lax.all_gather(times_rows(cross_mix, first_cols), 'row', axis=1, tiled=True)  24.2 us
  transfers between devices with their start and end apart: 8, of which 7 were waited for; matrix products, arithmetic and copies ran while one was open for 1% of the time, Pallas kernels for 0%

profile of v2, /device:TPU:1, one launch (start us, length us, event | category | flops | bytes accessed | tf_op | source)
XLA Modules:
  0.0 490.1 jit_solution(2785875868992799919)
XLA Ops:
  6.5 1.5 slice_bitcast_fusion.3
  8.0 0.0 reduce-scatter.5.cloned.1.call-start
  8.1 1.2 copy.11
  9.3 59.5 %all-gather.9.cloned.1.call-done = f32[1,2048,2,128]{3,2,0,1:T(2,128)} async-done(((f32[1,64,2,128]{3,2,0,1:T(2,128)}), f32[1,2048,2,128]{3,2,0,1:T(2,128)}) %all-gather.9.cloned.1.call-update) | async-done | bytes 2097168 | tf_op jit(solution)/shard_map/all_gather | solution.py:36
  68.8 3.2 fusion.24
  72.1 4.3 fusion.15
  76.4 0.0 reduce-scatter.5.cloned.1.call-update
  76.4 0.0 reduce-scatter.7.cloned.1.call-start
  76.4 41.6 %reduce-scatter.5.cloned.1.call-done = f32[128,768]{1,0:T(8,128)} async-done(((f32[1024,768]{1,0:T(8,128)}), f32[128,768]{1,0:T(8,128)}) %reduce-scatter.5.cloned.1.call-update) | async-done | bytes 393232 | tf_op jit(solution)/shard_map/reduce_scatter | solution.py:50
  118.1 5.3 %convolution_bitcast_fusion.1 = f32[1024,768]{0,1:T(8,128)} fusion(f32[128,768]{1,0:T(8,128)} %reduce-scatter.5.cloned.1.call-done, f32[1024,128]{1,0:T(8,128)S(1)} %bitcast.88), kind=kOutput, calls=%fused_computation.4 | convolution fusion | flops 1207959552 | bytes 4063232 | tf_op jit(solution)/shard_map/dot_general | solution.py:10
  123.4 0.0 reduce-scatter.7.cloned.1.call-update
  123.4 0.0 reduce-scatter.9.cloned.1.call-start
  123.4 48.2 %reduce-scatter.7.cloned.1.call-done = f32[128,768]{0,1:T(8,128)} async-done(((f32[1024,768]{0,1:T(8,128)}), f32[128,768]{0,1:T(8,128)}) %reduce-scatter.7.cloned.1.call-update) | async-done | bytes 393232 | tf_op jit(solution)/shard_map/reduce_scatter | solution.py:53
  171.7 5.3 %convolution_bitcast_fusion = f32[1024,768]{1,0:T(8,128)} fusion(f32[1024,128]{1,0:T(8,128)S(1)} %bitcast.98, f32[128,768]{0,1:T(8,128)} %reduce-scatter.7.cloned.1.call-done, f32[768,2,128]{2,0,1:T(8,128)S(1)} %bitcast.95), kind=kOutput, calls=%fused_computation.3 | convolution fusion | flops 1208057856 | bytes 4456448 | tf_op jit(solution)/shard_map/dot_general | solution.py:10
  177.0 0.0 all-gather.5.cloned.1.call-start
  177.0 48.3 %reduce-scatter.9.cloned.1.call-done = f32[128,768]{1,0:T(8,128)} async-done(((f32[1024,768]{1,0:T(8,128)}), f32[128,768]{1,0:T(8,128)}) %reduce-scatter.9.cloned.1.call-update) | async-done | bytes 393232 | tf_op jit(solution)/shard_map/reduce_scatter | solution.py:57
  225.3 0.8 pad_maximum_fusion.2
  226.2 0.7 copy.13
  226.9 0.0 all-gather.7.cloned.1.call-start
  227.0 0.8 dynamic-slice_bitcast_fusion.1
  227.8 16.3 %all_gather.19 = f32[64,2,1024]{2,1,0:T(2,128)S(1)} all-gather(f32[64,2,128]{2,1,0:T(2,128)S(1)} %pad_maximum_fusion.3), channel_id=1, replica_groups=mesh['row'=8,'col'=32] {'row'}, dimensions={2}, use_global_device_ids=true | all-gather | bytes 589824 | tf_op jit(solution)/shard_map/all_gather | solution.py:46
  244.1 0.2 fusion.25
  244.3 0.4 fusion.16
  244.8 22.0 %all_gather.21 = f32[32,1024]{1,0:T(8,128)S(1)} all-gather(f32[32,128]{1,0:T(8,128)S(1)} %fusion.16), channel_id=1, replica_groups=mesh['row'=8,'col'=32] {'row'}, dimensions={1}, use_global_device_ids=true | all-gather | bytes 147456 | tf_op jit(solution)/shard_map/all_gather | solution.py:64
  266.7 0.4 fusion.26
  267.1 24.2 %all_gather.22 = f32[32,1024]{1,0:T(8,128)S(1)} all-gather(f32[32,128]{1,0:T(8,128)S(1)} %fusion.26), channel_id=1, replica_groups=mesh['row'=8,'col'=32] {'row'}, dimensions={1}, use_global_device_ids=true | all-gather | bytes 147456 | tf_op jit(solution)/shard_map/all_gather | solution.py:65
  291.4 1.7 fusion.23
  293.0 0.6 fusion.3
  293.6 0.6 fusion.7
  294.2 0.6 convolution_subtract_fusion
  294.8 0.6 pad_maximum_fusion.4
  295.5 73.5 %all-gather.7.cloned.1.call-done = f32[2048,256]{1,0:T(8,128)} async-done(((f32[64,256]{1,0:T(8,128)}), f32[2048,256]{1,0:T(8,128)}) %all-gather.7.cloned.1.call-update) | async-done | bytes 2097168 | tf_op jit(solution)/shard_map/all_gather | solution.py:73
  369.0 1.7 copy.14
  370.7 1.3 copy-done
  372.0 1.5 copy.15
  373.5 4.3 all-to-all-start
  377.8 0.0 reduce-scatter.11.cloned.1.call-start
  377.9 26.2 %all-to-all-done = f32[8,2,128,256]{3,2,1,0:T(8,128)} async-done(((f32[8,2,128,256]{3,2,1,0:T(8,128)}), f32[8,2,128,256]{3,2,1,0:T(8,128)}, u32[]{:S(2)}, u32[]{:S(2)}) %all-to-all-start) | async-done | bytes 2097184 | tf_op jit(solution)/shard_map/all_to_all | solution.py:80
  404.0 2.8 copy.19
  406.9 6.8 %fusion = f32[2048,704]{0,1:T(8,128)} fusion(f32[256,8,2,128]{3,2,1,0:T(2,128)S(1)} %bitcast.81, f32[88,8,2,128]{3,2,1,0:T(2,128)S(1)} %bitcast.96), kind=kOutput, calls=%fused_computation | convolution fusion | flops 4429185024 | bytes 8585216 | tf_op jit(solution)/shard_map/dot_general | solution.py:14
  413.7 1.0 copy-done.2
  414.7 0.3 pad_maximum_fusion
  415.0 0.2 copy.17
  415.2 0.9 constant_dynamic-slice_fusion
  416.1 64.6 %reduce-scatter.11.cloned.1.call-done = f32[256,704]{0,1:T(8,128)} async-done(((f32[2048,704]{0,1:T(8,128)}), f32[256,704]{0,1:T(8,128)}) %reduce-scatter.11.cloned.1.call-update) | async-done | bytes 720912 | tf_op jit(solution)/shard_map/reduce_scatter | solution.py:83
  480.7 1.2 bitcast_subtract_fusion
  481.9 0.1 pad_maximum_fusion.1
  482.0 1.3 reshape.34
  (14 shorter events, 0.1 us)
Async XLA Ops:
  6.5 62.3 %all-gather.9.cloned.1.call-start = ((), (), s32[]{:S(2)}) async-start(), calls=%async_computation.11 | async-start | bytes 2162688 | tf_op jit(solution)/shard_map/all_gather | solution.py:36
  8.0 110.0 %reduce-scatter.5.cloned.1.call-start = ((), (), s32[]{:S(2)}) async-start(), calls=%async_computation.5 | async-start | bytes 3538944 | tf_op jit(solution)/shard_map/reduce_scatter | solution.py:50
  76.4 95.3 %reduce-scatter.7.cloned.1.call-start = ((), (), s32[]{:S(2)}) async-start(), calls=%async_computation.6 | async-start | bytes 3538944 | tf_op jit(solution)/shard_map/reduce_scatter | solution.py:53
  123.4 101.9 %reduce-scatter.9.cloned.1.call-start = ((), (), s32[]{:S(2)}) async-start(), calls=%async_computation.7 | async-start | bytes 3538944 | tf_op jit(solution)/shard_map/reduce_scatter | solution.py:57
  177.0 48.4 %copy-start.1 = (f32[128,768]{1,0:T(8,128)S(1)}, f32[128,768]{1,0:T(8,128)}, u32[]{:S(2)}) copy-start(f32[128,768]{1,0:T(8,128)} %reduce-scatter.5.cloned.1.call-done) | copy-start | bytes 1179652
  177.0 114.4 %all-gather.5.cloned.1.call-start = ((), (), s32[]{:S(2)}) async-start(), calls=%async_computation.8 | async-start | bytes 2162688 | tf_op jit(solution)/shard_map/all_gather | solution.py:67
  226.9 142.1 %all-gather.7.cloned.1.call-start = ((), (), s32[]{:S(2)}) async-start(), calls=%async_computation.9 | async-start | bytes 2162688 | tf_op jit(solution)/shard_map/all_gather | solution.py:73
  370.7 1.3 copy-start
  373.5 30.6 %all-to-all-start = ((f32[8,2,128,256]{3,2,1,0:T(8,128)}), f32[8,2,128,256]{3,2,1,0:T(8,128)}, u32[]{:S(2)}, u32[]{:S(2)}) async-start(f32[8,2,128,256]{3,2,1,0:T(8,128)} %copy.15), calls=%async_computation.3 | async-start | bytes 4194304 | tf_op jit(solution)/shard_map/all_to_all | solution.py:80
  377.8 102.9 %reduce-scatter.11.cloned.1.call-start = ((), (), s32[]{:S(2)}) async-start(), calls=%async_computation.10 | async-start | bytes 6488064 | tf_op jit(solution)/shard_map/reduce_scatter | solution.py:83
  377.9 29.0 %slice-start = ((f32[12,64,2,128]{3,2,1,0:T(2,128)}), f32[11,64,2,128]{3,2,1,0:T(2,128)S(1)}, s32[]{:S(2)}) async-start(f32[12,64,2,128]{3,2,1,0:T(2,128)} %param.3), calls=%async_computation.12 | async-start | bytes 1441792 | tf_op jit(solution)/shard_map/slice | solution.py:78
  413.7 1.0 copy-start.2
Sparse Core Ops, SparseCore 0:
  9.9 58.8 all-gather.8
  76.5 41.5 reduce-scatter.4
  123.5 48.1 reduce-scatter.6
  177.1 48.1 reduce-scatter.8
  227.7 59.2 all-gather.4
  295.6 73.3 all-gather.6
  413.8 66.8 reduce-scatter.10

commit v3 on v2

--- a/solution.py
+++ b/solution.py
@@ -28,11 +28,8 @@
     col_count = lax.axis_size("col")
     block_size = row_run * row_count
     cols_here = rounds * strip_width
-    trail_count = cols_here - strip_width
     share = block_size // col_count
-    local_strip = strip.reshape(cols_here, 2, row_run)
-    left_part = local_strip[:, 0, :]
-    right_part = local_strip[:, 1, :]
+    strip_rows = strip.reshape(cols_here, 2 * row_run)
     gathered = lax.all_gather(lower[0], "col", axis=0, tiled=True)
     first_cols = gathered[:block_size, 0, :]
     cross_cols = gathered[block_size:, 0, :]
@@ -47,25 +44,28 @@
     first_rows = picked_rows[:share, 0, :]
     second_rows = picked_rows[share:, 1, :]
 
-    upper_half = lax.psum_scatter(
-        times_rows_turned(first_cols, left_part), "row", scatter_dimension=0, tiled=True
+    cross_mix = lax.all_gather(times_rows(second_rows, cross_cols), "row", axis=1, tiled=True)
+    chained_piece = times_rows(cross_mix, first_cols)
+    chained = lax.all_gather(chained_piece, "row", axis=1, tiled=True)
+    chained_cols = lax.all_gather(chained_piece, "col", axis=0, tiled=True)
+
+    inverse_cols = jnp.concatenate(
+        [
+            jnp.concatenate([first_cols, jnp.zeros_like(first_cols)], axis=1),
+            jnp.concatenate([-chained_cols, second_cols], axis=1),
+        ],
+        axis=0,
     )
-    carried = lax.psum_scatter(
-        times_rows(cross_cols, upper_half), "row", scatter_dimension=0, tiled=True
-    )
-    remainder = right_part.T - carried
-    lower_half = lax.psum_scatter(
-        times_rows(second_cols, remainder), "row", scatter_dimension=0, tiled=True
-    )
-    solved = jnp.stack([upper_half.T, lower_half.T], axis=1)
-    lead_rows = solved[:strip_width]
-    tail_rows = solved[strip_width:].reshape(trail_count, 2 * row_run)
-
-    cross_mix = lax.all_gather(times_rows(second_rows, cross_cols), "row", axis=1, tiled=True)
-    chained = lax.all_gather(times_rows(cross_mix, first_cols), "row", axis=1, tiled=True)
+    inverse_cols = inverse_cols.reshape(2, row_count, row_run, 2 * row_run).transpose(1, 0, 2, 3)
+    inverse_cols = inverse_cols.reshape(2 * block_size, 2 * row_run)
+    lead_rows = lax.psum_scatter(
+        times_rows_turned(inverse_cols, strip_rows[:strip_width]),
+        "row",
+        scatter_dimension=0,
+        tiled=True,
+    ).T
 
     lead_all = lax.all_gather(lead_rows, "col", axis=0, tiled=True)
-    lead_all = lead_all.reshape(2 * block_size, 2 * row_run)
     lead_first = lead_all[:block_size]
     first_piece = times_rows(first_rows, lead_first)
     second_piece = times_rows(second_rows, lead_all[block_size:]) - times_rows(chained, lead_first)
@@ -75,16 +75,19 @@
     everything = everything.reshape(2 * block_size, 2 * row_run)
     solved_lead = lax.dynamic_slice_in_dim(everything, col_position * strip_width, strip_width, 0)
 
-    left_rows = lower[1:].reshape(trail_count, 2 * row_run)
+    left_rows = lower[1:].reshape(cols_here - strip_width, 2 * row_run)
     grouped = everything.reshape(2, row_count, row_run, 2 * row_run).transpose(1, 0, 2, 3)
     swapped = lax.all_to_all(grouped, "row", split_axis=0, concat_axis=0, tiled=True)
     turned_block = swapped.reshape(row_count, 2, row_run, 2, row_run).transpose(0, 3, 4, 1, 2)
     turned_block = turned_block.reshape(row_count * 2 * row_run, 2 * row_run)
     summed = lax.psum_scatter(
-        times_rows_turned(turned_block, left_rows), "row", scatter_dimension=0, tiled=True
+        times_rows_turned(inverse_cols, strip_rows[strip_width:])
+        - times_rows_turned(turned_block, left_rows),
+        "row",
+        scatter_dimension=0,
+        tiled=True,
     )
-    update = summed.T
-    reduced = jnp.concatenate([solved_lead, tail_rows - update], axis=0)
+    reduced = jnp.concatenate([solved_lead, summed.T], axis=0)
     return reduced.reshape(rounds, strip_width, 2, row_run)
 
 

time: 491 us -> 450 us (0.916)
  waiting for transfers between devices: 362 us -> 268 us
  blocking collectives: 62.5 us -> 123 us
  local copies, waits for them, and re-layouts: 20 us -> 14.8 us
    reduce_scatter x4 -> x2, waiting for transfers between devices: 203 us -> 96.8 us  [the longest x1 66.1 us: local(): lax.psum_scatter(times_rows_turned(inverse_cols, strip_rows[strip_width:]...]
    all_gather x1 -> x2, blocking collectives: 24.2 us -> 78 us  [the longest x1 56.2 us: local(): chained_cols = lax.all_gather(chained_piece, 'col', axis=0, tiled=True)]
    all_gather x1, waiting for transfers between devices: 0.01 us -> 39.9 us  [local(): lead_all = lax.all_gather(lead_rows, 'col', axis=0, tiled=True)]
    all_gather x1, waiting for transfers between devices: 73.5 us -> 51.8 us  [local(): everything = lax.all_gather(pieces, 'col', axis=0, tiled=True)]
    dot_general x7 -> x5, matrix products: 13.1 us -> 5.13 us  [times_rows(): jnp.dot(coeff, right_side, precision=highest, preferred_element_type=jnp....]
    all_to_all x1, waiting for transfers between devices: 26.2 us -> 18.5 us  [local(): lax.all_to_all(grouped, 'row', split_axis=0, concat_axis=0, tiled=True)]
    dot_general x2 -> x3, matrix products: 11.1 us -> 18.2 us  [times_rows_turned(): lax.dot_general(coeff, right_turned, (((1,), (1,)), ((), ())), precision=...]
    all_gather x1, blocking collectives: 16.3 us -> 22.8 us  [local(): picked_rows = lax.all_gather(picked, 'row', axis=2, tiled=True)]
  transfers between devices with their start and end apart: 8 -> 6, of which waited for: 7 -> 6; matrix products, arithmetic and copies ran while one was open for 1% -> 2% of each run, Pallas kernels for 0% -> 0%
where the time goes in v3:
time: 450 us; the launch traced here: 449 us
  waiting for transfers between devices  268 us (60%)
  blocking collectives  123 us (27%)
  matrix products  23.3 us (5%)
  local copies, waits for them, and re-layouts  14.8 us (3%)
  between operations  13.3 us (3%)
  starting transfers between devices  4.74 us (1%)
    reduce_scatter x1, waiting for transfers between devices, local(): lax.psum_scatter(times_rows_turned(inverse_cols, strip_rows[strip_width:]...  66.1 us
    all_gather x1, waiting for transfers between devices, local(): gathered = lax.all_gather(lower[0], 'col', axis=0, tiled=True)  60.8 us
    all_gather x1, blocking collectives, local(): chained_cols = lax.all_gather(chained_piece, 'col', axis=0, tiled=True)  56.2 us
    all_gather x1, waiting for transfers between devices, local(): everything = lax.all_gather(pieces, 'col', axis=0, tiled=True)  51.8 us
    all_gather x1, waiting for transfers between devices, local(): lead_all = lax.all_gather(lead_rows, 'col', axis=0, tiled=True)  39.9 us
    reduce_scatter x1, waiting for transfers between devices, local(): lax.psum_scatter(times_rows_turned(inverse_cols, strip_rows[:strip_width]...  30.7 us
    all_gather x1, blocking collectives, local(): picked_rows = lax.all_gather(picked, 'row', axis=2, tiled=True)  22.8 us
    all_gather x1, blocking collectives, local(): lax.all_gather(times_rows(second_rows, cross_cols), 'row', axis=1, tiled=...  22.1 us
  transfers between devices with their start and end apart: 6, of which 6 were waited for; matrix products, arithmetic and copies ran while one was open for 2% of the time, Pallas kernels for 0%

profile of v3, /device:TPU:1, one launch (start us, length us, event | category | flops | bytes accessed | tf_op | source)
XLA Modules:
  0.0 448.9 jit_solution(1289245343938174852)
XLA Ops:
  6.5 0.0 all-gather.9.cloned.1.call-start
  6.5 0.8 slice.39
  7.4 0.6 copy.15
  8.0 0.0 all-gather.9.cloned.1.call-update
  8.0 0.0 reduce-scatter.3.cloned.1.call-start
  8.1 60.8 %all-gather.9.cloned.1.call-done = f32[1,2048,2,128]{3,1,2,0:T(8,128)} async-done(((f32[1,64,2,128]{3,1,2,0:T(8,128)}), f32[1,2048,2,128]{3,1,2,0:T(8,128)}) %all-gather.9.cloned.1.call-update) | async-done | bytes 2097168 | tf_op jit(solution)/shard_map/all_gather | solution.py:33
  68.9 0.9 dynamic-slice_bitcast_fusion.1
  69.8 22.8 %all_gather.22 = f32[64,2,1024]{2,0,1:T(8,128)S(1)} all-gather(f32[64,2,128]{2,0,1:T(8,128)S(1)} %pad_maximum_fusion.1), channel_id=1, replica_groups=mesh['row'=8,'col'=32] {'row'}, dimensions={2}, use_global_device_ids=true | all-gather | bytes 589824 | tf_op jit(solution)/shard_map/all_gather | solution.py:43
  92.7 1.3 slice_bitcast_fusion
  93.9 0.4 fusion.12
  94.3 22.1 %all_gather.23 = f32[32,1024]{1,0:T(8,128)S(1)} all-gather(f32[32,128]{1,0:T(8,128)S(1)} %fusion.12), channel_id=1, replica_groups=mesh['row'=8,'col'=32] {'row'}, dimensions={1}, use_global_device_ids=true | all-gather | bytes 147456 | tf_op jit(solution)/shard_map/all_gather | solution.py:47
  116.5 0.4 fusion.16
  116.9 56.2 %all_gather.24 = f32[1024,128]{1,0:T(8,128)S(1)} all-gather(f32[32,128]{1,0:T(8,128)S(1)} %fusion.16), channel_id=1, replica_groups=mesh['row'=8,'col'=32] {'col'}, dimensions={0}, use_global_device_ids=true | all-gather | bytes 540672 | tf_op jit(solution)/shard_map/all_gather | solution.py:50
  173.1 0.1 select_maximum_fusion
  173.2 0.0 slice-start.1
  173.2 0.1 copy.10
  173.4 0.7 slice-done.1
  174.1 3.0 fusion.13
  177.0 0.0 reduce-scatter.3.cloned.1.call-update
  177.1 0.0 all-gather.5.cloned.1.call-start
  177.1 30.7 %reduce-scatter.3.cloned.1.call-done = f32[256,64]{0,1:T(8,128)} async-done(((f32[2048,64]{0,1:T(8,128)}), f32[256,64]{0,1:T(8,128)}) %reduce-scatter.3.cloned.1.call-update) | async-done | bytes 65552 | tf_op jit(solution)/shard_map/reduce_scatter | solution.py:61
  207.8 0.0 all-gather.5.cloned.1.call-update
  207.8 0.0 all-gather.7.cloned.1.call-start
  207.9 21.8 %all_gather.26 = f32[32,1024]{1,0:T(8,128)S(1)} all-gather(f32[32,128]{1,0:T(8,128)S(1)} %fusion.16), channel_id=1, replica_groups=mesh['row'=8,'col'=32] {'row'}, dimensions={1}, use_global_device_ids=true | all-gather | bytes 147456 | tf_op jit(solution)/shard_map/all_gather | solution.py:49
  229.7 39.9 %all-gather.5.cloned.1.call-done = f32[2048,256]{1,0:T(8,128)} async-done(((f32[64,256]{1,0:T(8,128)}), f32[2048,256]{1,0:T(8,128)}) %all-gather.5.cloned.1.call-update) | async-done | bytes 2097168 | tf_op jit(solution)/shard_map/all_gather | solution.py:68
  269.6 2.0 fusion.2
  271.5 1.8 fusion.5
  273.4 0.6 convolution_subtract_fusion.1
  274.0 0.6 pad_maximum_fusion.2
  274.6 0.0 all-gather.7.cloned.1.call-update
  274.6 51.8 %all-gather.7.cloned.1.call-done = f32[2048,256]{1,0:T(8,128)} async-done(((f32[64,256]{1,0:T(8,128)}), f32[2048,256]{1,0:T(8,128)}) %all-gather.7.cloned.1.call-update) | async-done | bytes 2097168 | tf_op jit(solution)/shard_map/all_gather | solution.py:73
  326.4 1.7 copy.11
  328.2 1.3 copy-done
  329.5 1.4 copy.12
  330.9 4.4 all-to-all-start
  335.4 0.0 slice-start.2
  335.4 0.2 reduce-scatter.5.cloned.1.call-start
  335.6 0.9 slice-done.2
  336.5 6.6 %fusion.9 = f32[2048,704]{0,1:T(8,128)} fusion(f32[2048,256]{1,0:T(8,128)S(1)} %bitcast.62, f32[88,8,2,128]{3,2,1,0:T(2,128)S(1)} %bitcast.69), kind=kOutput, calls=%fused_computation.14 | convolution fusion | flops 4429185024 | bytes 8585216 | tf_op jit(solution)/shard_map/dot_general | solution.py:14
  343.1 18.5 %all-to-all-done = f32[8,2,128,256]{3,2,1,0:T(8,128)} async-done(((f32[8,2,128,256]{3,2,1,0:T(8,128)}), f32[8,2,128,256]{3,2,1,0:T(8,128)}, u32[]{:S(2)}, u32[]{:S(2)}) %all-to-all-start) | async-done | bytes 2097184 | tf_op jit(solution)/shard_map/all_to_all | solution.py:80
  361.6 2.8 copy.14
  364.4 0.0 slice-done
  364.5 8.6 %convolution_subtract_fusion = f32[2048,704]{0,1:T(8,128)} fusion(f32[2048,704]{0,1:T(8,128)} %fusion.9, f32[256,8,2,128]{3,2,1,0:T(2,128)S(1)} %bitcast.65, f32[88,8,2,128]{3,2,1,0:T(2,128)S(1)} %bitcast.67), kind=kOutput, calls=%fused_computation | convolution fusion | flops 4430626816 | bytes 14352384 | tf_op jit(solution)/shard_map/dot_general | solution.py:14
  373.0 0.0 reduce-scatter.5.cloned.1.call-update
  373.1 0.8 constant_dynamic-slice_fusion
  373.9 66.1 %reduce-scatter.5.cloned.1.call-done = f32[256,704]{0,1:T(8,128)} async-done(((f32[2048,704]{0,1:T(8,128)}), f32[256,704]{0,1:T(8,128)}) %reduce-scatter.5.cloned.1.call-update) | async-done | bytes 720912 | tf_op jit(solution)/shard_map/reduce_scatter | solution.py:83
  440.0 1.2 pad_maximum_fusion
  441.1 1.3 reshape.34
  (8 shorter events, 0.1 us)
Async XLA Ops:
  6.5 62.4 %all-gather.9.cloned.1.call-start = ((), (), s32[]{:S(2)}) async-start(), calls=%async_computation.7 | async-start | bytes 2162688 | tf_op jit(solution)/shard_map/all_gather | solution.py:33
  8.0 199.7 %reduce-scatter.3.cloned.1.call-start = ((), (), s32[]{:S(2)}) async-start(), calls=%async_computation.3 | async-start | bytes 589824 | tf_op jit(solution)/shard_map/reduce_scatter | solution.py:61
  68.9 25.0 %copy-start.2 = (f32[1,2048,2,128]{3,1,2,0:T(8,128)S(1)}, f32[1,2048,2,128]{3,1,2,0:T(8,128)}, u32[]{:S(2)}) copy-start(f32[1,2048,2,128]{3,1,2,0:T(8,128)} %all-gather.9.cloned.1.call-done) | copy-start | bytes 6291460
  173.2 0.8 slice-start.1
  177.1 92.5 %all-gather.5.cloned.1.call-start = ((), (), s32[]{:S(2)}) async-start(), calls=%async_computation.4 | async-start | bytes 2162688 | tf_op jit(solution)/shard_map/all_gather | solution.py:68
  207.8 118.6 %all-gather.7.cloned.1.call-start = ((), (), s32[]{:S(2)}) async-start(), calls=%async_computation.5 | async-start | bytes 2162688 | tf_op jit(solution)/shard_map/all_gather | solution.py:73
  269.6 3.8 copy-start.1
  328.2 1.3 copy-start
  330.9 30.6 %all-to-all-start = ((f32[8,2,128,256]{3,2,1,0:T(8,128)}), f32[8,2,128,256]{3,2,1,0:T(8,128)}, u32[]{:S(2)}, u32[]{:S(2)}) async-start(f32[8,2,128,256]{3,2,1,0:T(8,128)} %copy.12), calls=%async_computation.1 | async-start | bytes 4194304 | tf_op jit(solution)/shard_map/all_to_all | solution.py:80
  335.4 1.1 slice-start.2
  335.4 104.6 %reduce-scatter.5.cloned.1.call-start = ((), (), s32[]{:S(2)}) async-start(), calls=%async_computation.6 | async-start | bytes 6488064 | tf_op jit(solution)/shard_map/reduce_scatter | solution.py:83
  343.1 21.3 %slice-start = ((f32[12,64,2,128]{3,2,1,0:T(2,128)}), f32[11,64,2,128]{3,2,1,0:T(2,128)S(1)}, s32[]{:S(2)}) async-start(f32[12,64,2,128]{3,2,1,0:T(2,128)} %param.3), calls=%async_computation.8 | async-start | bytes 1441792 | tf_op jit(solution)/shard_map/slice | solution.py:78
Sparse Core Ops, SparseCore 0:
  10.0 58.9 all-gather.8
  177.2 30.5 reduce-scatter.2
  210.7 58.8 all-gather.4
  274.7 51.6 all-gather.6
  373.2 66.7 reduce-scatter.4

commit v4 on v3

--- a/solution.py
+++ b/solution.py
@@ -58,18 +58,15 @@
     )
     inverse_cols = inverse_cols.reshape(2, row_count, row_run, 2 * row_run).transpose(1, 0, 2, 3)
     inverse_cols = inverse_cols.reshape(2 * block_size, 2 * row_run)
-    lead_rows = lax.psum_scatter(
-        times_rows_turned(inverse_cols, strip_rows[:strip_width]),
-        "row",
-        scatter_dimension=0,
-        tiled=True,
+    strip_lead = lax.all_gather(strip[0], "col", axis=0, tiled=True)
+    strip_lead = strip_lead.reshape(2 * block_size, 2 * row_run)
+    strip_first = strip_lead[:block_size]
+    first_mixed = times_rows(first_rows, strip_first)
+    second_mixed = times_rows(second_rows, strip_lead[block_size:]) - times_rows(chained, strip_first)
+    mixed = jnp.concatenate([first_mixed, second_mixed], axis=0)
+    pieces = lax.psum_scatter(
+        times_rows_turned(inverse_cols, mixed), "row", scatter_dimension=0, tiled=True
     ).T
-
-    lead_all = lax.all_gather(lead_rows, "col", axis=0, tiled=True)
-    lead_first = lead_all[:block_size]
-    first_piece = times_rows(first_rows, lead_first)
-    second_piece = times_rows(second_rows, lead_all[block_size:]) - times_rows(chained, lead_first)
-    pieces = jnp.concatenate([first_piece, second_piece], axis=0)
     everything = lax.all_gather(pieces, "col", axis=0, tiled=True)
     everything = everything.reshape(col_count, 2, share, 2 * row_run).transpose(1, 0, 2, 3)
     everything = everything.reshape(2 * block_size, 2 * row_run)

time: 450 us -> 427 us (0.949)
  waiting for transfers between devices: 268 us -> 237 us
  blocking collectives: 123 us -> 131 us
    all_gather x1, waiting for transfers between devices: 39.9 us -> 0.01 us  [local(): strip_lead = lax.all_gather(strip[0], 'col', axis=0, tiled=True)]
    all_gather x1, waiting for transfers between devices: 51.8 us -> 61.6 us  [local(): everything = lax.all_gather(pieces, 'col', axis=0, tiled=True)]
    all_gather x1, blocking collectives: 56.2 us -> 61.9 us  [local(): chained_cols = lax.all_gather(chained_piece, 'col', axis=0, tiled=True)]
  transfers between devices with their start and end apart: 6 -> 6, of which waited for: 6 -> 5; matrix products, arithmetic and copies ran while one was open for 2% -> 3% of each run, Pallas kernels for 0% -> 0%
where the time goes in v4:
time: 427 us
  waiting for transfers between devices  237 us (56%)
  blocking collectives  131 us (31%)
  matrix products  22.8 us (5%)
  local copies, waits for them, and re-layouts  17 us (4%)
  between operations  13.3 us (3%)
  starting transfers between devices  4.74 us (1%)
    reduce_scatter x1, waiting for transfers between devices, local(): lax.psum_scatter(times_rows_turned(inverse_cols, strip_rows[strip_width:]...  66.1 us
    all_gather x1, blocking collectives, local(): chained_cols = lax.all_gather(chained_piece, 'col', axis=0, tiled=True)  61.9 us
    all_gather x1, waiting for transfers between devices, local(): everything = lax.all_gather(pieces, 'col', axis=0, tiled=True)  61.6 us
    all_gather x1, waiting for transfers between devices, local(): gathered = lax.all_gather(lower[0], 'col', axis=0, tiled=True)  59.3 us
    reduce_scatter x1, waiting for transfers between devices, local(): lax.psum_scatter(times_rows_turned(inverse_cols, mixed), 'row', scatter_d...  31.2 us
    all_gather x1, blocking collectives, local(): picked_rows = lax.all_gather(picked, 'row', axis=2, tiled=True)  23.8 us
    all_gather x1, blocking collectives, local(): lax.all_gather(times_rows(second_rows, cross_cols), 'row', axis=1, tiled=...  22.7 us
    all_gather x1, blocking collectives, local(): chained = lax.all_gather(chained_piece, 'row', axis=1, tiled=True)  22.1 us
  transfers between devices with their start and end apart: 6, of which 5 were waited for; matrix products, arithmetic and copies ran while one was open for 3% of the time, Pallas kernels for 0%

profile of v4, /device:TPU:1, one launch (start us, length us, event | category | flops | bytes accessed | tf_op | source)
XLA Modules:
  0.0 426.6 jit_solution(12031750081110023101)
XLA Ops:
  6.5 0.0 all-gather.8.cloned.1.call-start
  6.5 0.8 slice.42
  7.4 0.6 copy.16
  8.0 0.0 all-gather.8.cloned.1.call-update
  8.0 0.0 all-gather.10.cloned.1.call-start
  8.1 1.5 slice_bitcast_fusion.9
  9.6 0.0 all-gather.10.cloned.1.call-update
  9.6 0.0 reduce-scatter.3.cloned.1.call-start
  9.6 59.3 %all-gather.8.cloned.1.call-done = f32[1,2048,2,128]{3,1,2,0:T(8,128)} async-done(((f32[1,64,2,128]{3,1,2,0:T(8,128)}), f32[1,2048,2,128]{3,1,2,0:T(8,128)}) %all-gather.8.cloned.1.call-update) | async-done | bytes 2097168 | tf_op jit(solution)/shard_map/all_gather | solution.py:33
  68.9 0.9 dynamic-slice_bitcast_fusion.1
  69.8 23.8 %all_gather.22 = f32[64,2,1024]{2,0,1:T(8,128)S(1)} all-gather(f32[64,2,128]{2,0,1:T(8,128)S(1)} %pad_maximum_fusion.1), channel_id=1, replica_groups=mesh['row'=8,'col'=32] {'row'}, dimensions={2}, use_global_device_ids=true | all-gather | bytes 589824 | tf_op jit(solution)/shard_map/all_gather | solution.py:43
  93.7 1.6 fusion.15
  95.3 22.7 %all_gather.23 = f32[32,1024]{1,0:T(8,128)S(1)} all-gather(f32[32,128]{1,0:T(8,128)S(1)} %fusion.15), channel_id=1, replica_groups=mesh['row'=8,'col'=32] {'row'}, dimensions={1}, use_global_device_ids=true | all-gather | bytes 147456 | tf_op jit(solution)/shard_map/all_gather | solution.py:47
  118.0 1.4 fusion.21
  119.5 22.1 %all_gather.26 = f32[32,1024]{1,0:T(8,128)S(1)} all-gather(f32[32,128]{1,0:T(8,128)S(1)} %fusion.21), channel_id=1, replica_groups=mesh['row'=8,'col'=32] {'row'}, dimensions={1}, use_global_device_ids=true | all-gather | bytes 147456 | tf_op jit(solution)/shard_map/all_gather | solution.py:49
  141.6 61.9 %all_gather.24 = f32[1024,128]{1,0:T(8,128)S(1)} all-gather(f32[32,128]{1,0:T(8,128)S(1)} %fusion.21), channel_id=1, replica_groups=mesh['row'=8,'col'=32] {'col'}, dimensions={0}, use_global_device_ids=true | all-gather | bytes 540672 | tf_op jit(solution)/shard_map/all_gather | solution.py:50
  203.5 0.9 slice_bitcast_fusion
  204.4 1.7 fusion.22
  206.1 0.0 copy-start.2
  206.1 0.6 fusion.2
  206.7 0.6 fusion.6
  207.4 0.0 copy-done.2
  207.4 0.2 select_maximum_fusion
  207.6 0.1 copy.10
  207.7 0.6 convolution_subtract_fusion.1
  208.3 3.0 fusion.16
  211.3 0.0 reduce-scatter.3.cloned.1.call-update
  211.3 0.0 all-gather.6.cloned.1.call-start
  211.4 31.2 %reduce-scatter.3.cloned.1.call-done = f32[256,64]{0,1:T(8,128)} async-done(((f32[2048,64]{0,1:T(8,128)}), f32[256,64]{0,1:T(8,128)}) %reduce-scatter.3.cloned.1.call-update) | async-done | bytes 65552 | tf_op jit(solution)/shard_map/reduce_scatter | solution.py:67
  242.5 0.0 all-gather.6.cloned.1.call-update
  242.5 61.6 %all-gather.6.cloned.1.call-done = f32[2048,256]{1,0:T(8,128)} async-done(((f32[64,256]{1,0:T(8,128)}), f32[2048,256]{1,0:T(8,128)}) %all-gather.6.cloned.1.call-update) | async-done | bytes 2097168 | tf_op jit(solution)/shard_map/all_gather | solution.py:70
  304.2 1.7 copy.12
  305.9 1.3 copy-done
  307.2 1.4 copy.13
  308.7 4.4 %all-to-all-start = ((f32[8,2,128,256]{3,2,1,0:T(8,128)}), f32[8,2,128,256]{3,2,1,0:T(8,128)}, u32[]{:S(2)}, u32[]{:S(2)}) async-start(f32[8,2,128,256]{3,2,1,0:T(8,128)} %copy.13), calls=%async_computation.1 | async-start | bytes 4194304 | tf_op jit(solution)/shard_map/all_to_all | solution.py:77
  313.1 0.0 slice-start.1
  313.1 0.2 reduce-scatter.5.cloned.1.call-start
  313.3 0.9 slice-done.1
  314.2 6.5 %fusion.12 = f32[2048,704]{0,1:T(8,128)} fusion(f32[2048,256]{1,0:T(8,128)S(1)} %bitcast.73, f32[88,8,2,128]{3,2,1,0:T(2,128)S(1)} %bitcast.82), kind=kOutput, calls=%fused_computation.17 | convolution fusion | flops 4429185024 | bytes 8585216 | tf_op jit(solution)/shard_map/dot_general | solution.py:14
  320.7 18.6 %all-to-all-done = f32[8,2,128,256]{3,2,1,0:T(8,128)} async-done(((f32[8,2,128,256]{3,2,1,0:T(8,128)}), f32[8,2,128,256]{3,2,1,0:T(8,128)}, u32[]{:S(2)}, u32[]{:S(2)}) %all-to-all-start) | async-done | bytes 2097184 | tf_op jit(solution)/shard_map/all_to_all | solution.py:77
  339.3 2.8 copy.15
  342.2 0.0 slice-done
  342.2 8.5 %convolution_subtract_fusion = f32[2048,704]{0,1:T(8,128)} fusion(f32[2048,704]{0,1:T(8,128)} %fusion.12, f32[256,8,2,128]{3,2,1,0:T(2,128)S(1)} %bitcast.78, f32[88,8,2,128]{3,2,1,0:T(2,128)S(1)} %bitcast.81), kind=kOutput, calls=%fused_computation | convolution fusion | flops 4430626816 | bytes 14352384 | tf_op jit(solution)/shard_map/dot_general | solution.py:14
  350.6 0.0 reduce-scatter.5.cloned.1.call-update
  350.7 0.8 constant_dynamic-slice_fusion
  351.5 66.1 %reduce-scatter.5.cloned.1.call-done = f32[256,704]{0,1:T(8,128)} async-done(((f32[2048,704]{0,1:T(8,128)}), f32[256,704]{0,1:T(8,128)}) %reduce-scatter.5.cloned.1.call-update) | async-done | bytes 720912 | tf_op jit(solution)/shard_map/reduce_scatter | solution.py:80
  417.6 1.2 pad_maximum_fusion
  418.8 1.3 reshape.36
  (11 shorter events, 0.1 us)
Async XLA Ops:
  6.5 62.4 %all-gather.8.cloned.1.call-start = ((), (), s32[]{:S(2)}) async-start(), calls=%async_computation.6 | async-start | bytes 2162688 | tf_op jit(solution)/shard_map/all_gather | solution.py:33
  8.0 196.3 %all-gather.10.cloned.1.call-start = ((), (), s32[]{:S(2)}) async-start(), calls=%async_computation.7 | async-start | bytes 2162688 | tf_op jit(solution)/shard_map/all_gather | solution.py:61
  9.6 232.9 %reduce-scatter.3.cloned.1.call-start = ((), (), s32[]{:S(2)}) async-start(), calls=%async_computation.3 | async-start | bytes 589824 | tf_op jit(solution)/shard_map/reduce_scatter | solution.py:67
  68.9 134.6 %copy-start.1 = (f32[1,2048,2,128]{3,1,2,0:T(8,128)S(1)}, f32[1,2048,2,128]{3,1,2,0:T(8,128)}, u32[]{:S(2)}) copy-start(f32[1,2048,2,128]{3,1,2,0:T(8,128)} %all-gather.8.cloned.1.call-done) | copy-start | bytes 6291460
  93.7 47.9 %copy-start.3 = (f32[64,2,1024]{2,0,1:T(8,128)}, f32[64,2,1024]{2,0,1:T(8,128)S(1)}, u32[]{:S(2)}) copy-start(f32[64,2,1024]{2,0,1:T(8,128)S(1)} %all_gather.22) | copy-start | bytes 1572868
  204.3 1.8 copy-start.4
  206.1 1.3 copy-start.2
  211.3 92.9 %all-gather.6.cloned.1.call-start = ((), (), s32[]{:S(2)}) async-start(), calls=%async_computation.4 | async-start | bytes 2162688 | tf_op jit(solution)/shard_map/all_gather | solution.py:70
  305.9 1.3 copy-start
  308.7 30.6 %all-to-all-start = ((f32[8,2,128,256]{3,2,1,0:T(8,128)}), f32[8,2,128,256]{3,2,1,0:T(8,128)}, u32[]{:S(2)}, u32[]{:S(2)}) async-start(f32[8,2,128,256]{3,2,1,0:T(8,128)} %copy.13), calls=%async_computation.1 | async-start | bytes 4194304 | tf_op jit(solution)/shard_map/all_to_all | solution.py:77
  313.1 1.1 slice-start.1
  313.1 104.5 %reduce-scatter.5.cloned.1.call-start = ((), (), s32[]{:S(2)}) async-start(), calls=%async_computation.5 | async-start | bytes 6488064 | tf_op jit(solution)/shard_map/reduce_scatter | solution.py:80
  320.7 21.4 %slice-start = ((f32[12,64,2,128]{3,2,1,0:T(2,128)}), f32[11,64,2,128]{3,2,1,0:T(2,128)S(1)}, s32[]{:S(2)}) async-start(f32[12,64,2,128]{3,2,1,0:T(2,128)} %param.3), calls=%async_computation.8 | async-start | bytes 1441792 | tf_op jit(solution)/shard_map/slice | solution.py:75
Sparse Core Ops, SparseCore 0:
  10.0 58.9 all-gather.7
  71.5 50.9 all-gather.9
  211.4 31.0 reduce-scatter.2
  245.2 58.8 all-gather.5
  350.8 66.7 reduce-scatter.4

commit v5 on v4

--- a/solution.py
+++ b/solution.py
@@ -28,7 +28,6 @@
     col_count = lax.axis_size("col")
     block_size = row_run * row_count
     cols_here = rounds * strip_width
-    share = block_size // col_count
     strip_rows = strip.reshape(cols_here, 2 * row_run)
     gathered = lax.all_gather(lower[0], "col", axis=0, tiled=True)
     first_cols = gathered[:block_size, 0, :]
@@ -36,18 +35,15 @@
     second_cols = gathered[block_size:, 1, :]
 
     col_position = lax.axis_index("col")
-    start = col_position * share
-    top_rows = lax.dynamic_slice_in_dim(gathered, start, share, 0)
-    bottom_rows = lax.dynamic_slice_in_dim(gathered, block_size + start, share, 0)
-    picked = jnp.concatenate([top_rows, bottom_rows], axis=0)
-    picked_rows = lax.all_gather(picked, "row", axis=2, tiled=True)
-    first_rows = picked_rows[:share, 0, :]
-    second_rows = picked_rows[share:, 1, :]
+    lower_half = col_position * strip_width // block_size
+    own_rows = lax.all_gather(lower[0], "row", axis=2, tiled=True)
+    diag_rows = lax.dynamic_index_in_dim(own_rows, lower_half, 1, keepdims=False)
+    below = lower_half == 1
 
-    cross_mix = lax.all_gather(times_rows(second_rows, cross_cols), "row", axis=1, tiled=True)
+    cross_mix = lax.all_gather(times_rows(own_rows[:, 1, :], cross_cols), "row", axis=1, tiled=True)
     chained_piece = times_rows(cross_mix, first_cols)
     chained = lax.all_gather(chained_piece, "row", axis=1, tiled=True)
-    chained_cols = lax.all_gather(chained_piece, "col", axis=0, tiled=True)
+    chained_cols = lax.all_gather(chained_piece, "col", axis=0, tiled=True)[block_size:]
 
     inverse_cols = jnp.concatenate(
         [
@@ -61,16 +57,13 @@
     strip_lead = lax.all_gather(strip[0], "col", axis=0, tiled=True)
     strip_lead = strip_lead.reshape(2 * block_size, 2 * row_run)
     strip_first = strip_lead[:block_size]
-    first_mixed = times_rows(first_rows, strip_first)
-    second_mixed = times_rows(second_rows, strip_lead[block_size:]) - times_rows(chained, strip_first)
-    mixed = jnp.concatenate([first_mixed, second_mixed], axis=0)
-    pieces = lax.psum_scatter(
+    strip_diag = lax.dynamic_slice_in_dim(strip_lead, lower_half * block_size, block_size, 0)
+    chained_term = jnp.where(below, times_rows(chained, strip_first), 0.0)
+    mixed = times_rows(diag_rows, strip_diag) - chained_term
+    solved_lead = lax.psum_scatter(
         times_rows_turned(inverse_cols, mixed), "row", scatter_dimension=0, tiled=True
     ).T
-    everything = lax.all_gather(pieces, "col", axis=0, tiled=True)
-    everything = everything.reshape(col_count, 2, share, 2 * row_run).transpose(1, 0, 2, 3)
-    everything = everything.reshape(2 * block_size, 2 * row_run)
-    solved_lead = lax.dynamic_slice_in_dim(everything, col_position * strip_width, strip_width, 0)
+    everything = lax.all_gather(solved_lead, "col", axis=0, tiled=True)
 
     left_rows = lower[1:].reshape(cols_here - strip_width, 2 * row_run)
     grouped = everything.reshape(2, row_count, row_run, 2 * row_run).transpose(1, 0, 2, 3)

time: 427 us -> 395 us (0.925)
  blocking collectives: 131 us -> 69.6 us
  waiting for transfers between devices: 237 us -> 268 us
    all_gather x3 -> x2, blocking collectives: 108 us -> 47.6 us  [the longest x1 25 us: local(): own_rows = lax.all_gather(lower[0], 'row', axis=2, tiled=True)]
    all_gather x1, waiting for transfers between devices: 0.01 us -> 28.1 us  [local(): strip_lead = lax.all_gather(strip[0], 'col', axis=0, tiled=True)]
    all_gather x1 -> x2, waiting for transfers between devices: 61.6 us -> 87.5 us  [the longest x1 61.6 us: local(): everything = lax.all_gather(solved_lead, 'col', axis=0, tiled=True)]
    all_gather x1, waiting for transfers between devices: 59.3 us -> 34.3 us  [local(): gathered = lax.all_gather(lower[0], 'col', axis=0, tiled=True)]
  transfers between devices with their start and end apart: 6 -> 7, of which waited for: 5 -> 7; matrix products, arithmetic and copies ran while one was open for 3% -> 4% of each run, Pallas kernels for 0% -> 0%
where the time goes in v5:
time: 395 us
  waiting for transfers between devices  268 us (68%)
  blocking collectives  69.6 us (18%)
  matrix products  22.8 us (6%)
  local copies, waits for them, and re-layouts  13.6 us (3%)
  between operations  13.6 us (3%)
  starting transfers between devices  4.78 us (1%)
    reduce_scatter x1, waiting for transfers between devices, local(): lax.psum_scatter(times_rows_turned(inverse_cols, strip_rows[strip_width:]...  67 us
    all_gather x1, waiting for transfers between devices, local(): everything = lax.all_gather(solved_lead, 'col', axis=0, tiled=True)  61.6 us
    all_gather x1, waiting for transfers between devices, local(): gathered = lax.all_gather(lower[0], 'col', axis=0, tiled=True)  34.3 us
    reduce_scatter x1, waiting for transfers between devices, local(): lax.psum_scatter(times_rows_turned(inverse_cols, mixed), 'row', scatter_d...  32.4 us
    all_gather x1, waiting for transfers between devices, local(): strip_lead = lax.all_gather(strip[0], 'col', axis=0, tiled=True)  28.1 us
    all_gather x1, waiting for transfers between devices, local(): lax.all_gather(chained_piece, 'col', axis=0, tiled=True)[block_size:]  25.9 us
    all_gather x1, blocking collectives, local(): own_rows = lax.all_gather(lower[0], 'row', axis=2, tiled=True)  25 us
    all_gather x1, blocking collectives, local(): lax.all_gather(times_rows(own_rows[:, 1, :], cross_cols), 'row', axis=1,...  22.5 us
  transfers between devices with their start and end apart: 7, of which 7 were waited for; matrix products, arithmetic and copies ran while one was open for 4% of the time, Pallas kernels for 0%

profile of v5, /device:TPU:1, one launch (start us, length us, event | category | flops | bytes accessed | tf_op | source)
XLA Modules:
  0.0 394.7 jit_solution(5752750095521305066)
XLA Ops:
  6.5 0.0 all-gather.12.cloned.1.call-start
  6.5 0.8 slice.37
  7.4 0.6 copy.13
  8.0 0.0 all-gather.12.cloned.1.call-update
  8.0 0.0 all-gather.14.cloned.1.call-start
  8.1 1.5 slice_bitcast_fusion.6
  9.6 0.0 all-gather.14.cloned.1.call-update
  9.6 0.0 all-gather.8.cloned.1.call-start
  9.6 25.0 %all-gather.1 = f32[1,64,2,1024]{3,1,2,0:T(8,128)S(1)} all-gather(f32[1,64,2,128]{3,1,2,0:T(8,128)} %copy.13), channel_id=3, replica_groups=mesh['row'=8,'col'=32] {'row'}, dimensions={3}, use_global_device_ids=true | all-gather | bytes 589824 | tf_op jit(solution)/shard_map/all_gather | solution.py:39
  34.6 34.3 %all-gather.12.cloned.1.call-done = f32[1,2048,2,128]{3,1,2,0:T(8,128)} async-done(((f32[1,64,2,128]{3,1,2,0:T(8,128)}), f32[1,2048,2,128]{3,1,2,0:T(8,128)}) %all-gather.12.cloned.1.call-update) | async-done | bytes 2097168 | tf_op jit(solution)/shard_map/all_gather | solution.py:32
  68.9 1.5 fusion.12
  70.4 22.5 %all_gather.23 = f32[64,1024]{1,0:T(8,128)S(1)} all-gather(f32[64,128]{1,0:T(8,128)S(1)} %fusion.12), channel_id=1, replica_groups=mesh['row'=8,'col'=32] {'row'}, dimensions={1}, use_global_device_ids=true | all-gather | bytes 294912 | tf_op jit(solution)/shard_map/all_gather | solution.py:43
  92.9 2.1 fusion.16
  95.0 0.0 all-gather.8.cloned.1.call-update
  95.0 0.0 reduce-scatter.3.cloned.1.call-start
  95.1 28.1 %all-gather.14.cloned.1.call-done = f32[1,2048,2,128]{3,2,0,1:T(2,128)} async-done(((f32[1,64,2,128]{3,2,0,1:T(2,128)}), f32[1,2048,2,128]{3,2,0,1:T(2,128)}) %all-gather.14.cloned.1.call-update) | async-done | bytes 2097168 | tf_op jit(solution)/shard_map/all_gather | solution.py:57
  123.2 1.9 copy.38
  125.1 0.3 copy-done
  125.4 0.1 slice.55
  125.5 0.6 fusion.5
  126.1 0.0 copy-done.2
  126.2 22.0 %all_gather.26 = f32[64,1024]{1,0:T(8,128)S(1)} all-gather(f32[64,128]{1,0:T(8,128)S(1)} %copy-done.2), channel_id=1, replica_groups=mesh['row'=8,'col'=32] {'row'}, dimensions={1}, use_global_device_ids=true | all-gather | bytes 294912 | tf_op jit(solution)/shard_map/all_gather | solution.py:45
  148.2 0.6 fusion.2
  148.8 0.0 copy-done.1
  148.8 0.1 slice_bitcast_fusion
  148.9 25.9 %all-gather.8.cloned.1.call-done = f32[2048,128]{1,0:T(8,128)} async-done(((f32[64,128]{1,0:T(8,128)}), f32[2048,128]{1,0:T(8,128)}) %all-gather.8.cloned.1.call-update) | async-done | bytes 1048592 | tf_op jit(solution)/shard_map/all_gather | solution.py:46
  174.8 1.1 slice_negate_fusion
  175.9 0.2 select_maximum_fusion
  176.1 0.1 copy.8
  176.2 3.0 fusion.17
  179.2 0.0 reduce-scatter.3.cloned.1.call-update
  179.2 0.0 all-gather.10.cloned.1.call-start
  179.3 32.4 %reduce-scatter.3.cloned.1.call-done = f32[256,64]{0,1:T(8,128)} async-done(((f32[2048,64]{0,1:T(8,128)}), f32[256,64]{0,1:T(8,128)}) %reduce-scatter.3.cloned.1.call-update) | async-done | bytes 65552 | tf_op jit(solution)/shard_map/reduce_scatter | solution.py:63
  211.7 0.0 all-gather.10.cloned.1.call-update
  211.7 61.6 %all-gather.10.cloned.1.call-done = f32[2048,256]{1,0:T(8,128)} async-done(((f32[64,256]{1,0:T(8,128)}), f32[2048,256]{1,0:T(8,128)}) %all-gather.10.cloned.1.call-update) | async-done | bytes 2097168 | tf_op jit(solution)/shard_map/all_gather | solution.py:66
  273.3 3.1 copy.39
  276.4 4.4 %all-to-all-start = ((f32[8,2,128,256]{3,2,1,0:T(8,128)}), f32[8,2,128,256]{3,2,1,0:T(8,128)}, u32[]{:S(2)}, u32[]{:S(2)}) async-start(f32[8,2,128,256]{3,2,1,0:T(8,128)} %bitcast.67), calls=%async_computation.1 | async-start | bytes 4194304 | tf_op jit(solution)/shard_map/all_to_all | solution.py:70
  280.8 0.0 slice-start.1
  280.8 0.2 reduce-scatter.5.cloned.1.call-start
  281.1 0.9 slice-done.1
  281.9 6.5 %fusion.9 = f32[2048,704]{0,1:T(8,128)} fusion(f32[2048,256]{1,0:T(8,128)S(1)} %bitcast.64, f32[88,8,2,128]{3,2,1,0:T(2,128)S(1)} %bitcast.72), kind=kOutput, calls=%fused_computation.16 | convolution fusion | flops 4429185024 | bytes 8585216 | tf_op jit(solution)/shard_map/dot_general | solution.py:14
  288.5 18.6 %all-to-all-done = f32[8,2,128,256]{3,2,1,0:T(8,128)} async-done(((f32[8,2,128,256]{3,2,1,0:T(8,128)}), f32[8,2,128,256]{3,2,1,0:T(8,128)}, u32[]{:S(2)}, u32[]{:S(2)}) %all-to-all-start) | async-done | bytes 2097184 | tf_op jit(solution)/shard_map/all_to_all | solution.py:70
  307.1 2.8 copy.12
  309.9 8.5 %convolution_subtract_fusion = f32[2048,704]{0,1:T(8,128)} fusion(f32[2048,704]{0,1:T(8,128)} %fusion.9, f32[256,8,2,128]{3,2,1,0:T(2,128)S(1)} %bitcast.65, f32[88,8,2,128]{3,2,1,0:T(2,128)S(1)} %bitcast.71), kind=kOutput, calls=%fused_computation | convolution fusion | flops 4430626816 | bytes 14352384 | tf_op jit(solution)/shard_map/dot_general | solution.py:14
  318.4 0.0 reduce-scatter.5.cloned.1.call-update
  318.4 67.0 %reduce-scatter.5.cloned.1.call-done = f32[256,704]{0,1:T(8,128)} async-done(((f32[2048,704]{0,1:T(8,128)}), f32[256,704]{0,1:T(8,128)}) %reduce-scatter.5.cloned.1.call-update) | async-done | bytes 720912 | tf_op jit(solution)/shard_map/reduce_scatter | solution.py:73
  385.4 1.2 pad_maximum_fusion
  386.5 1.3 reshape.34
  (7 shorter events, 0.0 us)
Async XLA Ops:
  6.5 62.4 %all-gather.12.cloned.1.call-start = ((), (), s32[]{:S(2)}) async-start(), calls=%async_computation.7 | async-start | bytes 2162688 | tf_op jit(solution)/shard_map/all_gather | solution.py:32
  8.0 115.1 %all-gather.14.cloned.1.call-start = ((), (), s32[]{:S(2)}) async-start(), calls=%async_computation.8 | async-start | bytes 2162688 | tf_op jit(solution)/shard_map/all_gather | solution.py:57
  9.6 165.2 %all-gather.8.cloned.1.call-start = ((), (), s32[]{:S(2)}) async-start(), calls=%async_computation.3 | async-start | bytes 1081344 | tf_op jit(solution)/shard_map/all_gather | solution.py:46
  95.0 116.7 %reduce-scatter.3.cloned.1.call-start = ((), (), s32[]{:S(2)}) async-start(), calls=%async_computation.4 | async-start | bytes 589824 | tf_op jit(solution)/shard_map/reduce_scatter | solution.py:63
  123.2 2.2 copy-start
  125.4 0.8 copy-start.2
  125.4 23.4 %copy-start.1 = (f32[1,2048,2,128]{3,1,2,0:T(8,128)S(1)}, f32[1,2048,2,128]{3,1,2,0:T(8,128)}, u32[]{:S(2)}) copy-start(f32[1,2048,2,128]{3,1,2,0:T(8,128)} %all-gather.12.cloned.1.call-done) | copy-start | bytes 6291460
  179.2 94.1 %all-gather.10.cloned.1.call-start = ((), (), s32[]{:S(2)}) async-start(), calls=%async_computation.5 | async-start | bytes 2162688 | tf_op jit(solution)/shard_map/all_gather | solution.py:66
  276.4 30.6 %all-to-all-start = ((f32[8,2,128,256]{3,2,1,0:T(8,128)}), f32[8,2,128,256]{3,2,1,0:T(8,128)}, u32[]{:S(2)}, u32[]{:S(2)}) async-start(f32[8,2,128,256]{3,2,1,0:T(8,128)} %bitcast.67), calls=%async_computation.1 | async-start | bytes 4194304 | tf_op jit(solution)/shard_map/all_to_all | solution.py:70
  280.8 1.1 slice-start.1
  280.8 104.5 %reduce-scatter.5.cloned.1.call-start = ((), (), s32[]{:S(2)}) async-start(), calls=%async_computation.6 | async-start | bytes 6488064 | tf_op jit(solution)/shard_map/reduce_scatter | solution.py:73
  288.5 21.4 %slice-start = ((f32[12,64,2,128]{3,2,1,0:T(2,128)}), f32[11,64,2,128]{3,2,1,0:T(2,128)S(1)}, s32[]{:S(2)}) async-start(f32[12,64,2,128]{3,2,1,0:T(2,128)} %param.3), calls=%async_computation.9 | async-start | bytes 1441792 | tf_op jit(solution)/shard_map/slice | solution.py:68
  318.4 67.0 %copy-start.3 = (f32[256,64]{0,1:T(8,128)S(1)}, f32[256,64]{0,1:T(8,128)}, u32[]{:S(2)}) copy-start(f32[256,64]{0,1:T(8,128)} %reduce-scatter.3.cloned.1.call-done) | copy-start | bytes 196612
Sparse Core Ops, SparseCore 0:
  10.0 58.9 all-gather.11
  71.5 51.6 all-gather.13
  125.7 49.0 all-gather.7
  179.3 32.3 reduce-scatter.2
  214.4 58.8 all-gather.9
  318.5 66.7 reduce-scatter.4

commit v6 on v5

--- a/solution.py
+++ b/solution.py
@@ -65,19 +65,18 @@
     ).T
     everything = lax.all_gather(solved_lead, "col", axis=0, tiled=True)
 
-    left_rows = lower[1:].reshape(cols_here - strip_width, 2 * row_run)
-    grouped = everything.reshape(2, row_count, row_run, 2 * row_run).transpose(1, 0, 2, 3)
-    swapped = lax.all_to_all(grouped, "row", split_axis=0, concat_axis=0, tiled=True)
-    turned_block = swapped.reshape(row_count, 2, row_run, 2, row_run).transpose(0, 3, 4, 1, 2)
-    turned_block = turned_block.reshape(row_count * 2 * row_run, 2 * row_run)
+    trail_count = cols_here - strip_width
+    copies = jnp.broadcast_to(lower[1:].reshape(1, trail_count, 2, row_run), (row_count, trail_count, 2, row_run))
+    full_left = lax.all_to_all(copies, "row", split_axis=0, concat_axis=0, tiled=True)
+    full_left = full_left.transpose(1, 2, 0, 3).reshape(trail_count, 2 * block_size)
     summed = lax.psum_scatter(
-        times_rows_turned(inverse_cols, strip_rows[strip_width:])
-        - times_rows_turned(turned_block, left_rows),
+        times_rows_turned(inverse_cols, strip_rows[strip_width:]),
         "row",
         scatter_dimension=0,
         tiled=True,
     )
-    reduced = jnp.concatenate([solved_lead, summed.T], axis=0)
+    tail_rows = summed.T - times_rows(full_left, everything)
+    reduced = jnp.concatenate([solved_lead, tail_rows], axis=0)
     return reduced.reshape(rounds, strip_width, 2, row_run)
 
 

time: 395 us -> 374 us (0.947)
  waiting for transfers between devices: 268 us -> 174 us
  blocking collectives: 69.6 us -> 145 us
  starting transfers between devices: 4.78 us -> 0.21 us
    all_to_all x0 -> x1, blocking collectives: none -> 75.7 us  [local(): lax.all_to_all(copies, 'row', split_axis=0, concat_axis=0, tiled=True)]
    all_gather x1, waiting for transfers between devices: 61.6 us -> 0.01 us  [local(): everything = lax.all_gather(solved_lead, 'col', axis=0, tiled=True)]
    all_to_all x1 -> x0, waiting for transfers between devices: 18.6 us -> none  [local(): lax.all_to_all(grouped, 'row', split_axis=0, concat_axis=0, tiled=True)]
    reduce_scatter x1, waiting for transfers between devices: 67 us -> 53.7 us  [local(): lax.psum_scatter(times_rows_turned(inverse_cols, strip_rows[strip_width:]...]
    dot_general x4 -> x5, matrix products: 4.86 us -> 13.8 us  [times_rows(): jnp.dot(coeff, right_side, precision=highest, preferred_element_type=jnp....]
    dot_general x3 -> x2, matrix products: 18 us -> 9.48 us  [times_rows_turned(): lax.dot_general(coeff, right_turned, (((1,), (1,)), ((), ())), precision=...]
    reshape x2 -> x0, local copies, waits for them, and re-layouts: 5.95 us -> none  [the longest x1 3.1 us: local(): everything.reshape(2, row_count, row_run, 2 * row_run).transpose(1, 0, 2, 3)]
    transpose x0 -> x1, local copies, waits for them, and re-layouts: none -> 5.84 us  [local(): full_left.transpose(1, 2, 0, 3).reshape(trail_count, 2 * block_size)]
  transfers between devices with their start and end apart: 7 -> 6, of which waited for: 7 -> 5; matrix products, arithmetic and copies ran while one was open for 4% -> 6% of each run, Pallas kernels for 0% -> 0%
where the time goes in v6:
time: 374 us; the launch traced here: 373 us
  waiting for transfers between devices  174 us (47%)
  blocking collectives  145 us (39%)
  matrix products  23.3 us (6%)
  local copies, waits for them, and re-layouts  15.2 us (4%)
  between operations  13.6 us (4%)
    all_to_all x1, blocking collectives, local(): lax.all_to_all(copies, 'row', split_axis=0, concat_axis=0, tiled=True)  75.7 us
    reduce_scatter x1, waiting for transfers between devices, local(): lax.psum_scatter(times_rows_turned(inverse_cols, strip_rows[strip_width:]...  53.7 us
    all_gather x1, waiting for transfers between devices, local(): gathered = lax.all_gather(lower[0], 'col', axis=0, tiled=True)  34.3 us
    reduce_scatter x1, waiting for transfers between devices, local(): lax.psum_scatter(times_rows_turned(inverse_cols, mixed), 'row', scatter_d...  32.5 us
    all_gather x1, waiting for transfers between devices, local(): strip_lead = lax.all_gather(strip[0], 'col', axis=0, tiled=True)  28.1 us
    all_gather x1, waiting for transfers between devices, local(): lax.all_gather(chained_piece, 'col', axis=0, tiled=True)[block_size:]  25.9 us
    all_gather x1, blocking collectives, local(): own_rows = lax.all_gather(lower[0], 'row', axis=2, tiled=True)  25 us
    all_gather x1, blocking collectives, local(): lax.all_gather(times_rows(own_rows[:, 1, :], cross_cols), 'row', axis=1,...  22.5 us
  transfers between devices with their start and end apart: 6, of which 5 were waited for; matrix products, arithmetic and copies ran while one was open for 6% of the time, Pallas kernels for 0%

profile of v6, /device:TPU:1, one launch (start us, length us, event | category | flops | bytes accessed | tf_op | source)
XLA Modules:
  0.0 373.4 jit_solution(12085110303640853926)
XLA Ops:
  6.5 0.0 all-gather.12.cloned.1.call-start
  6.5 0.8 slice.37
  7.4 0.6 copy.10
  8.0 0.0 all-gather.12.cloned.1.call-update
  8.0 0.0 all-gather.14.cloned.1.call-start
  8.1 1.5 slice_bitcast_fusion.6
  9.6 0.0 all-gather.14.cloned.1.call-update
  9.6 0.0 all-gather.8.cloned.1.call-start
  9.6 25.0 %all-gather.1 = f32[1,64,2,1024]{3,1,2,0:T(8,128)S(1)} all-gather(f32[1,64,2,128]{3,1,2,0:T(8,128)} %copy.10), channel_id=3, replica_groups=mesh['row'=8,'col'=32] {'row'}, dimensions={3}, use_global_device_ids=true | all-gather | bytes 589824 | tf_op jit(solution)/shard_map/all_gather | solution.py:39
  34.6 34.3 %all-gather.12.cloned.1.call-done = f32[1,2048,2,128]{3,1,2,0:T(8,128)} async-done(((f32[1,64,2,128]{3,1,2,0:T(8,128)}), f32[1,2048,2,128]{3,1,2,0:T(8,128)}) %all-gather.12.cloned.1.call-update) | async-done | bytes 2097168 | tf_op jit(solution)/shard_map/all_gather | solution.py:32
  68.9 1.5 fusion.17
  70.4 22.5 %all_gather.23 = f32[64,1024]{1,0:T(8,128)S(1)} all-gather(f32[64,128]{1,0:T(8,128)S(1)} %fusion.17), channel_id=1, replica_groups=mesh['row'=8,'col'=32] {'row'}, dimensions={1}, use_global_device_ids=true | all-gather | bytes 294912 | tf_op jit(solution)/shard_map/all_gather | solution.py:43
  92.9 2.1 fusion.21
  95.0 0.0 all-gather.8.cloned.1.call-update
  95.0 0.0 reduce-scatter.3.cloned.1.call-start
  95.1 28.1 %all-gather.14.cloned.1.call-done = f32[1,2048,2,128]{3,2,0,1:T(2,128)} async-done(((f32[1,64,2,128]{3,2,0,1:T(2,128)}), f32[1,2048,2,128]{3,2,0,1:T(2,128)}) %all-gather.14.cloned.1.call-update) | async-done | bytes 2097168 | tf_op jit(solution)/shard_map/all_gather | solution.py:57
  123.2 1.9 copy.33
  125.1 0.3 copy-done
  125.4 0.1 slice.55
  125.5 0.6 fusion.12
  126.1 0.0 copy-done.2
  126.2 22.0 %all_gather.26 = f32[64,1024]{1,0:T(8,128)S(1)} all-gather(f32[64,128]{1,0:T(8,128)S(1)} %copy-done.2), channel_id=1, replica_groups=mesh['row'=8,'col'=32] {'row'}, dimensions={1}, use_global_device_ids=true | all-gather | bytes 294912 | tf_op jit(solution)/shard_map/all_gather | solution.py:45
  148.2 0.6 fusion.9
  148.8 0.0 copy-done.1
  148.8 0.1 slice_bitcast_fusion
  148.9 25.9 %all-gather.8.cloned.1.call-done = f32[2048,128]{1,0:T(8,128)} async-done(((f32[64,128]{1,0:T(8,128)}), f32[2048,128]{1,0:T(8,128)}) %all-gather.8.cloned.1.call-update) | async-done | bytes 1048592 | tf_op jit(solution)/shard_map/all_gather | solution.py:46
  174.8 1.1 slice_negate_fusion
  175.9 0.2 select_maximum_fusion
  176.1 0.1 copy.7
  176.2 0.0 slice-start.1
  176.3 3.0 fusion.22
  179.2 0.0 reduce-scatter.3.cloned.1.call-update
  179.2 0.0 all-gather.10.cloned.1.call-start
  179.3 32.5 %reduce-scatter.3.cloned.1.call-done = f32[256,64]{0,1:T(8,128)} async-done(((f32[2048,64]{0,1:T(8,128)}), f32[256,64]{0,1:T(8,128)}) %reduce-scatter.3.cloned.1.call-update) | async-done | bytes 65552 | tf_op jit(solution)/shard_map/reduce_scatter | solution.py:63
  211.7 0.0 all-gather.10.cloned.1.call-update
  211.8 0.0 reduce-scatter.5.cloned.1.call-start
  211.8 0.0 slice-done.1
  211.8 6.5 %fusion.14 = f32[2048,704]{0,1:T(8,128)} fusion(f32[2048,256]{1,0:T(8,128)S(1)} %bitcast.60, f32[88,8,2,128]{3,2,1,0:T(2,128)S(1)} %bitcast.68), kind=kOutput, calls=%fused_computation.15 | convolution fusion | flops 4429185024 | bytes 8585216 | tf_op jit(solution)/shard_map/dot_general | solution.py:14
  218.4 0.0 reduce-scatter.5.cloned.1.call-update
  218.4 1.1 slice-done
  219.5 1.5 broadcast_in_dim.14
  220.9 75.7 %all_to_all.5 = f32[8,704,2,128]{3,2,1,0:T(2,128)S(1)} all-to-all(f32[8,704,2,128]{3,2,1,0:T(2,128)S(1)} %broadcast_in_dim.14), channel_id=1, replica_groups=mesh['row'=8,'col'=32] {'row'}, dimensions={0} | all-to-all | bytes 11534336 | tf_op jit(solution)/shard_map/all_to_all | solution.py:70
  296.6 5.8 %copy.9 = f32[704,2,8,128]{3,2,1,0:T(8,128)} copy(f32[704,2,8,128]{3,1,0,2:T(2,128)S(1)} %bitcast.62) | data formatting | bytes 11534336 | tf_op jit(solution)/shard_map/transpose | solution.py:71
  302.5 53.7 %reduce-scatter.5.cloned.1.call-done = f32[256,704]{0,1:T(8,128)} async-done(((f32[2048,704]{0,1:T(8,128)}), f32[256,704]{0,1:T(8,128)}) %reduce-scatter.5.cloned.1.call-update) | async-done | bytes 720912 | tf_op jit(solution)/shard_map/reduce_scatter | solution.py:72
  356.2 9.0 %fusion.6 = f32[704,256]{1,0:T(8,128)S(1)} fusion(f32[256,704]{0,1:T(8,128)} %reduce-scatter.5.cloned.1.call-done, f32[2048,256]{1,0:T(8,128)} %all-gather.10.cloned.1.call-done, f32[88,8,16,128]{3,2,1,0:T(8,128)} %bitcast.61), kind=kOutput, calls=%fused_computation.7 | convolution fusion | flops 4429365248 | bytes 9306112 | tf_op jit(solution)/shard_map/dot_general | solution.py:10
  365.2 0.0 copy-done.3
  365.2 0.1 pad_maximum_fusion
  365.2 1.3 reshape.24
  (6 shorter events, 0.0 us)
Async XLA Ops:
  6.5 62.4 %all-gather.12.cloned.1.call-start = ((), (), s32[]{:S(2)}) async-start(), calls=%async_computation.7 | async-start | bytes 2162688 | tf_op jit(solution)/shard_map/all_gather | solution.py:32
  8.0 115.1 %all-gather.14.cloned.1.call-start = ((), (), s32[]{:S(2)}) async-start(), calls=%async_computation.8 | async-start | bytes 2162688 | tf_op jit(solution)/shard_map/all_gather | solution.py:57
  9.6 165.2 %all-gather.8.cloned.1.call-start = ((), (), s32[]{:S(2)}) async-start(), calls=%async_computation.3 | async-start | bytes 1081344 | tf_op jit(solution)/shard_map/all_gather | solution.py:46
  95.0 116.7 %reduce-scatter.3.cloned.1.call-start = ((), (), s32[]{:S(2)}) async-start(), calls=%async_computation.4 | async-start | bytes 589824 | tf_op jit(solution)/shard_map/reduce_scatter | solution.py:63
  123.2 2.2 copy-start
  125.4 0.8 copy-start.2
  125.4 23.4 %copy-start.1 = (f32[1,2048,2,128]{3,1,2,0:T(8,128)S(1)}, f32[1,2048,2,128]{3,1,2,0:T(8,128)}, u32[]{:S(2)}) copy-start(f32[1,2048,2,128]{3,1,2,0:T(8,128)} %all-gather.12.cloned.1.call-done) | copy-start | bytes 6291460
  176.2 35.6 %slice-start.1 = ((f32[12,64,2,128]{3,2,1,0:T(2,128)}), f32[11,64,2,128]{3,2,1,0:T(2,128)S(1)}, s32[]{:S(2)}) async-start(f32[12,64,2,128]{3,2,1,0:T(2,128)} %param.2), calls=%async_computation.10 | async-start | bytes 1441792 | tf_op jit(solution)/shard_map/slice | solution.py:73
  179.2 123.2 %all-gather.10.cloned.1.call-start = ((), (), s32[]{:S(2)}) async-start(), calls=%async_computation.6 | async-start | bytes 2162688 | tf_op jit(solution)/shard_map/all_gather | solution.py:66
  211.8 144.4 %reduce-scatter.5.cloned.1.call-start = ((), (), s32[]{:S(2)}) async-start(), calls=%async_computation.5 | async-start | bytes 6488064 | tf_op jit(solution)/shard_map/reduce_scatter | solution.py:72
  218.4 1.1 slice-start
  356.2 9.0 %copy-start.3 = (f32[256,64]{0,1:T(8,128)S(1)}, f32[256,64]{0,1:T(8,128)}, u32[]{:S(2)}) copy-start(f32[256,64]{0,1:T(8,128)} %reduce-scatter.3.cloned.1.call-done) | copy-start | bytes 196612
Sparse Core Ops, SparseCore 0:
  10.0 58.9 all-gather.11
  71.5 51.6 all-gather.13
  125.7 49.0 all-gather.7
  179.4 32.3 reduce-scatter.2
  214.5 60.9 all-gather.9
  278.0 78.1 reduce-scatter.4

commit v7 on v6

--- a/solution.py
+++ b/solution.py
@@ -66,16 +66,18 @@
     everything = lax.all_gather(solved_lead, "col", axis=0, tiled=True)
 
     trail_count = cols_here - strip_width
-    copies = jnp.broadcast_to(lower[1:].reshape(1, trail_count, 2, row_run), (row_count, trail_count, 2, row_run))
-    full_left = lax.all_to_all(copies, "row", split_axis=0, concat_axis=0, tiled=True)
-    full_left = full_left.transpose(1, 2, 0, 3).reshape(trail_count, 2 * block_size)
+    trail_part = lower[1:].reshape(trail_count, 2, 1, row_run)
+    copies = jnp.broadcast_to(trail_part, (trail_count, 2, row_count, row_run))
+    full_left = lax.all_to_all(copies, "row", split_axis=2, concat_axis=2, tiled=True)
+    full_left = full_left.reshape(trail_count, 2 * block_size)
+    left_update = lax.optimization_barrier(times_rows(full_left, everything))
     summed = lax.psum_scatter(
         times_rows_turned(inverse_cols, strip_rows[strip_width:]),
         "row",
         scatter_dimension=0,
         tiled=True,
     )
-    tail_rows = summed.T - times_rows(full_left, everything)
+    tail_rows = summed.T - left_update
     reduced = jnp.concatenate([solved_lead, tail_rows], axis=0)
     return reduced.reshape(rounds, strip_width, 2, row_run)
 

time: 374 us -> 366 us (0.979)
  waiting for transfers between devices: 174 us -> 165 us
    reduce_scatter x1, waiting for transfers between devices: 53.7 us -> 44.5 us  [local(): lax.psum_scatter(times_rows_turned(inverse_cols, strip_rows[strip_width:]...]
    all_to_all x0 -> x1, local copies, waits for them, and re-layouts: none -> 5.86 us  [local(): lax.all_to_all(copies, 'row', split_axis=2, concat_axis=2, tiled=True)]
    transpose x1 -> x0, local copies, waits for them, and re-layouts: 5.84 us -> none  [local(): full_left.transpose(1, 2, 0, 3).reshape(trail_count, 2 * block_size)]
  transfers between devices with their start and end apart: 6 -> 6, of which waited for: 5 -> 5; matrix products, arithmetic and copies ran while one was open for 6% -> 9% of each run, Pallas kernels for 0% -> 0%
where the time goes in v7:
time: 366 us
  waiting for transfers between devices  165 us (45%)
  blocking collectives  145 us (40%)
  matrix products  23.6 us (6%)
  local copies, waits for them, and re-layouts  15.2 us (4%)
  between operations  13.6 us (4%)
    all_to_all x1, blocking collectives, local(): lax.all_to_all(copies, 'row', split_axis=2, concat_axis=2, tiled=True)  75.7 us
    reduce_scatter x1, waiting for transfers between devices, local(): lax.psum_scatter(times_rows_turned(inverse_cols, strip_rows[strip_width:]...  44.5 us
    all_gather x1, waiting for transfers between devices, local(): gathered = lax.all_gather(lower[0], 'col', axis=0, tiled=True)  34.3 us
    reduce_scatter x1, waiting for transfers between devices, local(): lax.psum_scatter(times_rows_turned(inverse_cols, mixed), 'row', scatter_d...  32.5 us
    all_gather x1, waiting for transfers between devices, local(): strip_lead = lax.all_gather(strip[0], 'col', axis=0, tiled=True)  28.1 us
    all_gather x1, waiting for transfers between devices, local(): lax.all_gather(chained_piece, 'col', axis=0, tiled=True)[block_size:]  25.9 us
    all_gather x1, blocking collectives, local(): own_rows = lax.all_gather(lower[0], 'row', axis=2, tiled=True)  25 us
    all_gather x1, blocking collectives, local(): lax.all_gather(times_rows(own_rows[:, 1, :], cross_cols), 'row', axis=1,...  22.5 us
  transfers between devices with their start and end apart: 6, of which 5 were waited for; matrix products, arithmetic and copies ran while one was open for 9% of the time, Pallas kernels for 0%

profile of v7, /device:TPU:1, one launch (start us, length us, event | category | flops | bytes accessed | tf_op | source)
XLA Modules:
  0.0 365.6 jit_solution(11977548743183644814)
XLA Ops:
  6.5 0.0 all-gather.12.cloned.1.call-start
  6.5 0.8 slice.37
  7.4 0.6 copy.13
  8.0 0.0 all-gather.12.cloned.1.call-update
  8.0 0.0 all-gather.14.cloned.1.call-start
  8.1 1.5 slice_bitcast_fusion.6
  9.6 0.0 all-gather.14.cloned.1.call-update
  9.6 0.0 all-gather.8.cloned.1.call-start
  9.6 25.0 %all-gather.1 = f32[1,64,2,1024]{3,1,2,0:T(8,128)S(1)} all-gather(f32[1,64,2,128]{3,1,2,0:T(8,128)} %copy.13), channel_id=3, replica_groups=mesh['row'=8,'col'=32] {'row'}, dimensions={3}, use_global_device_ids=true | all-gather | bytes 589824 | tf_op jit(solution)/shard_map/all_gather | solution.py:39
  34.6 34.3 %all-gather.12.cloned.1.call-done = f32[1,2048,2,128]{3,1,2,0:T(8,128)} async-done(((f32[1,64,2,128]{3,1,2,0:T(8,128)}), f32[1,2048,2,128]{3,1,2,0:T(8,128)}) %all-gather.12.cloned.1.call-update) | async-done | bytes 2097168 | tf_op jit(solution)/shard_map/all_gather | solution.py:32
  68.9 1.5 fusion.14
  70.4 22.5 %all_gather.23 = f32[64,1024]{1,0:T(8,128)S(1)} all-gather(f32[64,128]{1,0:T(8,128)S(1)} %fusion.14), channel_id=1, replica_groups=mesh['row'=8,'col'=32] {'row'}, dimensions={1}, use_global_device_ids=true | all-gather | bytes 294912 | tf_op jit(solution)/shard_map/all_gather | solution.py:43
  92.9 2.1 fusion.18
  95.0 0.0 all-gather.8.cloned.1.call-update
  95.0 0.0 reduce-scatter.3.cloned.1.call-start
  95.1 28.1 %all-gather.14.cloned.1.call-done = f32[1,2048,2,128]{3,2,0,1:T(2,128)} async-done(((f32[1,64,2,128]{3,2,0,1:T(2,128)}), f32[1,2048,2,128]{3,2,0,1:T(2,128)}) %all-gather.14.cloned.1.call-update) | async-done | bytes 2097168 | tf_op jit(solution)/shard_map/all_gather | solution.py:57
  123.2 1.9 copy.34
  125.1 0.3 copy-done
  125.4 0.1 slice.55
  125.5 0.6 fusion.9
  126.1 0.0 copy-done.2
  126.2 22.0 %all_gather.26 = f32[64,1024]{1,0:T(8,128)S(1)} all-gather(f32[64,128]{1,0:T(8,128)S(1)} %copy-done.2), channel_id=1, replica_groups=mesh['row'=8,'col'=32] {'row'}, dimensions={1}, use_global_device_ids=true | all-gather | bytes 294912 | tf_op jit(solution)/shard_map/all_gather | solution.py:45
  148.2 0.6 fusion.6
  148.8 0.0 copy-done.1
  148.8 0.1 slice_bitcast_fusion
  148.9 25.9 %all-gather.8.cloned.1.call-done = f32[2048,128]{1,0:T(8,128)} async-done(((f32[64,128]{1,0:T(8,128)}), f32[2048,128]{1,0:T(8,128)}) %all-gather.8.cloned.1.call-update) | async-done | bytes 1048592 | tf_op jit(solution)/shard_map/all_gather | solution.py:46
  174.8 1.1 slice_negate_fusion
  175.9 0.2 select_maximum_fusion
  176.1 0.1 copy.10
  176.2 0.0 slice-start.1
  176.3 3.0 fusion.19
  179.2 0.0 reduce-scatter.3.cloned.1.call-update
  179.2 0.0 all-gather.10.cloned.1.call-start
  179.3 32.5 %reduce-scatter.3.cloned.1.call-done = f32[256,64]{0,1:T(8,128)} async-done(((f32[2048,64]{0,1:T(8,128)}), f32[256,64]{0,1:T(8,128)}) %reduce-scatter.3.cloned.1.call-update) | async-done | bytes 65552 | tf_op jit(solution)/shard_map/reduce_scatter | solution.py:63
  211.7 0.0 all-gather.10.cloned.1.call-update
  211.8 0.0 reduce-scatter.5.cloned.1.call-start
  211.8 6.6 %fusion.11 = f32[2048,704]{0,1:T(8,128)} fusion(f32[2048,256]{1,0:T(8,128)S(1)} %bitcast.59, f32[88,8,2,128]{3,2,1,0:T(2,128)S(1)} %bitcast.66), kind=kOutput, calls=%fused_computation.14 | convolution fusion | flops 4429185024 | bytes 8585216 | tf_op jit(solution)/shard_map/dot_general | solution.py:14
  218.4 0.0 reduce-scatter.5.cloned.1.call-update
  218.4 1.1 slice-done
  219.5 1.5 broadcast_in_dim.14
  221.0 75.7 %all_to_all.5 = f32[704,2,8,128]{3,1,0,2:T(2,128)S(1)} all-to-all(f32[704,2,8,128]{3,1,0,2:T(2,128)S(1)} %broadcast_in_dim.14), channel_id=1, replica_groups=mesh['row'=8,'col'=32] {'row'}, dimensions={2} | all-to-all | bytes 11534336 | tf_op jit(solution)/shard_map/all_to_all | solution.py:71
  296.7 5.9 %copy.12 = f32[704,2,8,128]{3,2,1,0:T(8,128)} copy(f32[704,2,8,128]{3,1,0,2:T(2,128)S(1)} %all_to_all.5) | data formatting | bytes 11534336 | tf_op jit(solution)/shard_map/all_to_all | solution.py:71
  302.5 9.2 %fusion.3 = f32[704,256]{1,0:T(8,128)S(1)} fusion(f32[2048,256]{1,0:T(8,128)} %all-gather.10.cloned.1.call-done, f32[88,8,16,128]{3,2,1,0:T(8,128)} %bitcast.60), kind=kOutput, calls=%fused_computation.6 | convolution fusion | flops 4429185024 | bytes 8585216 | tf_op jit(solution)/shard_map/dot_general | solution.py:10
  311.8 0.0 copy-start.3
  311.8 44.5 %reduce-scatter.5.cloned.1.call-done = f32[256,704]{0,1:T(8,128)} async-done(((f32[2048,704]{0,1:T(8,128)}), f32[256,704]{0,1:T(8,128)}) %reduce-scatter.5.cloned.1.call-update) | async-done | bytes 720912 | tf_op jit(solution)/shard_map/reduce_scatter | solution.py:74
  356.2 1.2 bitcast_subtract_fusion
  357.4 0.1 pad_maximum_fusion
  357.5 1.3 reshape.24
  (7 shorter events, 0.0 us)
Async XLA Ops:
  6.5 62.4 %all-gather.12.cloned.1.call-start = ((), (), s32[]{:S(2)}) async-start(), calls=%async_computation.7 | async-start | bytes 2162688 | tf_op jit(solution)/shard_map/all_gather | solution.py:32
  8.0 115.1 %all-gather.14.cloned.1.call-start = ((), (), s32[]{:S(2)}) async-start(), calls=%async_computation.8 | async-start | bytes 2162688 | tf_op jit(solution)/shard_map/all_gather | solution.py:57
  9.6 165.2 %all-gather.8.cloned.1.call-start = ((), (), s32[]{:S(2)}) async-start(), calls=%async_computation.3 | async-start | bytes 1081344 | tf_op jit(solution)/shard_map/all_gather | solution.py:46
  95.0 116.7 %reduce-scatter.3.cloned.1.call-start = ((), (), s32[]{:S(2)}) async-start(), calls=%async_computation.4 | async-start | bytes 589824 | tf_op jit(solution)/shard_map/reduce_scatter | solution.py:63
  123.2 2.2 copy-start
  125.4 0.8 copy-start.2
  125.4 23.4 %copy-start.1 = (f32[1,2048,2,128]{3,1,2,0:T(8,128)S(1)}, f32[1,2048,2,128]{3,1,2,0:T(8,128)}, u32[]{:S(2)}) copy-start(f32[1,2048,2,128]{3,1,2,0:T(8,128)} %all-gather.12.cloned.1.call-done) | copy-start | bytes 6291460
  176.2 35.6 %slice-start.1 = ((f32[12,64,2,128]{3,2,1,0:T(2,128)}), f32[11,64,2,128]{3,2,1,0:T(2,128)S(1)}, s32[]{:S(2)}) async-start(f32[12,64,2,128]{3,2,1,0:T(2,128)} %param.2), calls=%async_computation.10 | async-start | bytes 1441792 | tf_op jit(solution)/shard_map/slice | solution.py:75
  179.2 123.3 %all-gather.10.cloned.1.call-start = ((), (), s32[]{:S(2)}) async-start(), calls=%async_computation.6 | async-start | bytes 2162688 | tf_op jit(solution)/shard_map/all_gather | solution.py:66
  211.8 144.5 %reduce-scatter.5.cloned.1.call-start = ((), (), s32[]{:S(2)}) async-start(), calls=%async_computation.5 | async-start | bytes 6488064 | tf_op jit(solution)/shard_map/reduce_scatter | solution.py:74
  218.4 1.1 slice-start
  311.8 45.7 %copy-start.3 = (f32[256,64]{0,1:T(8,128)S(1)}, f32[256,64]{0,1:T(8,128)}, u32[]{:S(2)}) copy-start(f32[256,64]{0,1:T(8,128)} %reduce-scatter.3.cloned.1.call-done) | copy-start | bytes 196612
Sparse Core Ops, SparseCore 0:
  10.0 58.9 all-gather.11
  71.5 51.6 all-gather.13
  125.7 49.0 all-gather.7
  179.4 32.3 reduce-scatter.2
  214.5 60.9 all-gather.9
  278.0 78.1 reduce-scatter.4

commit v8 on v7

--- a/solution.py
+++ b/solution.py
@@ -43,7 +43,10 @@
     cross_mix = lax.all_gather(times_rows(own_rows[:, 1, :], cross_cols), "row", axis=1, tiled=True)
     chained_piece = times_rows(cross_mix, first_cols)
     chained = lax.all_gather(chained_piece, "row", axis=1, tiled=True)
-    chained_cols = lax.all_gather(chained_piece, "col", axis=0, tiled=True)[block_size:]
+    joined = jnp.concatenate([strip[0].reshape(strip_width, 2 * row_run), chained_piece], axis=1)
+    joined = lax.all_gather(joined, "col", axis=0, tiled=True)
+    strip_lead = joined[:, : 2 * row_run]
+    chained_cols = joined[block_size:, 2 * row_run :]
 
     inverse_cols = jnp.concatenate(
         [
@@ -54,8 +57,6 @@
     )
     inverse_cols = inverse_cols.reshape(2, row_count, row_run, 2 * row_run).transpose(1, 0, 2, 3)
     inverse_cols = inverse_cols.reshape(2 * block_size, 2 * row_run)
-    strip_lead = lax.all_gather(strip[0], "col", axis=0, tiled=True)
-    strip_lead = strip_lead.reshape(2 * block_size, 2 * row_run)
     strip_first = strip_lead[:block_size]
     strip_diag = lax.dynamic_slice_in_dim(strip_lead, lower_half * block_size, block_size, 0)
     chained_term = jnp.where(below, times_rows(chained, strip_first), 0.0)

time: 366 us -> 351 us (0.959)
  waiting for transfers between devices: 165 us -> 150 us
    all_gather x2 -> x1, waiting for transfers between devices: 53.9 us -> 37.3 us  [local(): joined = lax.all_gather(joined, 'col', axis=0, tiled=True)]
  transfers between devices with their start and end apart: 6 -> 5, of which waited for: 5 -> 4; matrix products, arithmetic and copies ran while one was open for 9% -> 7% of each run, Pallas kernels for 0% -> 0%
where the time goes in v8:
time: 351 us; the launch traced here: 350 us
  waiting for transfers between devices  150 us (43%)
  blocking collectives  145 us (41%)
  matrix products  23.1 us (7%)
  local copies, waits for them, and re-layouts  14.9 us (4%)
  between operations  13.3 us (4%)
  other arithmetic  4.23 us (1%)
    all_to_all x1, blocking collectives, local(): lax.all_to_all(copies, 'row', split_axis=2, concat_axis=2, tiled=True)  75.6 us
    reduce_scatter x1, waiting for transfers between devices, local(): lax.psum_scatter(times_rows_turned(inverse_cols, strip_rows[strip_width:]...  44.5 us
    all_gather x1, waiting for transfers between devices, local(): joined = lax.all_gather(joined, 'col', axis=0, tiled=True)  37.3 us
    all_gather x1, waiting for transfers between devices, local(): gathered = lax.all_gather(lower[0], 'col', axis=0, tiled=True)  35 us
    reduce_scatter x1, waiting for transfers between devices, local(): lax.psum_scatter(times_rows_turned(inverse_cols, mixed), 'row', scatter_d...  32.8 us
    all_gather x1, blocking collectives, local(): own_rows = lax.all_gather(lower[0], 'row', axis=2, tiled=True)  25 us
    all_gather x1, blocking collectives, local(): chained = lax.all_gather(chained_piece, 'row', axis=1, tiled=True)  22.2 us
    all_gather x1, blocking collectives, local(): lax.all_gather(times_rows(own_rows[:, 1, :], cross_cols), 'row', axis=1,...  22 us
  transfers between devices with their start and end apart: 5, of which 4 were waited for; matrix products, arithmetic and copies ran while one was open for 7% of the time, Pallas kernels for 0%

profile of v8, /device:TPU:1, one launch (start us, length us, event | category | flops | bytes accessed | tf_op | source)
XLA Modules:
  0.0 350.2 jit_solution(1414454222778146429)
XLA Ops:
  6.5 0.0 all-gather.10.cloned.1.call-start
  6.5 0.8 slice.38
  7.4 0.6 copy.12
  8.0 0.0 all-gather.10.cloned.1.call-update
  8.0 0.0 all-gather.6.cloned.1.call-start
  8.1 0.8 slice.40
  8.9 25.0 %all-gather.1 = f32[1,64,2,1024]{3,1,2,0:T(8,128)S(1)} all-gather(f32[1,64,2,128]{3,1,2,0:T(8,128)} %copy.12), channel_id=3, replica_groups=mesh['row'=8,'col'=32] {'row'}, dimensions={3}, use_global_device_ids=true | all-gather | bytes 589824 | tf_op jit(solution)/shard_map/all_gather | solution.py:39
  34.0 35.0 %all-gather.10.cloned.1.call-done = f32[1,2048,2,128]{3,1,2,0:T(8,128)} async-done(((f32[1,64,2,128]{3,1,2,0:T(8,128)}), f32[1,2048,2,128]{3,1,2,0:T(8,128)}) %all-gather.10.cloned.1.call-update) | async-done | bytes 2097168 | tf_op jit(solution)/shard_map/all_gather | solution.py:32
  68.9 1.6 fusion.13
  70.5 22.0 %all_gather.20 = f32[64,1024]{1,0:T(8,128)S(1)} all-gather(f32[64,128]{1,0:T(8,128)S(1)} %fusion.13), channel_id=1, replica_groups=mesh['row'=8,'col'=32] {'row'}, dimensions={1}, use_global_device_ids=true | all-gather | bytes 294912 | tf_op jit(solution)/shard_map/all_gather | solution.py:43
  92.6 1.5 fusion.17
  94.0 0.7 pad_maximum_fusion.1
  94.7 0.0 all-gather.6.cloned.1.call-update
  94.7 0.0 reduce-scatter.3.cloned.1.call-start
  94.8 22.2 %all_gather.22 = f32[64,1024]{1,0:T(8,128)S(1)} all-gather(f32[64,128]{1,0:T(8,128)S(1)} %fusion.17), channel_id=1, replica_groups=mesh['row'=8,'col'=32] {'row'}, dimensions={1}, use_global_device_ids=true | all-gather | bytes 294912 | tf_op jit(solution)/shard_map/all_gather | solution.py:45
  117.0 0.0 copy-done.1
  117.0 0.9 slice_bitcast_fusion
  117.8 37.3 %all-gather.6.cloned.1.call-done = f32[2048,384]{1,0:T(8,128)} async-done(((f32[64,384]{1,0:T(8,128)}), f32[2048,384]{1,0:T(8,128)}) %all-gather.6.cloned.1.call-update) | async-done | bytes 3145744 | tf_op jit(solution)/shard_map/all_gather | solution.py:47
  155.1 1.1 slice_negate_fusion
  156.2 1.2 select_maximum_fusion
  157.4 0.1 copy.10
  157.6 0.0 slice-start
  157.6 0.0 copy-start
  157.6 1.6 slice-done
  159.2 0.6 fusion.8
  159.8 0.3 copy-done
  160.1 0.6 fusion.6
  160.7 0.0 slice-start.2
  160.8 3.0 fusion.18
  163.7 0.0 reduce-scatter.3.cloned.1.call-update
  163.7 0.0 all-gather.8.cloned.1.call-start
  163.8 32.8 %reduce-scatter.3.cloned.1.call-done = f32[256,64]{0,1:T(8,128)} async-done(((f32[2048,64]{0,1:T(8,128)}), f32[256,64]{0,1:T(8,128)}) %reduce-scatter.3.cloned.1.call-update) | async-done | bytes 65552 | tf_op jit(solution)/shard_map/reduce_scatter | solution.py:64
  196.6 0.0 all-gather.8.cloned.1.call-update
  196.6 0.0 reduce-scatter.5.cloned.1.call-start
  196.7 0.0 slice-done.2
  196.7 6.6 %fusion.10 = f32[2048,704]{0,1:T(8,128)} fusion(f32[2048,256]{1,0:T(8,128)S(1)} %bitcast.50, f32[88,8,2,128]{3,2,1,0:T(2,128)S(1)} %bitcast.54), kind=kOutput, calls=%fused_computation.12 | convolution fusion | flops 4429185024 | bytes 8585216 | tf_op jit(solution)/shard_map/dot_general | solution.py:14
  203.3 0.0 reduce-scatter.5.cloned.1.call-update
  203.3 1.1 slice-done.1
  204.4 1.5 broadcast_in_dim.14
  205.9 75.6 %all_to_all.5 = f32[704,2,8,128]{3,1,0,2:T(2,128)S(1)} all-to-all(f32[704,2,8,128]{3,1,0,2:T(2,128)S(1)} %broadcast_in_dim.14), channel_id=1, replica_groups=mesh['row'=8,'col'=32] {'row'}, dimensions={2} | all-to-all | bytes 11534336 | tf_op jit(solution)/shard_map/all_to_all | solution.py:72
  281.5 5.9 %copy.11 = f32[704,2,8,128]{3,2,1,0:T(8,128)} copy(f32[704,2,8,128]{3,1,0,2:T(2,128)S(1)} %all_to_all.5) | data formatting | bytes 11534336 | tf_op jit(solution)/shard_map/all_to_all | solution.py:72
  287.4 9.2 %fusion.3 = f32[704,256]{1,0:T(8,128)S(1)} fusion(f32[2048,256]{1,0:T(8,128)} %all-gather.8.cloned.1.call-done, f32[88,8,16,128]{3,2,1,0:T(8,128)} %bitcast.51), kind=kOutput, calls=%fused_computation.5 | convolution fusion | flops 4429185024 | bytes 8585216 | tf_op jit(solution)/shard_map/dot_general | solution.py:10
  296.6 0.0 copy-start.2
  296.6 44.5 %reduce-scatter.5.cloned.1.call-done = f32[256,704]{0,1:T(8,128)} async-done(((f32[2048,704]{0,1:T(8,128)}), f32[256,704]{0,1:T(8,128)}) %reduce-scatter.5.cloned.1.call-update) | async-done | bytes 720912 | tf_op jit(solution)/shard_map/reduce_scatter | solution.py:75
  341.1 1.2 bitcast_subtract_fusion
  342.3 0.0 copy-done.2
  342.4 0.1 pad_maximum_fusion
  342.4 1.3 reshape.19
  (4 shorter events, 0.0 us)
Async XLA Ops:
  6.5 62.4 %all-gather.10.cloned.1.call-start = ((), (), s32[]{:S(2)}) async-start(), calls=%async_computation.7 | async-start | bytes 2162688 | tf_op jit(solution)/shard_map/all_gather | solution.py:32
  8.0 147.1 %all-gather.6.cloned.1.call-start = ((), (), s32[]{:S(2)}) async-start(), calls=%async_computation.3 | async-start | bytes 3244032 | tf_op jit(solution)/shard_map/all_gather | solution.py:47
  68.9 48.1 %copy-start.1 = (f32[1,2048,2,128]{3,1,2,0:T(8,128)S(1)}, f32[1,2048,2,128]{3,1,2,0:T(8,128)}, u32[]{:S(2)}) copy-start(f32[1,2048,2,128]{3,1,2,0:T(8,128)} %all-gather.10.cloned.1.call-done) | copy-start | bytes 6291460
  94.7 101.9 %reduce-scatter.3.cloned.1.call-start = ((), (), s32[]{:S(2)}) async-start(), calls=%async_computation.4 | async-start | bytes 589824 | tf_op jit(solution)/shard_map/reduce_scatter | solution.py:64
  157.6 1.6 slice-start
  157.6 2.5 copy-start
  160.7 35.9 %slice-start.2 = ((f32[12,64,2,128]{3,2,1,0:T(2,128)}), f32[11,64,2,128]{3,2,1,0:T(2,128)S(1)}, s32[]{:S(2)}) async-start(f32[12,64,2,128]{3,2,1,0:T(2,128)} %param.2), calls=%async_computation.10 | async-start | bytes 1441792 | tf_op jit(solution)/shard_map/slice | solution.py:76
  163.7 123.6 %all-gather.8.cloned.1.call-start = ((), (), s32[]{:S(2)}) async-start(), calls=%async_computation.6 | async-start | bytes 2162688 | tf_op jit(solution)/shard_map/all_gather | solution.py:67
  196.6 144.5 %reduce-scatter.5.cloned.1.call-start = ((), (), s32[]{:S(2)}) async-start(), calls=%async_computation.5 | async-start | bytes 6488064 | tf_op jit(solution)/shard_map/reduce_scatter | solution.py:75
  203.3 1.1 slice-start.1
  296.6 45.7 %copy-start.2 = (f32[256,64]{0,1:T(8,128)S(1)}, f32[256,64]{0,1:T(8,128)}, u32[]{:S(2)}) copy-start(f32[256,64]{0,1:T(8,128)} %reduce-scatter.3.cloned.1.call-done) | copy-start | bytes 196612
Sparse Core Ops, SparseCore 0:
  10.0 58.9 all-gather.9
  94.8 60.2 all-gather.5
  163.9 32.7 reduce-scatter.2
  199.4 60.9 all-gather.7
  263.0 78.1 reduce-scatter.4

commit v9 on v8

--- a/solution.py
+++ b/solution.py
@@ -61,9 +61,9 @@
     strip_diag = lax.dynamic_slice_in_dim(strip_lead, lower_half * block_size, block_size, 0)
     chained_term = jnp.where(below, times_rows(chained, strip_first), 0.0)
     mixed = times_rows(diag_rows, strip_diag) - chained_term
-    solved_lead = lax.psum_scatter(
-        times_rows_turned(inverse_cols, mixed), "row", scatter_dimension=0, tiled=True
-    ).T
+    lead_parts = times_rows_turned(inverse_cols, mixed).reshape(row_count, 2 * row_run, strip_width)
+    lead_parts = lax.all_to_all(lead_parts, "row", split_axis=0, concat_axis=0, tiled=True)
+    solved_lead = lead_parts.sum(axis=0).T
     everything = lax.all_gather(solved_lead, "col", axis=0, tiled=True)
 
     trail_count = cols_here - strip_width

time: 351 us -> 332 us (0.946)
  waiting for transfers between devices: 150 us -> 96 us
  blocking collectives: 145 us -> 180 us
    reduce_scatter x1 -> x0, waiting for transfers between devices: 32.8 us -> none  [local(): lax.psum_scatter(times_rows_turned(inverse_cols, mixed), 'row', scatter_d...]
    all_to_all x1, blocking collectives: 75.6 us -> 97.8 us  [local(): lax.all_to_all(copies, 'row', split_axis=2, concat_axis=2, tiled=True)]
    reduce_scatter x1, waiting for transfers between devices: 44.5 us -> 23.7 us  [local(): lax.psum_scatter(times_rows_turned(inverse_cols, strip_rows[strip_width:]...]
    all_to_all x0 -> x1, blocking collectives: none -> 13.1 us  [local(): lax.all_to_all(lead_parts, 'row', split_axis=0, concat_axis=0, tiled=True)]
  transfers between devices with their start and end apart: 5 -> 4, of which waited for: 4 -> 3; matrix products, arithmetic and copies ran while one was open for 7% -> 8% of each run, Pallas kernels for 0% -> 0%
where the time goes in v9:
time: 332 us
  blocking collectives  180 us (54%)
  waiting for transfers between devices  96 us (29%)
  matrix products  22.4 us (7%)
  local copies, waits for them, and re-layouts  14.9 us (4%)
  between operations  13.3 us (4%)
  other arithmetic  4.91 us (1%)
    all_to_all x1, blocking collectives, local(): lax.all_to_all(copies, 'row', split_axis=2, concat_axis=2, tiled=True)  97.8 us
    all_gather x1, waiting for transfers between devices, local(): joined = lax.all_gather(joined, 'col', axis=0, tiled=True)  37.3 us
    all_gather x1, waiting for transfers between devices, local(): gathered = lax.all_gather(lower[0], 'col', axis=0, tiled=True)  35 us
    all_gather x1, blocking collectives, local(): own_rows = lax.all_gather(lower[0], 'row', axis=2, tiled=True)  25 us
    reduce_scatter x1, waiting for transfers between devices, local(): lax.psum_scatter(times_rows_turned(inverse_cols, strip_rows[strip_width:]...  23.7 us
    all_gather x1, blocking collectives, local(): chained = lax.all_gather(chained_piece, 'row', axis=1, tiled=True)  22.2 us
    all_gather x1, blocking collectives, local(): lax.all_gather(times_rows(own_rows[:, 1, :], cross_cols), 'row', axis=1,...  22 us
    dot_general x5, matrix products, times_rows(): jnp.dot(coeff, right_side, precision=highest, preferred_element_type=jnp....  13.6 us
  transfers between devices with their start and end apart: 4, of which 3 were waited for; matrix products, arithmetic and copies ran while one was open for 8% of the time, Pallas kernels for 0%

profile of v9, /device:TPU:1, one launch (start us, length us, event | category | flops | bytes accessed | tf_op | source)
XLA Modules:
  0.0 331.8 jit_solution(11375186526555395596)
XLA Ops:
  6.5 0.0 all-gather.10.cloned.1.call-start
  6.5 0.8 slice.38
  7.4 0.6 copy.12
  8.0 0.0 all-gather.10.cloned.1.call-update
  8.0 0.0 all-gather.6.cloned.1.call-start
  8.1 0.8 slice.40
  8.9 25.0 %all-gather.1 = f32[1,64,2,1024]{3,1,2,0:T(8,128)S(1)} all-gather(f32[1,64,2,128]{3,1,2,0:T(8,128)} %copy.12), channel_id=3, replica_groups=mesh['row'=8,'col'=32] {'row'}, dimensions={3}, use_global_device_ids=true | all-gather | bytes 589824 | tf_op jit(solution)/shard_map/all_gather | solution.py:39
  34.0 35.0 %all-gather.10.cloned.1.call-done = f32[1,2048,2,128]{3,1,2,0:T(8,128)} async-done(((f32[1,64,2,128]{3,1,2,0:T(8,128)}), f32[1,2048,2,128]{3,1,2,0:T(8,128)}) %all-gather.10.cloned.1.call-update) | async-done | bytes 2097168 | tf_op jit(solution)/shard_map/all_gather | solution.py:32
  68.9 0.0 copy-start.1
  68.9 1.6 fusion.14
  70.5 22.0 %all_gather.20 = f32[64,1024]{1,0:T(8,128)S(1)} all-gather(f32[64,128]{1,0:T(8,128)S(1)} %fusion.14), channel_id=1, replica_groups=mesh['row'=8,'col'=32] {'row'}, dimensions={1}, use_global_device_ids=true | all-gather | bytes 294912 | tf_op jit(solution)/shard_map/all_gather | solution.py:43
  92.6 1.5 fusion.18
  94.0 0.7 pad_maximum_fusion.1
  94.7 0.0 all-gather.6.cloned.1.call-update
  94.7 0.0 all-gather.8.cloned.1.call-start
  94.8 22.2 %all_gather.22 = f32[64,1024]{1,0:T(8,128)S(1)} all-gather(f32[64,128]{1,0:T(8,128)S(1)} %fusion.18), channel_id=1, replica_groups=mesh['row'=8,'col'=32] {'row'}, dimensions={1}, use_global_device_ids=true | all-gather | bytes 294912 | tf_op jit(solution)/shard_map/all_gather | solution.py:45
  117.0 0.0 copy-done.1
  117.0 0.9 slice_bitcast_fusion
  117.8 37.3 %all-gather.6.cloned.1.call-done = f32[2048,384]{1,0:T(8,128)} async-done(((f32[64,384]{1,0:T(8,128)}), f32[2048,384]{1,0:T(8,128)}) %all-gather.6.cloned.1.call-update) | async-done | bytes 3145744 | tf_op jit(solution)/shard_map/all_gather | solution.py:47
  155.1 1.1 slice_negate_fusion
  156.2 1.2 select_maximum_fusion
  157.5 0.1 copy.10
  157.6 0.0 slice-start
  157.6 0.0 copy-start
  157.6 1.6 slice-done
  159.2 0.6 fusion.9
  159.8 0.3 copy-done
  160.1 0.6 fusion.7
  160.8 2.2 fusion.19
  162.9 0.0 slice-start.2
  162.9 13.1 %all_to_all.10 = f32[8,256,64]{1,2,0:T(8,128)S(1)} all-to-all(f32[8,256,64]{1,2,0:T(8,128)S(1)} %fusion.19), channel_id=1, replica_groups=mesh['row'=8,'col'=32] {'row'}, dimensions={0} | all-to-all | bytes 1048576 | tf_op jit(solution)/shard_map/all_to_all | solution.py:65
  176.0 0.7 reduce_sum.9
  176.7 0.0 all-gather.8.cloned.1.call-update
  176.7 0.0 reduce-scatter.2.cloned.1.call-start
  176.8 0.0 slice-done.2
  176.8 6.7 %fusion.11 = f32[2048,704]{0,1:T(8,128)} fusion(f32[2048,256]{1,0:T(8,128)S(1)} %bitcast.54, f32[88,8,2,128]{3,2,1,0:T(2,128)S(1)} %bitcast.58), kind=kOutput, calls=%fused_computation.13 | convolution fusion | flops 4429185024 | bytes 8585216 | tf_op jit(solution)/shard_map/dot_general | solution.py:14
  183.5 0.0 reduce-scatter.2.cloned.1.call-update
  183.5 1.1 slice-done.1
  184.6 1.5 broadcast_in_dim.14
  186.1 97.8 %all_to_all.11 = f32[704,2,8,128]{3,1,0,2:T(2,128)S(1)} all-to-all(f32[704,2,8,128]{3,1,0,2:T(2,128)S(1)} %broadcast_in_dim.14), channel_id=1, replica_groups=mesh['row'=8,'col'=32] {'row'}, dimensions={2} | all-to-all | bytes 11534336 | tf_op jit(solution)/shard_map/all_to_all | solution.py:72
  283.9 5.9 %copy.11 = f32[704,2,8,128]{3,2,1,0:T(8,128)} copy(f32[704,2,8,128]{3,1,0,2:T(2,128)S(1)} %all_to_all.11) | data formatting | bytes 11534336 | tf_op jit(solution)/shard_map/all_to_all | solution.py:72
  289.7 9.2 %fusion.3 = f32[704,256]{1,0:T(8,128)S(1)} fusion(f32[2048,256]{1,0:T(8,128)} %all-gather.8.cloned.1.call-done, f32[88,8,16,128]{3,2,1,0:T(8,128)} %bitcast.55), kind=kOutput, calls=%fused_computation.5 | convolution fusion | flops 4429185024 | bytes 8585216 | tf_op jit(solution)/shard_map/dot_general | solution.py:10
  299.0 0.0 copy-start.2
  299.0 23.7 %reduce-scatter.2.cloned.1.call-done = f32[256,704]{0,1:T(8,128)} async-done(((f32[2048,704]{0,1:T(8,128)}), f32[256,704]{0,1:T(8,128)}) %reduce-scatter.2.cloned.1.call-update) | async-done | bytes 720912 | tf_op jit(solution)/shard_map/reduce_scatter | solution.py:75
  322.7 1.2 bitcast_subtract_fusion
  323.9 0.0 copy-done.2
  323.9 0.1 pad_maximum_fusion
  324.0 1.3 reshape.22
  (3 shorter events, 0.0 us)
Async XLA Ops:
  6.5 62.4 %all-gather.10.cloned.1.call-start = ((), (), s32[]{:S(2)}) async-start(), calls=%async_computation.6 | async-start | bytes 2162688 | tf_op jit(solution)/shard_map/all_gather | solution.py:32
  8.0 147.1 %all-gather.6.cloned.1.call-start = ((), (), s32[]{:S(2)}) async-start(), calls=%async_computation.3 | async-start | bytes 3244032 | tf_op jit(solution)/shard_map/all_gather | solution.py:47
  68.9 48.1 %copy-start.1 = (f32[1,2048,2,128]{3,1,2,0:T(8,128)S(1)}, f32[1,2048,2,128]{3,1,2,0:T(8,128)}, u32[]{:S(2)}) copy-start(f32[1,2048,2,128]{3,1,2,0:T(8,128)} %all-gather.10.cloned.1.call-done) | copy-start | bytes 6291460
  94.7 195.0 %all-gather.8.cloned.1.call-start = ((), (), s32[]{:S(2)}) async-start(), calls=%async_computation.5 | async-start | bytes 2162688 | tf_op jit(solution)/shard_map/all_gather | solution.py:67
  157.6 1.6 slice-start
  157.6 2.5 copy-start
  162.9 13.8 %slice-start.2 = ((f32[12,64,2,128]{3,2,1,0:T(2,128)}), f32[11,64,2,128]{3,2,1,0:T(2,128)S(1)}, s32[]{:S(2)}) async-start(f32[12,64,2,128]{3,2,1,0:T(2,128)} %param.2), calls=%async_computation.9 | async-start | bytes 1441792 | tf_op jit(solution)/shard_map/slice | solution.py:76
  176.7 146.0 %reduce-scatter.2.cloned.1.call-start = ((), (), s32[]{:S(2)}) async-start(), calls=%async_computation.4 | async-start | bytes 6488064 | tf_op jit(solution)/shard_map/reduce_scatter | solution.py:75
  183.5 1.1 slice-start.1
  299.0 25.0 %copy-start.2 = (f32[256,64]{0,1:T(8,128)S(1)}, f32[256,64]{0,1:T(8,128)}, u32[]{:S(2)}) copy-start(f32[256,64]{0,1:T(8,128)} %reduce_sum.9) | copy-start | bytes 196612
Sparse Core Ops, SparseCore 0:
  10.0 58.9 all-gather.9
  94.9 60.2 all-gather.5
  176.8 54.1 all-gather.7
  233.4 89.2 reduce-scatter.1

commit v10 on v9

--- a/solution.py
+++ b/solution.py
@@ -30,6 +30,17 @@
     cols_here = rounds * strip_width
     strip_rows = strip.reshape(cols_here, 2 * row_run)
     gathered = lax.all_gather(lower[0], "col", axis=0, tiled=True)
+
+    trail_count = cols_here - strip_width
+    chunk = trail_count // 4
+    bounds = [0, chunk, 2 * chunk, trail_count]
+    left_chunks = []
+    for lo, hi in zip(bounds[:-1], bounds[1:]):
+        trail_part = lower[1:].reshape(trail_count, 2, 1, row_run)[lo:hi]
+        copies = jnp.broadcast_to(trail_part, (hi - lo, 2, row_count, row_run))
+        moved = lax.all_to_all(copies, "row", split_axis=2, concat_axis=2, tiled=True)
+        left_chunks.append(moved.reshape(hi - lo, 2 * block_size))
+    left_chunks[0], gathered = lax.optimization_barrier((left_chunks[0], gathered))
     first_cols = gathered[:block_size, 0, :]
     cross_cols = gathered[block_size:, 0, :]
     second_cols = gathered[block_size:, 1, :]
@@ -43,6 +54,7 @@
     cross_mix = lax.all_gather(times_rows(own_rows[:, 1, :], cross_cols), "row", axis=1, tiled=True)
     chained_piece = times_rows(cross_mix, first_cols)
     chained = lax.all_gather(chained_piece, "row", axis=1, tiled=True)
+    left_chunks[1], chained = lax.optimization_barrier((left_chunks[1], chained))
     joined = jnp.concatenate([strip[0].reshape(strip_width, 2 * row_run), chained_piece], axis=1)
     joined = lax.all_gather(joined, "col", axis=0, tiled=True)
     strip_lead = joined[:, : 2 * row_run]
@@ -66,11 +78,7 @@
     solved_lead = lead_parts.sum(axis=0).T
     everything = lax.all_gather(solved_lead, "col", axis=0, tiled=True)
 
-    trail_count = cols_here - strip_width
-    trail_part = lower[1:].reshape(trail_count, 2, 1, row_run)
-    copies = jnp.broadcast_to(trail_part, (trail_count, 2, row_count, row_run))
-    full_left = lax.all_to_all(copies, "row", split_axis=2, concat_axis=2, tiled=True)
-    full_left = full_left.reshape(trail_count, 2 * block_size)
+    full_left = jnp.concatenate(left_chunks, axis=0)
     left_update = lax.optimization_barrier(times_rows(full_left, everything))
     summed = lax.psum_scatter(
         times_rows_turned(inverse_cols, strip_rows[strip_width:]),

time: 332 us -> 313 us (0.943)
  blocking collectives: 180 us -> 149 us
  starting transfers between devices: 0.13 us -> 10.3 us
    all_to_all x1, blocking collectives: 97.8 us -> 47.8 us  [local(): lax.all_to_all(copies, 'row', split_axis=2, concat_axis=2, tiled=True)]
    reduce_scatter x1, waiting for transfers between devices: 23.7 us -> 59.2 us  [local(): lax.psum_scatter(times_rows_turned(inverse_cols, strip_rows[strip_width:]...]
    all_gather x1, waiting for transfers between devices: 37.3 us -> 12.3 us  [local(): joined = lax.all_gather(joined, 'col', axis=0, tiled=True)]
    all_gather x1, waiting for transfers between devices: 35 us -> 10.5 us  [local(): gathered = lax.all_gather(lower[0], 'col', axis=0, tiled=True)]
    all_gather x1, blocking collectives: 25 us -> 39.9 us  [local(): own_rows = lax.all_gather(lower[0], 'row', axis=2, tiled=True)]
    all_to_all x0 -> x2, waiting for transfers between devices: none -> 14.1 us  [local(): lax.all_to_all(copies, 'row', split_axis=2, concat_axis=2, tiled=True)]
    all_to_all x0 -> x2, starting transfers between devices: none -> 9.95 us  [local(): lax.all_to_all(copies, 'row', split_axis=2, concat_axis=2, tiled=True)]
    unnamed x8 -> x15, local copies, waits for them, and re-layouts: 0.95 us -> 5.64 us
  transfers between devices with their start and end apart: 4 -> 6, of which waited for: 3 -> 4; matrix products, arithmetic and copies ran while one was open for 8% -> 9% of each run, Pallas kernels for 0% -> 0%
where the time goes in v10:
time: 313 us
  blocking collectives  149 us (48%)
  waiting for transfers between devices  96.1 us (31%)
  matrix products  20.9 us (7%)
  local copies, waits for them, and re-layouts  17.8 us (6%)
  between operations  13.4 us (4%)
  starting transfers between devices  10.3 us (3%)
  other arithmetic  5.1 us (2%)
    reduce_scatter x1, waiting for transfers between devices, local(): lax.psum_scatter(times_rows_turned(inverse_cols, strip_rows[strip_width:]...  59.2 us
    all_to_all x1, blocking collectives, local(): lax.all_to_all(copies, 'row', split_axis=2, concat_axis=2, tiled=True)  47.8 us
    all_gather x1, blocking collectives, local(): own_rows = lax.all_gather(lower[0], 'row', axis=2, tiled=True)  39.9 us
    all_gather x1, blocking collectives, local(): chained = lax.all_gather(chained_piece, 'row', axis=1, tiled=True)  25.8 us
    all_gather x1, blocking collectives, local(): lax.all_gather(times_rows(own_rows[:, 1, :], cross_cols), 'row', axis=1,...  22.1 us
    all_to_all x2, waiting for transfers between devices, local(): lax.all_to_all(copies, 'row', split_axis=2, concat_axis=2, tiled=True)  14.1 us
    all_to_all x1, blocking collectives, local(): lax.all_to_all(lead_parts, 'row', split_axis=0, concat_axis=0, tiled=True)  13.4 us
    all_gather x1, waiting for transfers between devices, local(): joined = lax.all_gather(joined, 'col', axis=0, tiled=True)  12.3 us
  transfers between devices with their start and end apart: 6, of which 4 were waited for; matrix products, arithmetic and copies ran while one was open for 9% of the time, Pallas kernels for 0%

profile of v10, /device:TPU:1, one launch (start us, length us, event | category | flops | bytes accessed | tf_op | source)
XLA Modules:
  0.0 312.5 jit_solution(3063881411641325493)
XLA Ops:
  6.5 0.8 slice.51
  7.4 0.6 copy.14
  8.0 0.0 all-gather.10.cloned.1.call-update
  8.0 1.2 slice.49
  9.3 1.5 broadcast_in_dim.27
  10.8 6.4 %all-to-all-start = ((f32[176,2,8,128]{3,1,0,2:T(2,128)}), f32[176,2,8,128]{3,1,0,2:T(2,128)S(1)}, u32[]{:S(2)}, u32[]{:S(2)}) async-start(f32[176,2,8,128]{3,1,0,2:T(2,128)} %broadcast_in_dim.27), calls=%async_computation | async-start | bytes 2883584 | tf_op jit(solution)/shard_map/all_to_all | solution.py:41
  17.1 0.0 all-gather.6.cloned.1.call-start
  17.2 39.9 %all-gather.1 = f32[1,64,2,1024]{3,1,2,0:T(8,128)S(1)} all-gather(f32[1,64,2,128]{3,1,2,0:T(8,128)S(1)} %copy-done.3), channel_id=3, replica_groups=mesh['row'=8,'col'=32] {'row'}, dimensions={3}, use_global_device_ids=true | all-gather | bytes 589824 | tf_op jit(solution)/shard_map/all_gather | solution.py:50
  57.1 0.8 copy.9
  58.0 1.7 copy.30
  59.7 10.5 %all-gather.10.cloned.1.call-done = f32[1,2048,2,128]{3,1,2,0:T(8,128)} async-done(((f32[1,64,2,128]{3,1,2,0:T(8,128)}), f32[1,2048,2,128]{3,1,2,0:T(8,128)}) %all-gather.10.cloned.1.call-update) | async-done | bytes 2097168 | tf_op jit(solution)/shard_map/all_gather | solution.py:32
  70.2 1.5 convolution_bitcast_fusion
  71.7 22.1 %all_gather.20 = f32[64,1024]{1,0:T(8,128)S(1)} all-gather(f32[64,128]{1,0:T(8,128)S(1)} %convolution_bitcast_fusion), channel_id=1, replica_groups=mesh['row'=8,'col'=32] {'row'}, dimensions={1}, use_global_device_ids=true | all-gather | bytes 294912 | tf_op jit(solution)/shard_map/all_gather | solution.py:54
  93.8 1.5 fusion.20
  95.2 0.6 pad_maximum_fusion.1
  95.9 0.0 all-gather.6.cloned.1.call-update
  95.9 1.5 broadcast_in_dim.29
  97.4 3.6 %all-to-all-start.1 = ((f32[176,2,8,128]{3,1,0,2:T(2,128)}), f32[176,2,8,128]{3,1,0,2:T(2,128)S(1)}, u32[]{:S(2)}, u32[]{:S(2)}) async-start(f32[176,2,8,128]{3,1,0,2:T(2,128)} %broadcast_in_dim.29), calls=%async_computation.1 | async-start | bytes 2883584 | tf_op jit(solution)/shard_map/all_to_all | solution.py:41
  101.0 0.0 all-gather.8.cloned.1.call-start
  101.1 14.1 %all-to-all-done.1 = f32[176,2,8,128]{3,1,0,2:T(2,128)S(1)} async-done(((f32[176,2,8,128]{3,1,0,2:T(2,128)}), f32[176,2,8,128]{3,1,0,2:T(2,128)S(1)}, u32[]{:S(2)}, u32[]{:S(2)}) %all-to-all-start.1) | async-done | bytes 1441824 | tf_op jit(solution)/shard_map/all_to_all | solution.py:41
  115.1 0.8 copy.12
  116.0 1.7 copy.29
  117.7 25.8 %all_gather.22 = f32[64,1024]{1,0:T(8,128)} all-gather(f32[64,128]{1,0:T(8,128)S(1)} %fusion.20), channel_id=1, replica_groups=mesh['row'=8,'col'=32] {'row'}, dimensions={1}, use_global_device_ids=true | all-gather | bytes 294912 | tf_op jit(solution)/shard_map/all_gather | solution.py:56
  143.5 0.1 slice_bitcast_fusion
  143.5 12.3 %all-gather.6.cloned.1.call-done = f32[2048,384]{1,0:T(8,128)} async-done(((f32[64,384]{1,0:T(8,128)}), f32[2048,384]{1,0:T(8,128)}) %all-gather.6.cloned.1.call-update) | async-done | bytes 3145744 | tf_op jit(solution)/shard_map/all_gather | solution.py:59
  155.8 1.1 slice_negate_fusion
  156.9 0.2 select_maximum_fusion
  157.1 0.1 copy.11
  157.2 1.6 slice-done
  158.8 0.6 fusion.9
  159.4 0.3 copy-done
  159.7 0.6 fusion.7
  160.4 2.2 fusion.21
  162.6 13.4 %all_to_all.20 = f32[8,256,64]{1,2,0:T(8,128)} all-to-all(f32[8,256,64]{1,2,0:T(8,128)S(1)} %fusion.21), channel_id=1, replica_groups=mesh['row'=8,'col'=32] {'row'}, dimensions={0} | all-to-all | bytes 1048576 | tf_op jit(solution)/shard_map/all_to_all | solution.py:77
  176.0 1.7 reduce_sum.9
  177.7 0.0 all-gather.8.cloned.1.call-update
  177.7 0.2 reduce-scatter.2.cloned.1.call-start
  177.9 6.6 %fusion.11 = f32[2048,704]{0,1:T(8,128)} fusion(f32[2048,256]{1,0:T(8,128)S(1)} %bitcast.68, f32[88,8,2,128]{3,2,1,0:T(2,128)S(1)} %bitcast.77), kind=kOutput, calls=%fused_computation.19 | convolution fusion | flops 4429185024 | bytes 8585216 | tf_op jit(solution)/shard_map/dot_general | solution.py:14
  184.6 0.7 broadcast_in_dim.32
  185.3 47.8 %all_to_all.21 = f32[352,2,8,128]{3,1,0,2:T(2,128)S(1)} all-to-all(f32[352,2,8,128]{3,1,0,2:T(2,128)S(1)} %broadcast_in_dim.32), channel_id=1, replica_groups=mesh['row'=8,'col'=32] {'row'}, dimensions={2} | all-to-all | bytes 5767168 | tf_op jit(solution)/shard_map/all_to_all | solution.py:41
  233.1 1.7 copy.13
  234.8 1.3 copy.28
  236.0 0.0 all-gather.8.cloned.1.call-done
  236.1 8.0 %fusion = f32[704,256]{1,0:T(8,128)} fusion(f32[2048,256]{1,0:T(8,128)} %all-gather.8.cloned.1.call-done, f32[352,2048]{1,0:T(8,128)S(1)} %bitcast.73, f32[176,2048]{1,0:T(8,128)} %bitcast.83, f32[176,2048]{1,0:T(8,128)} %bitcast.82), kind=kOutput, calls=%fused_computation | convolution fusion | flops 4432068608 | bytes 8585216 | tf_op jit(solution)/shard_map/dot_general | solution.py:10
  244.0 59.2 %reduce-scatter.2.cloned.1.call-done = f32[256,704]{0,1:T(8,128)} async-done(((f32[2048,704]{0,1:T(8,128)}), f32[256,704]{0,1:T(8,128)}) %reduce-scatter.2.cloned.1.call-update) | async-done | bytes 720912 | tf_op jit(solution)/shard_map/reduce_scatter | solution.py:83
  303.2 1.4 bitcast_subtract_fusion
  304.7 0.1 pad_maximum_fusion
  304.7 1.3 reshape.34
  (20 shorter events, 0.1 us)
Async XLA Ops:
  6.5 63.7 %all-gather.10.cloned.1.call-start = ((), (), s32[]{:S(2)}) async-start(), calls=%async_computation.8 | async-start | bytes 2162688 | tf_op jit(solution)/shard_map/all_gather | solution.py:32
  9.2 7.9 %slice-start.1 = ((f32[12,64,2,128]{3,2,1,0:T(2,128)}), f32[1,64,2,128]{3,2,1,0:T(2,128)S(1)}, s32[]{:S(2)}) async-start(f32[12,64,2,128]{3,2,1,0:T(2,128)} %param.2), calls=%async_computation.10 | async-start | bytes 131072 | tf_op jit(solution)/shard_map/slice | solution.py:58
  9.3 8.0 %copy-start.3 = (f32[1,64,2,128]{3,1,2,0:T(8,128)S(1)}, f32[1,64,2,128]{3,1,2,0:T(8,128)}, u32[]{:S(2)}) copy-start(f32[1,64,2,128]{3,1,2,0:T(8,128)} %copy.14) | copy-start | bytes 196612
  10.8 46.4 %all-to-all-start = ((f32[176,2,8,128]{3,1,0,2:T(2,128)}), f32[176,2,8,128]{3,1,0,2:T(2,128)S(1)}, u32[]{:S(2)}, u32[]{:S(2)}) async-start(f32[176,2,8,128]{3,1,0,2:T(2,128)} %broadcast_in_dim.27), calls=%async_computation | async-start | bytes 2883584 | tf_op jit(solution)/shard_map/all_to_all | solution.py:41
  17.1 138.6 %all-gather.6.cloned.1.call-start = ((), (), s32[]{:S(2)}) async-start(), calls=%async_computation.5 | async-start | bytes 3244032 | tf_op jit(solution)/shard_map/all_gather | solution.py:59
  97.4 17.7 %all-to-all-start.1 = ((f32[176,2,8,128]{3,1,0,2:T(2,128)}), f32[176,2,8,128]{3,1,0,2:T(2,128)S(1)}, u32[]{:S(2)}, u32[]{:S(2)}) async-start(f32[176,2,8,128]{3,1,0,2:T(2,128)} %broadcast_in_dim.29), calls=%async_computation.1 | async-start | bytes 2883584 | tf_op jit(solution)/shard_map/all_to_all | solution.py:41
  101.0 135.1 %all-gather.8.cloned.1.call-start = ((), (), s32[]{:S(2)}) async-start(), calls=%async_computation.7 | async-start | bytes 2162688 | tf_op jit(solution)/shard_map/all_gather | solution.py:79
  116.0 27.5 %copy-start.1 = (f32[1,2048,2,128]{3,1,2,0:T(8,128)S(1)}, f32[1,2048,2,128]{3,1,2,0:T(8,128)}, u32[]{:S(2)}) copy-start(f32[1,2048,2,128]{3,1,2,0:T(8,128)} %all-gather.10.cloned.1.call-done) | copy-start | bytes 6291460
  157.2 1.6 slice-start
  157.2 2.5 copy-start
  157.2 2.5 copy-start.2
  162.5 15.4 %slice-start.2 = ((f32[12,64,2,128]{3,2,1,0:T(2,128)}), f32[11,64,2,128]{3,2,1,0:T(2,128)S(1)}, s32[]{:S(2)}) async-start(f32[12,64,2,128]{3,2,1,0:T(2,128)} %param.2), calls=%async_computation.11 | async-start | bytes 1441792 | tf_op jit(solution)/shard_map/slice | solution.py:84
  177.7 125.5 %reduce-scatter.2.cloned.1.call-start = ((), (), s32[]{:S(2)}) async-start(), calls=%async_computation.6 | async-start | bytes 6488064 | tf_op jit(solution)/shard_map/reduce_scatter | solution.py:83
  244.0 60.6 %copy-start.4 = (f32[256,64]{0,1:T(8,128)S(1)}, f32[256,64]{0,1:T(8,128)}, u32[]{:S(2)}) copy-start(f32[256,64]{0,1:T(8,128)} %reduce_sum.9) | copy-start | bytes 196612
Sparse Core Ops, SparseCore 0:
  10.0 60.2 all-gather.9
  96.0 59.6 all-gather.5
  177.8 54.4 all-gather.7
  234.7 68.4 reduce-scatter.1

commit v11 on v10

--- a/solution.py
+++ b/solution.py
@@ -51,7 +51,10 @@
     diag_rows = lax.dynamic_index_in_dim(own_rows, lower_half, 1, keepdims=False)
     below = lower_half == 1
 
-    cross_mix = lax.all_gather(times_rows(own_rows[:, 1, :], cross_cols), "row", axis=1, tiled=True)
+    cross_piece = times_rows(own_rows[:, 1, :], cross_cols)[:, None, :]
+    cross_copies = jnp.broadcast_to(cross_piece, (strip_width, row_count, row_run))
+    cross_mix = lax.all_to_all(cross_copies, "row", split_axis=1, concat_axis=1, tiled=True)
+    cross_mix = cross_mix.reshape(strip_width, block_size)
     chained_piece = times_rows(cross_mix, first_cols)
     chained = lax.all_gather(chained_piece, "row", axis=1, tiled=True)
     left_chunks[1], chained = lax.optimization_barrier((left_chunks[1], chained))

time: 313 us -> 298 us (0.952)
  blocking collectives: 149 us -> 112 us
  waiting for transfers between devices: 96.1 us -> 113 us
  starting transfers between devices: 10.3 us -> 14.1 us
    all_gather x1 -> x0, blocking collectives: 22.1 us -> none  [local(): lax.all_gather(times_rows(own_rows[:, 1, :], cross_cols), 'row', axis=1,...]
    all_to_all x1, blocking collectives: 47.8 us -> 34.3 us  [local(): lax.all_to_all(copies, 'row', split_axis=2, concat_axis=2, tiled=True)]
    all_gather x1, waiting for transfers between devices: 0.02 us -> 12.7 us  [local(): everything = lax.all_gather(solved_lead, 'col', axis=0, tiled=True)]
    all_gather x1, waiting for transfers between devices: 12.3 us -> 2.54 us  [local(): joined = lax.all_gather(joined, 'col', axis=0, tiled=True)]
    all_to_all x0 -> x1, waiting for transfers between devices: none -> 6.03 us  [local(): lax.all_to_all(cross_copies, 'row', split_axis=1, concat_axis=1, tiled=True)]
    all_to_all x2, waiting for transfers between devices: 14.1 us -> 19.6 us  [local(): lax.all_to_all(copies, 'row', split_axis=2, concat_axis=2, tiled=True)]
    all_to_all x0 -> x1, starting transfers between devices: none -> 3.41 us  [local(): lax.all_to_all(cross_copies, 'row', split_axis=1, concat_axis=1, tiled=True)]
  transfers between devices with their start and end apart: 6 -> 7, of which waited for: 4 -> 6; matrix products, arithmetic and copies ran while one was open for 9% -> 9% of each run, Pallas kernels for 0% -> 0%
where the time goes in v11:
time: 298 us
  waiting for transfers between devices  113 us (38%)
  blocking collectives  112 us (38%)
  matrix products  20.9 us (7%)
  local copies, waits for them, and re-layouts  18.6 us (6%)
  starting transfers between devices  14.1 us (5%)
  between operations  13.3 us (4%)
  other arithmetic  5.1 us (2%)
    reduce_scatter x1, waiting for transfers between devices, local(): lax.psum_scatter(times_rows_turned(inverse_cols, strip_rows[strip_width:]...  61.8 us
    all_gather x1, blocking collectives, local(): own_rows = lax.all_gather(lower[0], 'row', axis=2, tiled=True)  40 us
    all_to_all x1, blocking collectives, local(): lax.all_to_all(copies, 'row', split_axis=2, concat_axis=2, tiled=True)  34.3 us
    all_gather x1, blocking collectives, local(): chained = lax.all_gather(chained_piece, 'row', axis=1, tiled=True)  25.5 us
    all_to_all x2, waiting for transfers between devices, local(): lax.all_to_all(copies, 'row', split_axis=2, concat_axis=2, tiled=True)  19.6 us
    all_gather x1, waiting for transfers between devices, local(): everything = lax.all_gather(solved_lead, 'col', axis=0, tiled=True)  12.7 us
    all_to_all x1, blocking collectives, local(): lax.all_to_all(lead_parts, 'row', split_axis=0, concat_axis=0, tiled=True)  12.5 us
    dot_general x5, matrix products, times_rows(): jnp.dot(coeff, right_side, precision=highest, preferred_element_type=jnp....  12.2 us
  transfers between devices with their start and end apart: 7, of which 6 were waited for; matrix products, arithmetic and copies ran while one was open for 9% of the time, Pallas kernels for 0%

profile of v11, /device:TPU:1, one launch (start us, length us, event | category | flops | bytes accessed | tf_op | source)
XLA Modules:
  0.0 297.7 jit_solution(10487278771492480469)
XLA Ops:
  6.5 0.8 slice.51
  7.4 0.6 copy.15
  8.0 1.2 slice.49
  9.3 1.5 broadcast_in_dim.33
  10.8 6.4 %all-to-all-start = ((f32[176,2,8,128]{3,1,0,2:T(2,128)}), f32[176,2,8,128]{3,1,0,2:T(2,128)S(1)}, u32[]{:S(2)}, u32[]{:S(2)}) async-start(f32[176,2,8,128]{3,1,0,2:T(2,128)} %broadcast_in_dim.33), calls=%async_computation | async-start | bytes 2883584 | tf_op jit(solution)/shard_map/all_to_all | solution.py:41
  17.1 40.0 %all-gather.1 = f32[1,64,2,1024]{3,1,2,0:T(8,128)S(1)} all-gather(f32[1,64,2,128]{3,1,2,0:T(8,128)S(1)} %copy-done.3), channel_id=3, replica_groups=mesh['row'=8,'col'=32] {'row'}, dimensions={3}, use_global_device_ids=true | all-gather | bytes 589824 | tf_op jit(solution)/shard_map/all_gather | solution.py:50
  57.1 0.8 copy.9
  58.0 1.7 copy.36
  59.7 10.5 %all-gather.10.cloned.1.call-done = f32[1,2048,2,128]{3,1,2,0:T(8,128)} async-done(((f32[1,64,2,128]{3,1,2,0:T(8,128)}), f32[1,2048,2,128]{3,1,2,0:T(8,128)}) %all-gather.10.cloned.1.call-update) | async-done | bytes 2097168 | tf_op jit(solution)/shard_map/all_gather | solution.py:32
  70.2 1.5 convolution_bitcast_fusion
  71.7 0.7 broadcast_in_dim.34
  72.4 3.4 %all-to-all-start.1 = ((f32[64,8,128]{2,0,1:T(8,128)}), f32[64,8,128]{2,0,1:T(8,128)S(1)}, u32[]{:S(2)}, u32[]{:S(2)}) async-start(f32[64,8,128]{2,0,1:T(8,128)} %broadcast_in_dim.34), calls=%async_computation.1 | async-start | bytes 524288 | tf_op jit(solution)/shard_map/all_to_all | solution.py:56
  75.9 0.0 all-gather.6.cloned.1.call-start
  75.9 6.0 %all-to-all-done.1 = f32[64,8,128]{2,0,1:T(8,128)S(1)} async-done(((f32[64,8,128]{2,0,1:T(8,128)}), f32[64,8,128]{2,0,1:T(8,128)S(1)}, u32[]{:S(2)}, u32[]{:S(2)}) %all-to-all-start.1) | async-done | bytes 262176 | tf_op jit(solution)/shard_map/all_to_all | solution.py:56
  82.0 1.5 fusion.16
  83.4 0.6 pad_maximum_fusion.1
  84.1 1.5 broadcast_in_dim.36
  85.6 4.0 %all-to-all-start.2 = ((f32[176,2,8,128]{3,1,0,2:T(2,128)}), f32[176,2,8,128]{3,1,0,2:T(2,128)S(1)}, u32[]{:S(2)}, u32[]{:S(2)}) async-start(f32[176,2,8,128]{3,1,0,2:T(2,128)} %broadcast_in_dim.36), calls=%async_computation.2 | async-start | bytes 2883584 | tf_op jit(solution)/shard_map/all_to_all | solution.py:41
  89.6 0.0 all-gather.8.cloned.1.call-start
  89.7 19.6 %all-to-all-done.2 = f32[176,2,8,128]{3,1,0,2:T(2,128)S(1)} async-done(((f32[176,2,8,128]{3,1,0,2:T(2,128)}), f32[176,2,8,128]{3,1,0,2:T(2,128)S(1)}, u32[]{:S(2)}, u32[]{:S(2)}) %all-to-all-start.2) | async-done | bytes 1441824 | tf_op jit(solution)/shard_map/all_to_all | solution.py:41
  109.3 0.8 copy.13
  110.1 1.7 copy.35
  111.8 0.1 copy-done.1
  111.9 0.1 slice_bitcast_fusion
  111.9 25.5 %all_gather.18 = f32[64,1024]{1,0:T(8,128)} all-gather(f32[64,128]{1,0:T(8,128)S(1)} %fusion.16), channel_id=1, replica_groups=mesh['row'=8,'col'=32] {'row'}, dimensions={1}, use_global_device_ids=true | all-gather | bytes 294912 | tf_op jit(solution)/shard_map/all_gather | solution.py:59
  137.5 2.5 all-gather.6.cloned.1.call-done
  140.0 1.1 slice_negate_fusion
  141.1 0.2 select_maximum_fusion
  141.3 0.1 copy.12
  141.5 1.6 slice-done
  143.0 0.6 fusion.9
  143.7 0.3 copy-done
  144.0 0.6 fusion.7
  144.6 2.2 fusion.23
  146.8 12.5 %all_to_all.25 = f32[8,256,64]{1,2,0:T(8,128)} all-to-all(f32[8,256,64]{1,2,0:T(8,128)S(1)} %fusion.23), channel_id=1, replica_groups=mesh['row'=8,'col'=32] {'row'}, dimensions={0} | all-to-all | bytes 1048576 | tf_op jit(solution)/shard_map/all_to_all | solution.py:80
  159.3 1.7 reduce_sum.9
  161.0 0.2 reduce-scatter.2.cloned.1.call-start
  161.3 6.6 %fusion.11 = f32[2048,704]{0,1:T(8,128)} fusion(f32[2048,256]{1,0:T(8,128)S(1)} %bitcast.74, f32[88,8,2,128]{3,2,1,0:T(2,128)S(1)} %bitcast.83), kind=kOutput, calls=%fused_computation.19 | convolution fusion | flops 4429185024 | bytes 8585216 | tf_op jit(solution)/shard_map/dot_general | solution.py:14
  167.9 0.7 broadcast_in_dim.39
  168.6 34.3 %all_to_all.26 = f32[352,2,8,128]{3,1,0,2:T(2,128)S(1)} all-to-all(f32[352,2,8,128]{3,1,0,2:T(2,128)S(1)} %broadcast_in_dim.39), channel_id=1, replica_groups=mesh['row'=8,'col'=32] {'row'}, dimensions={2} | all-to-all | bytes 5767168 | tf_op jit(solution)/shard_map/all_to_all | solution.py:41
  202.9 1.7 copy.14
  204.6 1.3 copy.34
  205.9 12.7 %all-gather.8.cloned.1.call-done = f32[2048,256]{1,0:T(8,128)} async-done(((f32[64,256]{1,0:T(8,128)}), f32[2048,256]{1,0:T(8,128)}) %all-gather.8.cloned.1.call-update) | async-done | bytes 2097168 | tf_op jit(solution)/shard_map/all_gather | solution.py:82
  218.6 8.0 %fusion = f32[704,256]{1,0:T(8,128)} fusion(f32[2048,256]{1,0:T(8,128)} %all-gather.8.cloned.1.call-done, f32[352,2048]{1,0:T(8,128)S(1)} %bitcast.79, f32[176,2048]{1,0:T(8,128)} %bitcast.89, f32[176,2048]{1,0:T(8,128)} %bitcast.88), kind=kOutput, calls=%fused_computation | convolution fusion | flops 4432068608 | bytes 8585216 | tf_op jit(solution)/shard_map/dot_general | solution.py:10
  226.6 61.8 %reduce-scatter.2.cloned.1.call-done = f32[256,704]{0,1:T(8,128)} async-done(((f32[2048,704]{0,1:T(8,128)}), f32[256,704]{0,1:T(8,128)}) %reduce-scatter.2.cloned.1.call-update) | async-done | bytes 720912 | tf_op jit(solution)/shard_map/reduce_scatter | solution.py:86
  288.4 1.4 bitcast_subtract_fusion
  289.8 0.1 pad_maximum_fusion
  289.9 1.3 reshape.39
  (22 shorter events, 0.2 us)
Async XLA Ops:
  6.5 63.7 %all-gather.10.cloned.1.call-start = ((), (), s32[]{:S(2)}) async-start(), calls=%async_computation.9 | async-start | bytes 2162688 | tf_op jit(solution)/shard_map/all_gather | solution.py:32
  9.2 7.9 %copy-start.3 = (f32[1,64,2,128]{3,1,2,0:T(8,128)S(1)}, f32[1,64,2,128]{3,1,2,0:T(8,128)}, u32[]{:S(2)}) copy-start(f32[1,64,2,128]{3,1,2,0:T(8,128)} %copy.15) | copy-start | bytes 196612
  10.8 46.4 %all-to-all-start = ((f32[176,2,8,128]{3,1,0,2:T(2,128)}), f32[176,2,8,128]{3,1,0,2:T(2,128)S(1)}, u32[]{:S(2)}, u32[]{:S(2)}) async-start(f32[176,2,8,128]{3,1,0,2:T(2,128)} %broadcast_in_dim.33), calls=%async_computation | async-start | bytes 2883584 | tf_op jit(solution)/shard_map/all_to_all | solution.py:41
  58.0 17.9 %slice-start.1 = ((f32[12,64,2,128]{3,2,1,0:T(2,128)}), f32[1,64,2,128]{3,2,1,0:T(2,128)S(1)}, s32[]{:S(2)}) async-start(f32[12,64,2,128]{3,2,1,0:T(2,128)} %param.2), calls=%async_computation.11 | async-start | bytes 131072 | tf_op jit(solution)/shard_map/slice | solution.py:61
  72.4 9.5 %all-to-all-start.1 = ((f32[64,8,128]{2,0,1:T(8,128)}), f32[64,8,128]{2,0,1:T(8,128)S(1)}, u32[]{:S(2)}, u32[]{:S(2)}) async-start(f32[64,8,128]{2,0,1:T(8,128)} %broadcast_in_dim.34), calls=%async_computation.1 | async-start | bytes 524288 | tf_op jit(solution)/shard_map/all_to_all | solution.py:56
  75.9 64.1 %all-gather.6.cloned.1.call-start = ((), (), s32[]{:S(2)}) async-start(), calls=%async_computation.6 | async-start | bytes 3244032 | tf_op jit(solution)/shard_map/all_gather | solution.py:62
  85.6 23.7 %all-to-all-start.2 = ((f32[176,2,8,128]{3,1,0,2:T(2,128)}), f32[176,2,8,128]{3,1,0,2:T(2,128)S(1)}, u32[]{:S(2)}, u32[]{:S(2)}) async-start(f32[176,2,8,128]{3,1,0,2:T(2,128)} %broadcast_in_dim.36), calls=%async_computation.2 | async-start | bytes 2883584 | tf_op jit(solution)/shard_map/all_to_all | solution.py:41
  89.6 129.0 %all-gather.8.cloned.1.call-start = ((), (), s32[]{:S(2)}) async-start(), calls=%async_computation.8 | async-start | bytes 2162688 | tf_op jit(solution)/shard_map/all_gather | solution.py:82
  110.1 1.8 copy-start.1
  141.4 1.6 slice-start
  141.4 2.5 copy-start
  141.4 2.5 copy-start.2
  146.8 14.5 %slice-start.2 = ((f32[12,64,2,128]{3,2,1,0:T(2,128)}), f32[11,64,2,128]{3,2,1,0:T(2,128)S(1)}, s32[]{:S(2)}) async-start(f32[12,64,2,128]{3,2,1,0:T(2,128)} %param.2), calls=%async_computation.12 | async-start | bytes 1441792 | tf_op jit(solution)/shard_map/slice | solution.py:87
  161.0 127.4 %reduce-scatter.2.cloned.1.call-start = ((), (), s32[]{:S(2)}) async-start(), calls=%async_computation.7 | async-start | bytes 6488064 | tf_op jit(solution)/shard_map/reduce_scatter | solution.py:86
  226.6 63.3 %copy-start.4 = (f32[256,64]{0,1:T(8,128)S(1)}, f32[256,64]{0,1:T(8,128)}, u32[]{:S(2)}) copy-start(f32[256,64]{0,1:T(8,128)} %reduce_sum.9) | copy-start | bytes 196612
Sparse Core Ops, SparseCore 0:
  10.0 60.2 all-gather.9
  84.2 55.7 all-gather.5
  161.1 57.4 all-gather.7
  221.0 67.3 reduce-scatter.1

commit v12 on v11

--- a/solution.py
+++ b/solution.py
@@ -56,7 +56,9 @@
     cross_mix = lax.all_to_all(cross_copies, "row", split_axis=1, concat_axis=1, tiled=True)
     cross_mix = cross_mix.reshape(strip_width, block_size)
     chained_piece = times_rows(cross_mix, first_cols)
-    chained = lax.all_gather(chained_piece, "row", axis=1, tiled=True)
+    chained_copies = jnp.broadcast_to(chained_piece[:, None, :], (strip_width, row_count, row_run))
+    chained = lax.all_to_all(chained_copies, "row", split_axis=1, concat_axis=1, tiled=True)
+    chained = chained.reshape(strip_width, block_size)
     left_chunks[1], chained = lax.optimization_barrier((left_chunks[1], chained))
     joined = jnp.concatenate([strip[0].reshape(strip_width, 2 * row_run), chained_piece], axis=1)
     joined = lax.all_gather(joined, "col", axis=0, tiled=True)

time: 298 us -> 296 us (level)
  waiting for transfers between devices: 113 us -> 97.5 us
  blocking collectives: 112 us -> 126 us
    all_to_all x1 -> x2, blocking collectives: 34.3 us -> 73.1 us  [local(): lax.all_to_all(copies, 'row', split_axis=2, concat_axis=2, tiled=True)]
    all_gather x1 -> x0, blocking collectives: 25.5 us -> none  [local(): chained = lax.all_gather(chained_piece, 'row', axis=1, tiled=True)]
    all_to_all x2 -> x1, waiting for transfers between devices: 19.6 us -> 0.01 us  [local(): lax.all_to_all(copies, 'row', split_axis=2, concat_axis=2, tiled=True)]
    all_gather x1, waiting for transfers between devices: 2.54 us -> 18.9 us  [local(): joined = lax.all_gather(joined, 'col', axis=0, tiled=True)]
    all_gather x1, waiting for transfers between devices: 12.7 us -> 0.02 us  [local(): everything = lax.all_gather(solved_lead, 'col', axis=0, tiled=True)]
    all_to_all x2 -> x1, starting transfers between devices: 10.4 us -> 6.37 us  [local(): lax.all_to_all(copies, 'row', split_axis=2, concat_axis=2, tiled=True)]
    all_to_all x0 -> x1, starting transfers between devices: none -> 3.41 us  [local(): lax.all_to_all(chained_copies, 'row', split_axis=1, concat_axis=1, tiled=...]
    all_to_all x0 -> x1, waiting for transfers between devices: none -> 3.25 us  [local(): lax.all_to_all(chained_copies, 'row', split_axis=1, concat_axis=1, tiled=...]
  transfers between devices with their start and end apart: 7 -> 7, of which waited for: 6 -> 5; matrix products, arithmetic and copies ran while one was open for 9% -> 9% of each run, Pallas kernels for 0% -> 0%
where the time goes in v12:
time: 296 us; the launch traced here: 295 us
  blocking collectives  126 us (43%)
  waiting for transfers between devices  97.5 us (33%)
  matrix products  20.9 us (7%)
  local copies, waits for them, and re-layouts  18.9 us (6%)
  starting transfers between devices  13.5 us (5%)
  between operations  13.4 us (5%)
  other arithmetic  5.1 us (2%)
    all_to_all x2, blocking collectives, local(): lax.all_to_all(copies, 'row', split_axis=2, concat_axis=2, tiled=True)  73.1 us
    reduce_scatter x1, waiting for transfers between devices, local(): lax.psum_scatter(times_rows_turned(inverse_cols, strip_rows[strip_width:]...  58.8 us
    all_gather x1, blocking collectives, local(): own_rows = lax.all_gather(lower[0], 'row', axis=2, tiled=True)  40 us
    all_gather x1, waiting for transfers between devices, local(): joined = lax.all_gather(joined, 'col', axis=0, tiled=True)  18.9 us
    all_to_all x1, blocking collectives, local(): lax.all_to_all(lead_parts, 'row', split_axis=0, concat_axis=0, tiled=True)  12.9 us
    dot_general x5, matrix products, times_rows(): jnp.dot(coeff, right_side, precision=highest, preferred_element_type=jnp....  12.2 us
    all_gather x1, waiting for transfers between devices, local(): gathered = lax.all_gather(lower[0], 'col', axis=0, tiled=True)  10.5 us
    dot_general x2, matrix products, times_rows_turned(): lax.dot_general(coeff, right_turned, (((1,), (1,)), ((), ())), precision=...  8.73 us
  transfers between devices with their start and end apart: 7, of which 5 were waited for; matrix products, arithmetic and copies ran while one was open for 9% of the time, Pallas kernels for 0%

profile of v12, /device:TPU:1, one launch (start us, length us, event | category | flops | bytes accessed | tf_op | source)
XLA Modules:
  0.0 295.4 jit_solution(12178064369159470238)
XLA Ops:
  6.5 0.8 slice.51
  7.4 0.6 copy.16
  8.0 1.2 slice.49
  9.3 1.5 broadcast_in_dim.39
  10.8 6.4 %all-to-all-start = ((f32[176,2,8,128]{3,1,0,2:T(2,128)}), f32[176,2,8,128]{3,1,0,2:T(2,128)S(1)}, u32[]{:S(2)}, u32[]{:S(2)}) async-start(f32[176,2,8,128]{3,1,0,2:T(2,128)} %broadcast_in_dim.39), calls=%async_computation | async-start | bytes 2883584 | tf_op jit(solution)/shard_map/all_to_all | solution.py:41
  17.1 40.0 %all-gather.1 = f32[1,64,2,1024]{3,1,2,0:T(8,128)S(1)} all-gather(f32[1,64,2,128]{3,1,2,0:T(8,128)S(1)} %copy-done.3), channel_id=3, replica_groups=mesh['row'=8,'col'=32] {'row'}, dimensions={3}, use_global_device_ids=true | all-gather | bytes 589824 | tf_op jit(solution)/shard_map/all_gather | solution.py:50
  57.1 0.8 copy.9
  58.0 1.7 copy.39
  59.7 10.5 %all-gather.10.cloned.1.call-done = f32[1,2048,2,128]{3,1,2,0:T(8,128)} async-done(((f32[1,64,2,128]{3,1,2,0:T(8,128)}), f32[1,2048,2,128]{3,1,2,0:T(8,128)}) %all-gather.10.cloned.1.call-update) | async-done | bytes 2097168 | tf_op jit(solution)/shard_map/all_gather | solution.py:32
  70.2 1.5 convolution_bitcast_fusion
  71.7 0.7 broadcast_in_dim.40
  72.4 3.4 %all-to-all-start.1 = ((f32[64,8,128]{2,0,1:T(8,128)}), f32[64,8,128]{2,0,1:T(8,128)S(1)}, u32[]{:S(2)}, u32[]{:S(2)}) async-start(f32[64,8,128]{2,0,1:T(8,128)} %broadcast_in_dim.40), calls=%async_computation.1 | async-start | bytes 524288 | tf_op jit(solution)/shard_map/all_to_all | solution.py:56
  75.9 6.0 %all-to-all-done.1 = f32[64,8,128]{2,0,1:T(8,128)S(1)} async-done(((f32[64,8,128]{2,0,1:T(8,128)}), f32[64,8,128]{2,0,1:T(8,128)S(1)}, u32[]{:S(2)}, u32[]{:S(2)}) %all-to-all-start.1) | async-done | bytes 262176 | tf_op jit(solution)/shard_map/all_to_all | solution.py:56
  82.0 1.5 fusion.16
  83.4 0.6 pad_maximum_fusion.1
  84.1 0.4 broadcast_in_dim.42
  84.5 25.3 %all_to_all.30 = f32[176,2,8,128]{3,1,0,2:T(2,128)S(1)} all-to-all(f32[176,2,8,128]{3,1,0,2:T(2,128)S(1)} %broadcast_in_dim.42), channel_id=1, replica_groups=mesh['row'=8,'col'=32] {'row'}, dimensions={2} | all-to-all | bytes 2883584 | tf_op jit(solution)/shard_map/all_to_all | solution.py:41
  109.7 0.7 broadcast_in_dim.43
  110.5 3.4 %all-to-all-start.3 = ((f32[64,8,128]{2,0,1:T(8,128)}), f32[64,8,128]{2,0,1:T(8,128)S(1)}, u32[]{:S(2)}, u32[]{:S(2)}) async-start(f32[64,8,128]{2,0,1:T(8,128)} %broadcast_in_dim.43), calls=%async_computation.3 | async-start | bytes 524288 | tf_op jit(solution)/shard_map/all_to_all | solution.py:60
  113.9 0.0 all-gather.8.cloned.1.call-start
  114.0 0.8 copy.13
  114.8 1.7 copy.38
  116.5 0.1 copy-done.1
  116.6 0.1 slice_bitcast_fusion
  116.6 3.3 %all-to-all-done.3 = f32[64,8,128]{2,0,1:T(8,128)S(1)} async-done(((f32[64,8,128]{2,0,1:T(8,128)}), f32[64,8,128]{2,0,1:T(8,128)S(1)}, u32[]{:S(2)}, u32[]{:S(2)}) %all-to-all-start.3) | async-done | bytes 262176 | tf_op jit(solution)/shard_map/all_to_all | solution.py:60
  119.9 0.7 copy_bitcast_fusion.3
  120.6 18.9 %all-gather.6.cloned.1.call-done = f32[2048,384]{1,0:T(8,128)} async-done(((f32[64,384]{1,0:T(8,128)}), f32[2048,384]{1,0:T(8,128)}) %all-gather.6.cloned.1.call-update) | async-done | bytes 3145744 | tf_op jit(solution)/shard_map/all_gather | solution.py:64
  139.5 1.1 slice_negate_fusion
  140.6 0.2 select_maximum_fusion
  140.8 0.1 copy.12
  140.9 1.6 slice-done
  142.5 0.6 fusion.9
  143.1 0.3 copy-done
  143.4 0.6 fusion.7
  144.1 2.2 fusion.23
  146.2 12.9 %all_to_all.31 = f32[8,256,64]{1,2,0:T(8,128)} all-to-all(f32[8,256,64]{1,2,0:T(8,128)S(1)} %fusion.23), channel_id=1, replica_groups=mesh['row'=8,'col'=32] {'row'}, dimensions={0} | all-to-all | bytes 1048576 | tf_op jit(solution)/shard_map/all_to_all | solution.py:82
  159.2 1.7 reduce_sum.9
  160.9 0.2 reduce-scatter.2.cloned.1.call-start
  161.2 6.6 %fusion.11 = f32[2048,704]{0,1:T(8,128)} fusion(f32[2048,256]{1,0:T(8,128)S(1)} %bitcast.79, f32[88,8,2,128]{3,2,1,0:T(2,128)S(1)} %bitcast.88), kind=kOutput, calls=%fused_computation.19 | convolution fusion | flops 4429185024 | bytes 8585216 | tf_op jit(solution)/shard_map/dot_general | solution.py:14
  167.8 0.7 broadcast_in_dim.46
  168.5 47.9 %all_to_all.32 = f32[352,2,8,128]{3,1,0,2:T(2,128)S(1)} all-to-all(f32[352,2,8,128]{3,1,0,2:T(2,128)S(1)} %broadcast_in_dim.46), channel_id=1, replica_groups=mesh['row'=8,'col'=32] {'row'}, dimensions={2} | all-to-all | bytes 5767168 | tf_op jit(solution)/shard_map/all_to_all | solution.py:41
  216.4 1.7 copy.15
  218.1 1.3 copy.37
  219.4 8.0 %fusion = f32[704,256]{1,0:T(8,128)} fusion(f32[2048,256]{1,0:T(8,128)} %all-gather.8.cloned.1.call-done, f32[352,2048]{1,0:T(8,128)S(1)} %bitcast.84, f32[176,2048]{1,0:T(8,128)} %bitcast.94, f32[176,2048]{1,0:T(8,128)} %bitcast.93), kind=kOutput, calls=%fused_computation | convolution fusion | flops 4432068608 | bytes 8585216 | tf_op jit(solution)/shard_map/dot_general | solution.py:10
  227.4 58.8 %reduce-scatter.2.cloned.1.call-done = f32[256,704]{0,1:T(8,128)} async-done(((f32[2048,704]{0,1:T(8,128)}), f32[256,704]{0,1:T(8,128)}) %reduce-scatter.2.cloned.1.call-update) | async-done | bytes 720912 | tf_op jit(solution)/shard_map/reduce_scatter | solution.py:88
  286.1 1.4 bitcast_subtract_fusion
  287.6 0.1 pad_maximum_fusion
  287.6 1.3 reshape.44
  (24 shorter events, 0.2 us)
Async XLA Ops:
  6.5 63.7 %all-gather.10.cloned.1.call-start = ((), (), s32[]{:S(2)}) async-start(), calls=%async_computation.10 | async-start | bytes 2162688 | tf_op jit(solution)/shard_map/all_gather | solution.py:32
  9.2 7.9 %copy-start.3 = (f32[1,64,2,128]{3,1,2,0:T(8,128)S(1)}, f32[1,64,2,128]{3,1,2,0:T(8,128)}, u32[]{:S(2)}) copy-start(f32[1,64,2,128]{3,1,2,0:T(8,128)} %copy.16) | copy-start | bytes 196612
  10.8 46.4 %all-to-all-start = ((f32[176,2,8,128]{3,1,0,2:T(2,128)}), f32[176,2,8,128]{3,1,0,2:T(2,128)S(1)}, u32[]{:S(2)}, u32[]{:S(2)}) async-start(f32[176,2,8,128]{3,1,0,2:T(2,128)} %broadcast_in_dim.39), calls=%async_computation | async-start | bytes 2883584 | tf_op jit(solution)/shard_map/all_to_all | solution.py:41
  58.0 17.9 %slice-start.1 = ((f32[12,64,2,128]{3,2,1,0:T(2,128)}), f32[1,64,2,128]{3,2,1,0:T(2,128)S(1)}, s32[]{:S(2)}) async-start(f32[12,64,2,128]{3,2,1,0:T(2,128)} %param.2), calls=%async_computation.12 | async-start | bytes 131072 | tf_op jit(solution)/shard_map/slice | solution.py:63
  72.4 9.5 %all-to-all-start.1 = ((f32[64,8,128]{2,0,1:T(8,128)}), f32[64,8,128]{2,0,1:T(8,128)S(1)}, u32[]{:S(2)}, u32[]{:S(2)}) async-start(f32[64,8,128]{2,0,1:T(8,128)} %broadcast_in_dim.40), calls=%async_computation.1 | async-start | bytes 524288 | tf_op jit(solution)/shard_map/all_to_all | solution.py:56
  75.9 63.6 %all-gather.6.cloned.1.call-start = ((), (), s32[]{:S(2)}) async-start(), calls=%async_computation.7 | async-start | bytes 3244032 | tf_op jit(solution)/shard_map/all_gather | solution.py:64
  110.5 9.4 %all-to-all-start.3 = ((f32[64,8,128]{2,0,1:T(8,128)}), f32[64,8,128]{2,0,1:T(8,128)S(1)}, u32[]{:S(2)}, u32[]{:S(2)}) async-start(f32[64,8,128]{2,0,1:T(8,128)} %broadcast_in_dim.43), calls=%async_computation.3 | async-start | bytes 524288 | tf_op jit(solution)/shard_map/all_to_all | solution.py:60
  113.9 105.5 %all-gather.8.cloned.1.call-start = ((), (), s32[]{:S(2)}) async-start(), calls=%async_computation.9 | async-start | bytes 2162688 | tf_op jit(solution)/shard_map/all_gather | solution.py:84
  114.8 1.8 copy-start.1
  140.9 1.6 slice-start
  140.9 2.5 copy-start
  140.9 2.5 copy-start.2
  146.2 14.9 %slice-start.2 = ((f32[12,64,2,128]{3,2,1,0:T(2,128)}), f32[11,64,2,128]{3,2,1,0:T(2,128)S(1)}, s32[]{:S(2)}) async-start(f32[12,64,2,128]{3,2,1,0:T(2,128)} %param.2), calls=%async_computation.13 | async-start | bytes 1441792 | tf_op jit(solution)/shard_map/slice | solution.py:89
  160.9 125.2 %reduce-scatter.2.cloned.1.call-start = ((), (), s32[]{:S(2)}) async-start(), calls=%async_computation.8 | async-start | bytes 6488064 | tf_op jit(solution)/shard_map/reduce_scatter | solution.py:88
  227.4 60.2 %copy-start.4 = (f32[256,64]{0,1:T(8,128)S(1)}, f32[256,64]{0,1:T(8,128)}, u32[]{:S(2)}) copy-start(f32[256,64]{0,1:T(8,128)} %reduce_sum.9) | copy-start | bytes 196612
Sparse Core Ops, SparseCore 0:
  10.0 60.2 all-gather.9
  84.2 55.1 all-gather.5
  161.0 54.5 all-gather.7
  218.0 68.0 reduce-scatter.1

commit v13 on v12

--- a/solution.py
+++ b/solution.py
@@ -33,7 +33,7 @@
 
     trail_count = cols_here - strip_width
     chunk = trail_count // 4
-    bounds = [0, chunk, 2 * chunk, trail_count]
+    bounds = [0, chunk, 2 * chunk, 3 * chunk, trail_count]
     left_chunks = []
     for lo, hi in zip(bounds[:-1], bounds[1:]):
         trail_part = lower[1:].reshape(trail_count, 2, 1, row_run)[lo:hi]
@@ -59,7 +59,7 @@
     chained_copies = jnp.broadcast_to(chained_piece[:, None, :], (strip_width, row_count, row_run))
     chained = lax.all_to_all(chained_copies, "row", split_axis=1, concat_axis=1, tiled=True)
     chained = chained.reshape(strip_width, block_size)
-    left_chunks[1], chained = lax.optimization_barrier((left_chunks[1], chained))
+    left_chunks[1:], chained = lax.optimization_barrier((left_chunks[1:], chained))
     joined = jnp.concatenate([strip[0].reshape(strip_width, 2 * row_run), chained_piece], axis=1)
     joined = lax.all_gather(joined, "col", axis=0, tiled=True)
     strip_lead = joined[:, : 2 * row_run]
@@ -85,12 +85,11 @@
 
     full_left = jnp.concatenate(left_chunks, axis=0)
     left_update = lax.optimization_barrier(times_rows(full_left, everything))
-    summed = lax.psum_scatter(
-        times_rows_turned(inverse_cols, strip_rows[strip_width:]),
-        "row",
-        scatter_dimension=0,
-        tiled=True,
-    )
+    trail_parts = times_rows_turned(inverse_cols, strip_rows[strip_width:])
+    trail_parts = trail_parts.reshape(row_count, 2 * row_run, trail_count)
+    trail_parts, solved_lead = lax.optimization_barrier((trail_parts, solved_lead))
+    trail_parts = lax.all_to_all(trail_parts, "row", split_axis=0, concat_axis=0, tiled=True)
+    summed = trail_parts.sum(axis=0)
     tail_rows = summed.T - left_update
     reduced = jnp.concatenate([solved_lead, tail_rows], axis=0)
     return reduced.reshape(rounds, strip_width, 2, row_run)

time: 296 us -> 289 us (0.976); the launches traced: 295 us -> 283 us
  blocking collectives: 126 us -> 49 us
  waiting for transfers between devices: 97.5 us -> 129 us
  starting transfers between devices: 13.5 us -> 33.4 us
  local copies, waits for them, and re-layouts: 18.9 us -> 29.3 us
    all_to_all x3 -> x1, blocking collectives: 86.1 us -> 9.33 us  [local(): lax.all_to_all(cross_copies, 'row', split_axis=1, concat_axis=1, tiled=True)]
    all_gather x1, waiting for transfers between devices: 0.02 us -> 60.9 us  [local(): everything = lax.all_gather(solved_lead, 'col', axis=0, tiled=True)]
    reduce_scatter x1 -> x0, waiting for transfers between devices: 58.8 us -> none  [local(): lax.psum_scatter(times_rows_turned(inverse_cols, strip_rows[strip_width:]...]
    all_to_all x1 -> x4, waiting for transfers between devices: 0.01 us -> 56.7 us  [local(): lax.all_to_all(copies, 'row', split_axis=2, concat_axis=2, tiled=True)]
    all_gather x1, waiting for transfers between devices: 18.9 us -> 0.02 us  [local(): joined = lax.all_gather(joined, 'col', axis=0, tiled=True)]
    all_to_all x1 -> x4, starting transfers between devices: 6.37 us -> 18.2 us  [local(): lax.all_to_all(copies, 'row', split_axis=2, concat_axis=2, tiled=True)]
    all_to_all x1 -> x2, starting transfers between devices: 3.41 us -> 10.5 us  [the longest x1 5.34 us: local(): lax.all_to_all(trail_parts, 'row', split_axis=0, concat_axis=0, tiled=True)]
    all_to_all x1 -> x2, waiting for transfers between devices: 6.03 us -> 0.06 us  [the longest x1 0.06 us: local(): lax.all_to_all(lead_parts, 'row', split_axis=0, concat_axis=0, tiled=True)]
  transfers between devices with their start and end apart: 7 -> 10, of which waited for: 5 -> 6; matrix products, arithmetic and copies ran while one was open for 9% -> 13% of each run, Pallas kernels for 0% -> 0%
where the time goes in v13:
time: 289 us; the launch traced here: 283 us
  waiting for transfers between devices  129 us (45%)
  blocking collectives  49 us (17%)
  starting transfers between devices  33.4 us (12%)
  local copies, waits for them, and re-layouts  29.3 us (10%)
  matrix products  22.2 us (8%)
  between operations  13.3 us (5%)
  other arithmetic  6.94 us (2%)
    all_gather x1, waiting for transfers between devices, local(): everything = lax.all_gather(solved_lead, 'col', axis=0, tiled=True)  60.9 us
    all_to_all x4, waiting for transfers between devices, local(): lax.all_to_all(copies, 'row', split_axis=2, concat_axis=2, tiled=True)  56.7 us
    all_gather x1, blocking collectives, local(): own_rows = lax.all_gather(lower[0], 'row', axis=2, tiled=True)  39.7 us
    all_to_all x4, starting transfers between devices, local(): lax.all_to_all(copies, 'row', split_axis=2, concat_axis=2, tiled=True)  18.2 us
    dot_general x5, matrix products, times_rows(): jnp.dot(coeff, right_side, precision=highest, preferred_element_type=jnp....  12.7 us
    all_gather x1, waiting for transfers between devices, local(): gathered = lax.all_gather(lower[0], 'col', axis=0, tiled=True)  11.1 us
    dot_general x2, matrix products, times_rows_turned(): lax.dot_general(coeff, right_turned, (((1,), (1,)), ((), ())), precision=...  9.54 us
    all_to_all x1, blocking collectives, local(): lax.all_to_all(cross_copies, 'row', split_axis=1, concat_axis=1, tiled=True)  9.33 us
  transfers between devices with their start and end apart: 10, of which 6 were waited for; matrix products, arithmetic and copies ran while one was open for 13% of the time, Pallas kernels for 0%

profile of v13, /device:TPU:1, one launch (start us, length us, event | category | flops | bytes accessed | tf_op | source)
XLA Modules:
  0.0 283.5 jit_solution(2771626508432192078)
XLA Ops:
  6.5 0.9 slice.55
  7.5 0.6 copy.17
  8.1 0.7 slice_bitcast_fusion.4
  8.8 1.5 broadcast_in_dim.46
  10.3 6.4 %all-to-all-start = ((f32[176,2,8,128]{3,1,0,2:T(2,128)}), f32[176,2,8,128]{3,1,0,2:T(2,128)S(1)}, u32[]{:S(2)}, u32[]{:S(2)}) async-start(f32[176,2,8,128]{3,1,0,2:T(2,128)} %broadcast_in_dim.46), calls=%async_computation | async-start | bytes 2883584 | tf_op jit(solution)/shard_map/all_to_all | solution.py:41
  16.7 39.7 %all-gather.1 = f32[1,64,2,1024]{3,1,2,0:T(8,128)S(1)} all-gather(f32[1,64,2,128]{3,1,2,0:T(8,128)S(1)} %copy-done.6), channel_id=3, replica_groups=mesh['row'=8,'col'=32] {'row'}, dimensions={3}, use_global_device_ids=true | all-gather | bytes 589824 | tf_op jit(solution)/shard_map/all_gather | solution.py:50
  56.4 0.8 copy.9
  57.3 1.6 copy.36
  58.9 11.1 %all-gather.10.cloned.1.call-done = f32[1,2048,2,128]{3,1,2,0:T(8,128)} async-done(((f32[1,64,2,128]{3,1,2,0:T(8,128)}), f32[1,2048,2,128]{3,1,2,0:T(8,128)}) %all-gather.10.cloned.1.call-update) | async-done | bytes 2097168 | tf_op jit(solution)/shard_map/all_gather | solution.py:32
  70.0 1.5 convolution_bitcast_fusion
  71.5 9.3 %all_to_all.40 = f32[64,8,128]{2,0,1:T(8,128)S(1)} all-to-all(f32[64,8,128]{2,0,1:T(8,128)S(1)} %broadcast_in_dim.47), channel_id=1, replica_groups=mesh['row'=8,'col'=32] {'row'}, dimensions={1} | all-to-all | bytes 524288 | tf_op jit(solution)/shard_map/all_to_all | solution.py:56
  80.8 1.5 broadcast_in_dim.53
  82.3 3.8 %all-to-all-start.4 = ((f32[176,2,8,128]{3,1,0,2:T(2,128)}), f32[176,2,8,128]{3,1,0,2:T(2,128)S(1)}, u32[]{:S(2)}, u32[]{:S(2)}) async-start(f32[176,2,8,128]{3,1,0,2:T(2,128)} %broadcast_in_dim.53), calls=%async_computation.4 | async-start | bytes 2883584 | tf_op jit(solution)/shard_map/all_to_all | solution.py:41
  86.1 1.5 fusion.15
  87.6 17.6 %all-to-all-done.4 = f32[176,2,8,128]{3,1,0,2:T(2,128)S(1)} async-done(((f32[176,2,8,128]{3,1,0,2:T(2,128)}), f32[176,2,8,128]{3,1,0,2:T(2,128)S(1)}, u32[]{:S(2)}, u32[]{:S(2)}) %all-to-all-start.4) | async-done | bytes 1441824 | tf_op jit(solution)/shard_map/all_to_all | solution.py:41
  105.2 1.5 broadcast_in_dim.51
  106.8 3.7 %all-to-all-start.3 = ((f32[176,2,8,128]{3,1,0,2:T(2,128)}), f32[176,2,8,128]{3,1,0,2:T(2,128)S(1)}, u32[]{:S(2)}, u32[]{:S(2)}) async-start(f32[176,2,8,128]{3,1,0,2:T(2,128)} %broadcast_in_dim.51), calls=%async_computation.3 | async-start | bytes 2883584 | tf_op jit(solution)/shard_map/all_to_all | solution.py:41
  110.5 0.6 pad_maximum_fusion.1
  111.2 18.4 %all-to-all-done.3 = f32[176,2,8,128]{3,1,0,2:T(2,128)S(1)} async-done(((f32[176,2,8,128]{3,1,0,2:T(2,128)}), f32[176,2,8,128]{3,1,0,2:T(2,128)S(1)}, u32[]{:S(2)}, u32[]{:S(2)}) %all-to-all-start.3) | async-done | bytes 1441824 | tf_op jit(solution)/shard_map/all_to_all | solution.py:41
  129.6 2.4 broadcast_in_dim.49
  132.1 4.3 %all-to-all-start.2 = ((f32[176,2,8,128]{3,1,0,2:T(2,128)}), f32[176,2,8,128]{3,1,0,2:T(2,128)}, u32[]{:S(2)}, u32[]{:S(2)}) async-start(f32[176,2,8,128]{3,1,0,2:T(2,128)} %broadcast_in_dim.49), calls=%async_computation.2 | async-start | bytes 2883584 | tf_op jit(solution)/shard_map/all_to_all | solution.py:41
  136.4 1.9 copy.15
  138.3 2.0 copy.14
  140.3 20.6 %all-to-all-done.2 = f32[176,2,8,128]{3,1,0,2:T(2,128)} async-done(((f32[176,2,8,128]{3,1,0,2:T(2,128)}), f32[176,2,8,128]{3,1,0,2:T(2,128)}, u32[]{:S(2)}, u32[]{:S(2)}) %all-to-all-start.2) | async-done | bytes 1441824 | tf_op jit(solution)/shard_map/all_to_all | solution.py:41
  161.0 0.7 broadcast_in_dim.54
  161.7 4.5 %all-to-all-start.5 = ((f32[64,8,128]{2,0,1:T(8,128)}), f32[64,8,128]{2,0,1:T(8,128)S(1)}, u32[]{:S(2)}, u32[]{:S(2)}) async-start(f32[64,8,128]{2,0,1:T(8,128)} %broadcast_in_dim.54), calls=%async_computation.5 | async-start | bytes 524288 | tf_op jit(solution)/shard_map/all_to_all | solution.py:60
  166.2 4.2 %copy_bitcast_fusion = (f32[176,2048]{1,0:T(8,128)}, f32[176,2048]{1,0:T(8,128)}) fusion(f32[22,8,16,128]{3,2,1,0:T(8,128)S(1)} %bitcast.82, f32[22,8,16,128]{3,2,1,0:T(8,128)} %bitcast.83), kind=kLoop, calls=%fused_computation.10 | loop fusion | bytes 5767168 | tf_op jit(solution)/shard_map/reshape | solution.py:42
  170.4 2.2 copy.13
  172.6 1.7 copy.35
  174.5 1.1 slice_negate_fusion
  175.6 0.2 select_maximum_fusion
  176.0 1.6 slice-done
  177.5 0.6 fusion.11
  178.2 0.3 copy-done.1
  178.5 0.6 fusion.9
  179.1 3.0 %fusion.23 = f32[8,256,64]{1,2,0:T(8,128)} fusion(f32[8,256,256]{2,1,0:T(8,128)S(1)} %bitcast.77, f32[64,256,1]{1,0,2:T(8,128)S(1)} %fusion.9), kind=kOutput, calls=%fused_computation.44 | convolution fusion | flops 402653184 | bytes 2686976 | tf_op jit(solution)/shard_map/dot_general | solution.py:14
  182.1 5.1 %all-to-all-start.6 = ((f32[8,256,64]{1,2,0:T(8,128)}), f32[8,256,64]{1,2,0:T(8,128)}, u32[]{:S(2)}, u32[]{:S(2)}) async-start(f32[8,256,64]{1,2,0:T(8,128)} %fusion.23), calls=%async_computation.6 | async-start | bytes 1048576 | tf_op jit(solution)/shard_map/all_to_all | solution.py:82
  187.2 0.6 reshape.54
  187.8 6.6 %fusion.22 = f32[8,256,704]{1,2,0:T(8,128)} fusion(f32[8,256,256]{2,1,0:T(8,128)S(1)} %bitcast.78, f32[704,256,1]{1,0,2:T(8,128)S(1)} %reshape.54), kind=kOutput, calls=%fused_computation.43 | convolution fusion | flops 4429185024 | bytes 8585216 | tf_op jit(solution)/shard_map/dot_general | solution.py:14
  194.5 1.7 reduce_sum.18
  196.2 5.3 %all-to-all-start.7 = ((f32[8,256,704]{1,2,0:T(8,128)}), f32[8,256,704]{1,2,0:T(8,128)}, u32[]{:S(2)}, u32[]{:S(2)}) async-start(f32[8,256,704]{1,2,0:T(8,128)} %fusion.22), calls=%async_computation.7 | async-start | bytes 11534336 | tf_op jit(solution)/shard_map/all_to_all | solution.py:91
  201.5 0.3 all-gather.8.cloned.1.call-start
  201.8 0.5 all-gather.8.cloned.1.call-update
  202.2 60.9 %all-gather.8.cloned.1.call-done = f32[2048,256]{1,0:T(8,128)} async-done(((f32[64,256]{1,0:T(8,128)}), f32[2048,256]{1,0:T(8,128)}) %all-gather.8.cloned.1.call-update) | async-done | bytes 2097168 | tf_op jit(solution)/shard_map/all_gather | solution.py:84
  263.2 8.5 %fusion = f32[704,256]{1,0:T(8,128)} fusion(f32[2048,256]{1,0:T(8,128)} %all-gather.8.cloned.1.call-done, f32[176,2048]{1,0:T(8,128)} %get-tuple-element.20, f32[176,2048]{1,0:T(8,128)} %get-tuple-element.19, f32[176,2048]{1,0:T(8,128)S(1)} %bitcast.91, f32[176,2048]{1,0:T(8,128)S(1)} %bitcast.90), kind=kOutput, calls=%fused_computation | convolution fusion | flops 4433510400 | bytes 8585216 | tf_op jit(solution)/shard_map/dot_general | solution.py:10
  271.6 3.2 %reduce_sum.19 = f32[256,704]{0,1:T(8,128)S(1)} reduce(f32[8,256,704]{1,2,0:T(8,128)} %all-to-all-done.7, f32[]{:T(128)} %constant.13.clone.1), dimensions={0}, to_apply=%region_1.2 | reduce | flops 1261568 | bytes 6488068 | tf_op jit(solution)/shard_map/reduce_sum | solution.py:92
  274.9 0.7 copy-done.7
  275.7 1.3 reshape.49
  (37 shorter events, 0.7 us)
Async XLA Ops:
  6.5 1.6 slice-start.1
  6.5 63.5 %all-gather.10.cloned.1.call-start = ((), (), s32[]{:S(2)}) async-start(), calls=%async_computation.10 | async-start | bytes 2162688 | tf_op jit(solution)/shard_map/all_gather | solution.py:32
  8.8 7.9 %copy-start.6 = (f32[1,64,2,128]{3,1,2,0:T(8,128)S(1)}, f32[1,64,2,128]{3,1,2,0:T(8,128)}, u32[]{:S(2)}) copy-start(f32[1,64,2,128]{3,1,2,0:T(8,128)} %copy.17) | copy-start | bytes 196612
  10.3 46.1 %all-to-all-start = ((f32[176,2,8,128]{3,1,0,2:T(2,128)}), f32[176,2,8,128]{3,1,0,2:T(2,128)S(1)}, u32[]{:S(2)}, u32[]{:S(2)}) async-start(f32[176,2,8,128]{3,1,0,2:T(2,128)} %broadcast_in_dim.46), calls=%async_computation | async-start | bytes 2883584 | tf_op jit(solution)/shard_map/all_to_all | solution.py:41
  80.8 5.3 %slice-start.2 = ((f32[12,64,2,128]{3,2,1,0:T(2,128)}), f32[1,64,2,128]{3,2,1,0:T(2,128)S(1)}, s32[]{:S(2)}) async-start(f32[12,64,2,128]{3,2,1,0:T(2,128)} %param.2), calls=%async_computation.13 | async-start | bytes 131072 | tf_op jit(solution)/shard_map/slice | solution.py:63
  82.3 22.9 %all-to-all-start.4 = ((f32[176,2,8,128]{3,1,0,2:T(2,128)}), f32[176,2,8,128]{3,1,0,2:T(2,128)S(1)}, u32[]{:S(2)}, u32[]{:S(2)}) async-start(f32[176,2,8,128]{3,1,0,2:T(2,128)} %broadcast_in_dim.53), calls=%async_computation.4 | async-start | bytes 2883584 | tf_op jit(solution)/shard_map/all_to_all | solution.py:41
  106.8 22.9 %all-to-all-start.3 = ((f32[176,2,8,128]{3,1,0,2:T(2,128)}), f32[176,2,8,128]{3,1,0,2:T(2,128)S(1)}, u32[]{:S(2)}, u32[]{:S(2)}) async-start(f32[176,2,8,128]{3,1,0,2:T(2,128)} %broadcast_in_dim.51), calls=%async_computation.3 | async-start | bytes 2883584 | tf_op jit(solution)/shard_map/all_to_all | solution.py:41
  110.5 64.0 %all-gather.6.cloned.1.call-start = ((), (), s32[]{:S(2)}) async-start(), calls=%async_computation.8 | async-start | bytes 3244032 | tf_op jit(solution)/shard_map/all_gather | solution.py:64
  132.1 28.9 %all-to-all-start.2 = ((f32[176,2,8,128]{3,1,0,2:T(2,128)}), f32[176,2,8,128]{3,1,0,2:T(2,128)}, u32[]{:S(2)}, u32[]{:S(2)}) async-start(f32[176,2,8,128]{3,1,0,2:T(2,128)} %broadcast_in_dim.49), calls=%async_computation.2 | async-start | bytes 2883584 | tf_op jit(solution)/shard_map/all_to_all | solution.py:41
  138.3 27.9 %copy-start = (f32[176,2,8,128]{3,2,1,0:T(8,128)S(1)}, f32[176,2,8,128]{3,2,1,0:T(8,128)}, u32[]{:S(2)}) copy-start(f32[176,2,8,128]{3,2,1,0:T(8,128)} %copy.15) | copy-start | bytes 4325380
  161.7 12.8 %all-to-all-start.5 = ((f32[64,8,128]{2,0,1:T(8,128)}), f32[64,8,128]{2,0,1:T(8,128)S(1)}, u32[]{:S(2)}, u32[]{:S(2)}) async-start(f32[64,8,128]{2,0,1:T(8,128)} %broadcast_in_dim.54), calls=%async_computation.5 | async-start | bytes 524288 | tf_op jit(solution)/shard_map/all_to_all | solution.py:60
  172.6 1.8 copy-start.2
  176.0 1.6 slice-start
  176.0 2.5 copy-start.1
  179.1 8.1 %slice-start.3 = ((f32[12,64,2,128]{3,2,1,0:T(2,128)}), f32[11,64,2,128]{3,2,1,0:T(2,128)S(1)}, s32[]{:S(2)}) async-start(f32[12,64,2,128]{3,2,1,0:T(2,128)} %param.2), calls=%async_computation.14 | async-start | bytes 1441792 | tf_op jit(solution)/shard_map/slice | solution.py:88
  182.1 12.4 %all-to-all-start.6 = ((f32[8,256,64]{1,2,0:T(8,128)}), f32[8,256,64]{1,2,0:T(8,128)}, u32[]{:S(2)}, u32[]{:S(2)}) async-start(f32[8,256,64]{1,2,0:T(8,128)} %fusion.23), calls=%async_computation.6 | async-start | bytes 1048576 | tf_op jit(solution)/shard_map/all_to_all | solution.py:82
  196.2 67.0 %copy-start.3 = (f32[22,8,16,128]{3,1,2,0:T(8,128)S(1)}, f32[22,8,16,128]{3,1,2,0:T(8,128)}, u32[]{:S(2)}) copy-start(f32[22,8,16,128]{3,1,2,0:T(8,128)} %copy.36) | copy-start | bytes 4325380
  196.2 67.0 %copy-start.4 = (f32[22,8,16,128]{3,1,2,0:T(8,128)S(1)}, f32[22,8,16,128]{3,1,2,0:T(8,128)}, u32[]{:S(2)}) copy-start(f32[22,8,16,128]{3,1,2,0:T(8,128)} %copy.35) | copy-start | bytes 4325380
  196.2 75.5 %all-to-all-start.7 = ((f32[8,256,704]{1,2,0:T(8,128)}), f32[8,256,704]{1,2,0:T(8,128)}, u32[]{:S(2)}, u32[]{:S(2)}) async-start(f32[8,256,704]{1,2,0:T(8,128)} %fusion.22), calls=%async_computation.7 | async-start | bytes 11534336 | tf_op jit(solution)/shard_map/all_to_all | solution.py:91
  201.5 61.6 %all-gather.8.cloned.1.call-start = ((), (), s32[]{:S(2)}) async-start(), calls=%async_computation.9 | async-start | bytes 2162688 | tf_op jit(solution)/shard_map/all_gather | solution.py:84
  271.6 3.2 %copy-start.5 = (f32[704,256]{1,0:T(8,128)S(1)}, f32[704,256]{1,0:T(8,128)}, u32[]{:S(2)}) copy-start(f32[704,256]{1,0:T(8,128)} %fusion) | copy-start | bytes 2162692
  274.8 0.8 copy-start.7
Sparse Core Ops, SparseCore 0:
  10.0 59.9 all-gather.9
  113.9 56.8 all-gather.5
  204.9 58.2 all-gather.7

commit v14 on v13

--- a/solution.py
+++ b/solution.py
@@ -59,9 +59,9 @@
     chained_copies = jnp.broadcast_to(chained_piece[:, None, :], (strip_width, row_count, row_run))
     chained = lax.all_to_all(chained_copies, "row", split_axis=1, concat_axis=1, tiled=True)
     chained = chained.reshape(strip_width, block_size)
-    left_chunks[1:], chained = lax.optimization_barrier((left_chunks[1:], chained))
     joined = jnp.concatenate([strip[0].reshape(strip_width, 2 * row_run), chained_piece], axis=1)
     joined = lax.all_gather(joined, "col", axis=0, tiled=True)
+    left_chunks[1:], joined = lax.optimization_barrier((left_chunks[1:], joined))
     strip_lead = joined[:, : 2 * row_run]
     chained_cols = joined[block_size:, 2 * row_run :]
 

time: 289 us -> 282 us (0.976)
  blocking collectives: 49 us -> 71.8 us
  waiting for transfers between devices: 129 us -> 113 us
  local copies, waits for them, and re-layouts: 29.3 us -> 21 us
  starting transfers between devices: 33.4 us -> 28.5 us
    all_to_all x0 -> x1, blocking collectives: none -> 23.8 us  [local(): lax.all_to_all(copies, 'row', split_axis=2, concat_axis=2, tiled=True)]
    all_to_all x4 -> x3, waiting for transfers between devices: 56.7 us -> 34.9 us  [local(): lax.all_to_all(copies, 'row', split_axis=2, concat_axis=2, tiled=True)]
    all_to_all x4 -> x3, starting transfers between devices: 18.2 us -> 13.7 us  [local(): lax.all_to_all(copies, 'row', split_axis=2, concat_axis=2, tiled=True)]
    all_to_all x4, local copies, waits for them, and re-layouts: 6.97 us -> 3.35 us  [local(): lax.all_to_all(copies, 'row', split_axis=2, concat_axis=2, tiled=True)]
  transfers between devices with their start and end apart: 10 -> 9, of which waited for: 6 -> 6; matrix products, arithmetic and copies ran while one was open for 13% -> 12% of each run, Pallas kernels for 0% -> 0%
where the time goes in v14:
time: 282 us; the launch traced here: 278 us
  waiting for transfers between devices  113 us (40%)
  blocking collectives  71.8 us (25%)
  starting transfers between devices  28.5 us (10%)
  matrix products  23.4 us (8%)
  local copies, waits for them, and re-layouts  21 us (7%)
  between operations  13.4 us (5%)
  other arithmetic  6.87 us (2%)
    all_gather x1, waiting for transfers between devices, local(): everything = lax.all_gather(solved_lead, 'col', axis=0, tiled=True)  61.8 us
    all_gather x1, blocking collectives, local(): own_rows = lax.all_gather(lower[0], 'row', axis=2, tiled=True)  39 us
    all_to_all x3, waiting for transfers between devices, local(): lax.all_to_all(copies, 'row', split_axis=2, concat_axis=2, tiled=True)  34.9 us
    all_to_all x1, blocking collectives, local(): lax.all_to_all(copies, 'row', split_axis=2, concat_axis=2, tiled=True)  23.8 us
    dot_general x5, matrix products, times_rows(): jnp.dot(coeff, right_side, precision=highest, preferred_element_type=jnp....  13.9 us
    all_to_all x3, starting transfers between devices, local(): lax.all_to_all(copies, 'row', split_axis=2, concat_axis=2, tiled=True)  13.7 us
    all_gather x1, waiting for transfers between devices, local(): gathered = lax.all_gather(lower[0], 'col', axis=0, tiled=True)  12.4 us
    dot_general x2, matrix products, times_rows_turned(): lax.dot_general(coeff, right_turned, (((1,), (1,)), ((), ())), precision=...  9.53 us
  transfers between devices with their start and end apart: 9, of which 6 were waited for; matrix products, arithmetic and copies ran while one was open for 12% of the time, Pallas kernels for 0%

profile of v14, /device:TPU:1, one launch (start us, length us, event | category | flops | bytes accessed | tf_op | source)
XLA Modules:
  0.0 277.8 jit_solution(11032870231870016681)
XLA Ops:
  6.5 0.9 slice.55
  7.5 0.6 copy.17
  8.2 1.5 broadcast_in_dim.46
  9.7 6.4 %all-to-all-start = ((f32[176,2,8,128]{3,1,0,2:T(2,128)}), f32[176,2,8,128]{3,1,0,2:T(2,128)S(1)}, u32[]{:S(2)}, u32[]{:S(2)}) async-start(f32[176,2,8,128]{3,1,0,2:T(2,128)} %broadcast_in_dim.46), calls=%async_computation | async-start | bytes 2883584 | tf_op jit(solution)/shard_map/all_to_all | solution.py:41
  16.1 39.0 %all-gather.1 = f32[1,64,2,1024]{3,1,2,0:T(8,128)S(1)} all-gather(f32[1,64,2,128]{3,1,2,0:T(8,128)S(1)} %copy-done.5), channel_id=3, replica_groups=mesh['row'=8,'col'=32] {'row'}, dimensions={3}, use_global_device_ids=true | all-gather | bytes 589824 | tf_op jit(solution)/shard_map/all_gather | solution.py:50
  55.1 0.8 copy.9
  55.9 1.6 copy.39
  57.6 12.4 %all-gather.10.cloned.1.call-done = f32[1,2048,2,128]{3,1,2,0:T(8,128)} async-done(((f32[1,64,2,128]{3,1,2,0:T(8,128)}), f32[1,2048,2,128]{3,1,2,0:T(8,128)}) %all-gather.10.cloned.1.call-update) | async-done | bytes 2097168 | tf_op jit(solution)/shard_map/all_gather | solution.py:32
  69.9 1.5 convolution_bitcast_fusion
  71.5 9.0 %all_to_all.40 = f32[64,8,128]{2,0,1:T(8,128)S(1)} all-to-all(f32[64,8,128]{2,0,1:T(8,128)S(1)} %broadcast_in_dim.53), channel_id=1, replica_groups=mesh['row'=8,'col'=32] {'row'}, dimensions={1} | all-to-all | bytes 524288 | tf_op jit(solution)/shard_map/all_to_all | solution.py:56
  80.5 1.5 broadcast_in_dim.48
  82.0 3.8 %all-to-all-start.1 = ((f32[176,2,8,128]{3,1,0,2:T(2,128)}), f32[176,2,8,128]{3,1,0,2:T(2,128)S(1)}, u32[]{:S(2)}, u32[]{:S(2)}) async-start(f32[176,2,8,128]{3,1,0,2:T(2,128)} %broadcast_in_dim.48), calls=%async_computation.1 | async-start | bytes 2883584 | tf_op jit(solution)/shard_map/all_to_all | solution.py:41
  85.9 1.5 fusion.17
  87.3 0.6 pad_maximum_fusion.1
  88.0 16.9 %all-to-all-done.1 = f32[176,2,8,128]{3,1,0,2:T(2,128)S(1)} async-done(((f32[176,2,8,128]{3,1,0,2:T(2,128)}), f32[176,2,8,128]{3,1,0,2:T(2,128)S(1)}, u32[]{:S(2)}, u32[]{:S(2)}) %all-to-all-start.1) | async-done | bytes 1441824 | tf_op jit(solution)/shard_map/all_to_all | solution.py:41
  104.9 0.4 broadcast_in_dim.52
  105.3 23.8 %all_to_all.41 = f32[176,2,8,128]{3,1,0,2:T(2,128)} all-to-all(f32[176,2,8,128]{3,1,0,2:T(2,128)S(1)} %broadcast_in_dim.52), channel_id=1, replica_groups=mesh['row'=8,'col'=32] {'row'}, dimensions={2} | all-to-all | bytes 2883584 | tf_op jit(solution)/shard_map/all_to_all | solution.py:41
  129.1 1.5 broadcast_in_dim.50
  130.6 3.6 %all-to-all-start.2 = ((f32[176,2,8,128]{3,1,0,2:T(2,128)}), f32[176,2,8,128]{3,1,0,2:T(2,128)S(1)}, u32[]{:S(2)}, u32[]{:S(2)}) async-start(f32[176,2,8,128]{3,1,0,2:T(2,128)} %broadcast_in_dim.50), calls=%async_computation.2 | async-start | bytes 2883584 | tf_op jit(solution)/shard_map/all_to_all | solution.py:41
  134.2 0.8 copy.11
  135.1 1.6 copy.38
  136.7 0.8 copy.13
  137.5 18.0 %all-to-all-done.2 = f32[176,2,8,128]{3,1,0,2:T(2,128)S(1)} async-done(((f32[176,2,8,128]{3,1,0,2:T(2,128)}), f32[176,2,8,128]{3,1,0,2:T(2,128)S(1)}, u32[]{:S(2)}, u32[]{:S(2)}) %all-to-all-start.2) | async-done | bytes 1441824 | tf_op jit(solution)/shard_map/all_to_all | solution.py:41
  155.5 0.8 copy.12
  156.4 2.9 %copy_bitcast_fusion = (f32[176,2048]{1,0:T(8,128)}, f32[176,2048]{1,0:T(8,128)}) fusion(f32[22,8,16,128]{3,2,1,0:T(8,128)S(1)} %bitcast.83, f32[22,8,16,128]{3,2,1,0:T(8,128)S(1)} %bitcast.84), kind=kLoop, calls=%fused_computation.10 | loop fusion | bytes 5767168 | tf_op jit(solution)/shard_map/reshape | solution.py:42
  159.3 0.7 broadcast_in_dim.54
  160.0 5.2 %all-to-all-start.5 = ((f32[64,8,128]{2,0,1:T(8,128)}), f32[64,8,128]{2,0,1:T(8,128)S(1)}, u32[]{:S(2)}, u32[]{:S(2)}) async-start(f32[64,8,128]{2,0,1:T(8,128)} %broadcast_in_dim.54), calls=%async_computation.5 | async-start | bytes 524288 | tf_op jit(solution)/shard_map/all_to_all | solution.py:60
  165.3 1.1 slice_negate_fusion
  166.4 0.2 select_maximum_fusion
  166.6 0.1 copy.15
  166.8 1.4 slice-done
  168.2 0.6 fusion.11
  168.8 2.5 all-to-all-done.5
  171.4 1.9 fusion.9
  173.2 3.0 %fusion.25 = f32[8,256,64]{1,2,0:T(8,128)} fusion(f32[8,256,256]{2,1,0:T(8,128)S(1)} %bitcast.78, f32[64,256,1]{1,0,2:T(8,128)S(1)} %fusion.9), kind=kOutput, calls=%fused_computation.45 | convolution fusion | flops 402653184 | bytes 2686976 | tf_op jit(solution)/shard_map/dot_general | solution.py:14
  176.2 4.1 %all-to-all-start.6 = ((f32[8,256,64]{1,2,0:T(8,128)}), f32[8,256,64]{1,2,0:T(8,128)}, u32[]{:S(2)}, u32[]{:S(2)}) async-start(f32[8,256,64]{1,2,0:T(8,128)} %fusion.25), calls=%async_computation.6 | async-start | bytes 1048576 | tf_op jit(solution)/shard_map/all_to_all | solution.py:82
  180.4 0.6 reshape.54
  180.9 6.6 %fusion.24 = f32[8,256,704]{1,2,0:T(8,128)} fusion(f32[8,256,256]{2,1,0:T(8,128)S(1)} %bitcast.79, f32[704,256,1]{1,0,2:T(8,128)S(1)} %reshape.54), kind=kOutput, calls=%fused_computation.44 | convolution fusion | flops 4429185024 | bytes 8585216 | tf_op jit(solution)/shard_map/dot_general | solution.py:14
  187.5 1.7 reduce_sum.18
  189.2 5.3 %all-to-all-start.7 = ((f32[8,256,704]{1,2,0:T(8,128)}), f32[8,256,704]{1,2,0:T(8,128)}, u32[]{:S(2)}, u32[]{:S(2)}) async-start(f32[8,256,704]{1,2,0:T(8,128)} %fusion.24), calls=%async_computation.7 | async-start | bytes 11534336 | tf_op jit(solution)/shard_map/all_to_all | solution.py:91
  194.6 0.7 all-gather.8.cloned.1.call-update
  195.3 61.8 %all-gather.8.cloned.1.call-done = f32[2048,256]{1,0:T(8,128)} async-done(((f32[64,256]{1,0:T(8,128)}), f32[2048,256]{1,0:T(8,128)}) %all-gather.8.cloned.1.call-update) | async-done | bytes 2097168 | tf_op jit(solution)/shard_map/all_gather | solution.py:84
  257.1 8.5 %fusion = f32[704,256]{1,0:T(8,128)} fusion(f32[2048,256]{1,0:T(8,128)} %all-gather.8.cloned.1.call-done, f32[176,2048]{1,0:T(8,128)} %get-tuple-element.20, f32[176,2048]{1,0:T(8,128)} %get-tuple-element.19, f32[176,2048]{1,0:T(8,128)S(1)} %bitcast.92, f32[176,2048]{1,0:T(8,128)S(1)} %bitcast.91), kind=kOutput, calls=%fused_computation | convolution fusion | flops 4433510400 | bytes 8585216 | tf_op jit(solution)/shard_map/dot_general | solution.py:10
  265.5 0.5 all-to-all-done.7
  266.0 3.1 %reduce_sum.19 = f32[256,704]{0,1:T(8,128)S(1)} reduce(f32[8,256,704]{1,2,0:T(8,128)} %all-to-all-done.7, f32[]{:T(128)} %constant.13.clone.1), dimensions={0}, to_apply=%region_1.2 | reduce | flops 1261568 | bytes 6488068 | tf_op jit(solution)/shard_map/reduce_sum | solution.py:92
  269.2 0.1 bitcast_subtract_fusion
  269.3 0.7 copy-done.6
  270.1 1.3 reshape.49
  (33 shorter events, 0.4 us)
Async XLA Ops:
  6.5 1.6 slice-start.1
  6.5 63.4 %all-gather.10.cloned.1.call-start = ((), (), s32[]{:S(2)}) async-start(), calls=%async_computation.10 | async-start | bytes 2162688 | tf_op jit(solution)/shard_map/all_gather | solution.py:32
  8.2 7.9 %copy-start.5 = (f32[1,64,2,128]{3,1,2,0:T(8,128)S(1)}, f32[1,64,2,128]{3,1,2,0:T(8,128)}, u32[]{:S(2)}) copy-start(f32[1,64,2,128]{3,1,2,0:T(8,128)} %copy.17) | copy-start | bytes 196612
  9.7 45.4 %all-to-all-start = ((f32[176,2,8,128]{3,1,0,2:T(2,128)}), f32[176,2,8,128]{3,1,0,2:T(2,128)S(1)}, u32[]{:S(2)}, u32[]{:S(2)}) async-start(f32[176,2,8,128]{3,1,0,2:T(2,128)} %broadcast_in_dim.46), calls=%async_computation | async-start | bytes 2883584 | tf_op jit(solution)/shard_map/all_to_all | solution.py:41
  80.5 5.3 %slice-start.2 = ((f32[12,64,2,128]{3,2,1,0:T(2,128)}), f32[1,64,2,128]{3,2,1,0:T(2,128)S(1)}, s32[]{:S(2)}) async-start(f32[12,64,2,128]{3,2,1,0:T(2,128)} %param.2), calls=%async_computation.13 | async-start | bytes 131072 | tf_op jit(solution)/shard_map/slice | solution.py:62
  82.0 22.9 %all-to-all-start.1 = ((f32[176,2,8,128]{3,1,0,2:T(2,128)}), f32[176,2,8,128]{3,1,0,2:T(2,128)S(1)}, u32[]{:S(2)}, u32[]{:S(2)}) async-start(f32[176,2,8,128]{3,1,0,2:T(2,128)} %broadcast_in_dim.48), calls=%async_computation.1 | async-start | bytes 2883584 | tf_op jit(solution)/shard_map/all_to_all | solution.py:41
  85.8 79.5 %all-gather.6.cloned.1.call-start = ((), (), s32[]{:S(2)}) async-start(), calls=%async_computation.8 | async-start | bytes 3244032 | tf_op jit(solution)/shard_map/all_gather | solution.py:63
  130.6 24.9 %all-to-all-start.2 = ((f32[176,2,8,128]{3,1,0,2:T(2,128)}), f32[176,2,8,128]{3,1,0,2:T(2,128)S(1)}, u32[]{:S(2)}, u32[]{:S(2)}) async-start(f32[176,2,8,128]{3,1,0,2:T(2,128)} %broadcast_in_dim.50), calls=%async_computation.2 | async-start | bytes 2883584 | tf_op jit(solution)/shard_map/all_to_all | solution.py:41
  135.0 1.7 copy-start
  156.4 2.9 %copy-start.1 = (f32[1,2048,2,128]{3,1,2,0:T(8,128)S(1)}, f32[1,2048,2,128]{3,1,2,0:T(8,128)}, u32[]{:S(2)}) copy-start(f32[1,2048,2,128]{3,1,2,0:T(8,128)} %all-gather.10.cloned.1.call-done) | copy-start | bytes 6291460
  160.0 11.3 %all-to-all-start.5 = ((f32[64,8,128]{2,0,1:T(8,128)}), f32[64,8,128]{2,0,1:T(8,128)S(1)}, u32[]{:S(2)}, u32[]{:S(2)}) async-start(f32[64,8,128]{2,0,1:T(8,128)} %broadcast_in_dim.54), calls=%async_computation.5 | async-start | bytes 524288 | tf_op jit(solution)/shard_map/all_to_all | solution.py:60
  166.6 1.6 slice-start
  173.2 7.1 %slice-start.3 = ((f32[12,64,2,128]{3,2,1,0:T(2,128)}), f32[11,64,2,128]{3,2,1,0:T(2,128)S(1)}, s32[]{:S(2)}) async-start(f32[12,64,2,128]{3,2,1,0:T(2,128)} %param.2), calls=%async_computation.14 | async-start | bytes 1441792 | tf_op jit(solution)/shard_map/slice | solution.py:88
  176.2 11.3 %all-to-all-start.6 = ((f32[8,256,64]{1,2,0:T(8,128)}), f32[8,256,64]{1,2,0:T(8,128)}, u32[]{:S(2)}, u32[]{:S(2)}) async-start(f32[8,256,64]{1,2,0:T(8,128)} %fusion.25), calls=%async_computation.6 | async-start | bytes 1048576 | tf_op jit(solution)/shard_map/all_to_all | solution.py:82
  189.2 67.9 %copy-start.2 = (f32[22,8,16,128]{3,1,2,0:T(8,128)S(1)}, f32[22,8,16,128]{3,1,2,0:T(8,128)}, u32[]{:S(2)}) copy-start(f32[22,8,16,128]{3,1,2,0:T(8,128)} %copy.39) | copy-start | bytes 4325380
  189.2 67.9 %copy-start.3 = (f32[22,8,16,128]{3,1,2,0:T(8,128)S(1)}, f32[22,8,16,128]{3,1,2,0:T(8,128)}, u32[]{:S(2)}) copy-start(f32[22,8,16,128]{3,1,2,0:T(8,128)} %copy.38) | copy-start | bytes 4325380
  189.2 76.8 %all-to-all-start.7 = ((f32[8,256,704]{1,2,0:T(8,128)}), f32[8,256,704]{1,2,0:T(8,128)}, u32[]{:S(2)}, u32[]{:S(2)}) async-start(f32[8,256,704]{1,2,0:T(8,128)} %fusion.24), calls=%async_computation.7 | async-start | bytes 11534336 | tf_op jit(solution)/shard_map/all_to_all | solution.py:91
  194.5 62.6 %all-gather.8.cloned.1.call-start = ((), (), s32[]{:S(2)}) async-start(), calls=%async_computation.9 | async-start | bytes 2162688 | tf_op jit(solution)/shard_map/all_gather | solution.py:84
  265.5 3.6 %copy-start.4 = (f32[704,256]{1,0:T(8,128)S(1)}, f32[704,256]{1,0:T(8,128)}, u32[]{:S(2)}) copy-start(f32[704,256]{1,0:T(8,128)} %fusion) | copy-start | bytes 2162692
  269.2 0.8 copy-start.6
Sparse Core Ops, SparseCore 0:
  10.0 59.9 all-gather.9
  89.2 58.8 all-gather.5
  197.9 59.1 all-gather.7

commit v15 on v14

--- a/solution.py
+++ b/solution.py
@@ -61,7 +61,7 @@
     chained = chained.reshape(strip_width, block_size)
     joined = jnp.concatenate([strip[0].reshape(strip_width, 2 * row_run), chained_piece], axis=1)
     joined = lax.all_gather(joined, "col", axis=0, tiled=True)
-    left_chunks[1:], joined = lax.optimization_barrier((left_chunks[1:], joined))
+    left_chunks[1:3], joined = lax.optimization_barrier((left_chunks[1:3], joined))
     strip_lead = joined[:, : 2 * row_run]
     chained_cols = joined[block_size:, 2 * row_run :]
 

time: 282 us -> 301 us (1.067); the launches traced: 278 us -> 300 us
  waiting for transfers between devices: 113 us -> 126 us
  local copies, waits for them, and re-layouts: 21 us -> 26.5 us
  blocking collectives: 71.8 us -> 75.6 us
    all_gather x1, waiting for transfers between devices: 61.8 us -> 78.8 us  [local(): everything = lax.all_gather(solved_lead, 'col', axis=0, tiled=True)]
    all_to_all x3, waiting for transfers between devices: 34.9 us -> 26.5 us  [local(): lax.all_to_all(copies, 'row', split_axis=2, concat_axis=2, tiled=True)]
    all_to_all x1, waiting for transfers between devices: 0.01 us -> 5.99 us  [local(): lax.all_to_all(cross_copies, 'row', split_axis=1, concat_axis=1, tiled=True)]
    slice x3 -> x2, local copies, waits for them, and re-layouts: 0.58 us -> 4.62 us  [local(): trail_parts = times_rows_turned(inverse_cols, strip_rows[strip_width:])]
  transfers between devices with their start and end apart: 9 -> 9, of which waited for: 6 -> 6; matrix products, arithmetic and copies ran while one was open for 12% -> 13% of each run, Pallas kernels for 0% -> 0%
where the time goes in v15:
time: 301 us; the launch traced here: 300 us
  waiting for transfers between devices  126 us (42%)
  blocking collectives  75.6 us (25%)
  starting transfers between devices  28.8 us (10%)
  local copies, waits for them, and re-layouts  26.5 us (9%)
  matrix products  23.2 us (8%)
  between operations  13.4 us (4%)
  other arithmetic  6.92 us (2%)
    all_gather x1, waiting for transfers between devices, local(): everything = lax.all_gather(solved_lead, 'col', axis=0, tiled=True)  78.8 us
    all_gather x1, blocking collectives, local(): own_rows = lax.all_gather(lower[0], 'row', axis=2, tiled=True)  39.7 us
    all_to_all x3, waiting for transfers between devices, local(): lax.all_to_all(copies, 'row', split_axis=2, concat_axis=2, tiled=True)  26.5 us
    all_to_all x1, blocking collectives, local(): lax.all_to_all(copies, 'row', split_axis=2, concat_axis=2, tiled=True)  25.4 us
    all_to_all x3, starting transfers between devices, local(): lax.all_to_all(copies, 'row', split_axis=2, concat_axis=2, tiled=True)  13.5 us
    dot_general x5, matrix products, times_rows(): jnp.dot(coeff, right_side, precision=highest, preferred_element_type=jnp....  13.4 us
    all_gather x1, waiting for transfers between devices, local(): gathered = lax.all_gather(lower[0], 'col', axis=0, tiled=True)  11.1 us
    all_to_all x1, blocking collectives, local(): lax.all_to_all(lead_parts, 'row', split_axis=0, concat_axis=0, tiled=True)  10.6 us
  transfers between devices with their start and end apart: 9, of which 6 were waited for; matrix products, arithmetic and copies ran while one was open for 13% of the time, Pallas kernels for 0%

profile of v15, /device:TPU:1, one launch (start us, length us, event | category | flops | bytes accessed | tf_op | source)
XLA Modules:
  0.0 300.0 jit_solution(8988438626771743240)
XLA Ops:
  6.5 0.9 slice.55
  7.5 0.6 copy.17
  8.1 0.7 slice_bitcast_fusion.4
  8.8 1.5 broadcast_in_dim.46
  10.3 6.4 %all-to-all-start = ((f32[176,2,8,128]{3,1,0,2:T(2,128)}), f32[176,2,8,128]{3,1,0,2:T(2,128)S(1)}, u32[]{:S(2)}, u32[]{:S(2)}) async-start(f32[176,2,8,128]{3,1,0,2:T(2,128)} %broadcast_in_dim.46), calls=%async_computation | async-start | bytes 2883584 | tf_op jit(solution)/shard_map/all_to_all | solution.py:41
  16.7 39.7 %all-gather.1 = f32[1,64,2,1024]{3,1,2,0:T(8,128)S(1)} all-gather(f32[1,64,2,128]{3,1,2,0:T(8,128)S(1)} %copy-done.7), channel_id=3, replica_groups=mesh['row'=8,'col'=32] {'row'}, dimensions={3}, use_global_device_ids=true | all-gather | bytes 589824 | tf_op jit(solution)/shard_map/all_gather | solution.py:50
  56.4 0.8 copy.9
  57.3 1.6 copy.39
  58.9 11.1 %all-gather.10.cloned.1.call-done = f32[1,2048,2,128]{3,1,2,0:T(8,128)} async-done(((f32[1,64,2,128]{3,1,2,0:T(8,128)}), f32[1,2048,2,128]{3,1,2,0:T(8,128)}) %all-gather.10.cloned.1.call-update) | async-done | bytes 2097168 | tf_op jit(solution)/shard_map/all_gather | solution.py:32
  70.0 1.5 convolution_bitcast_fusion
  71.5 0.7 broadcast_in_dim.51
  72.2 3.4 %all-to-all-start.3 = ((f32[64,8,128]{2,0,1:T(8,128)}), f32[64,8,128]{2,0,1:T(8,128)S(1)}, u32[]{:S(2)}, u32[]{:S(2)}) async-start(f32[64,8,128]{2,0,1:T(8,128)} %broadcast_in_dim.51), calls=%async_computation.3 | async-start | bytes 524288 | tf_op jit(solution)/shard_map/all_to_all | solution.py:56
  75.7 6.0 %all-to-all-done.3 = f32[64,8,128]{2,0,1:T(8,128)S(1)} async-done(((f32[64,8,128]{2,0,1:T(8,128)}), f32[64,8,128]{2,0,1:T(8,128)S(1)}, u32[]{:S(2)}, u32[]{:S(2)}) %all-to-all-start.3) | async-done | bytes 262176 | tf_op jit(solution)/shard_map/all_to_all | solution.py:56
  81.7 1.5 fusion.17
  83.2 0.6 pad_maximum_fusion.1
  83.9 0.4 broadcast_in_dim.50
  84.2 25.4 %all_to_all.40 = f32[176,2,8,128]{3,1,0,2:T(2,128)S(1)} all-to-all(f32[176,2,8,128]{3,1,0,2:T(2,128)S(1)} %broadcast_in_dim.50), channel_id=1, replica_groups=mesh['row'=8,'col'=32] {'row'}, dimensions={2} | all-to-all | bytes 2883584 | tf_op jit(solution)/shard_map/all_to_all | solution.py:41
  109.6 1.5 broadcast_in_dim.48
  111.1 3.6 %all-to-all-start.1 = ((f32[176,2,8,128]{3,1,0,2:T(2,128)}), f32[176,2,8,128]{3,1,0,2:T(2,128)S(1)}, u32[]{:S(2)}, u32[]{:S(2)}) async-start(f32[176,2,8,128]{3,1,0,2:T(2,128)} %broadcast_in_dim.48), calls=%async_computation.1 | async-start | bytes 2883584 | tf_op jit(solution)/shard_map/all_to_all | solution.py:41
  114.7 2.0 copy.12
  116.7 26.3 %all-to-all-done.1 = f32[176,2,8,128]{3,1,0,2:T(2,128)S(1)} async-done(((f32[176,2,8,128]{3,1,0,2:T(2,128)}), f32[176,2,8,128]{3,1,0,2:T(2,128)S(1)}, u32[]{:S(2)}, u32[]{:S(2)}) %all-to-all-start.1) | async-done | bytes 1441824 | tf_op jit(solution)/shard_map/all_to_all | solution.py:41
  143.0 0.8 copy.11
  143.9 2.9 copy_bitcast_fusion.1
  146.8 0.7 broadcast_in_dim.52
  147.5 4.0 %all-to-all-start.4 = ((f32[64,8,128]{2,0,1:T(8,128)}), f32[64,8,128]{2,0,1:T(8,128)S(1)}, u32[]{:S(2)}, u32[]{:S(2)}) async-start(f32[64,8,128]{2,0,1:T(8,128)} %broadcast_in_dim.52), calls=%async_computation.4 | async-start | bytes 524288 | tf_op jit(solution)/shard_map/all_to_all | solution.py:60
  151.5 1.1 slice_negate_fusion
  152.6 0.2 select_maximum_fusion
  153.0 1.4 slice-done
  154.5 0.6 fusion.11
  155.1 2.5 all-to-all-done.4
  157.6 1.9 fusion.9
  159.5 2.2 fusion.25
  161.6 10.6 %all_to_all.41 = f32[8,256,64]{1,2,0:T(8,128)} all-to-all(f32[8,256,64]{1,2,0:T(8,128)S(1)} %fusion.25), channel_id=1, replica_groups=mesh['row'=8,'col'=32] {'row'}, dimensions={0} | all-to-all | bytes 1048576 | tf_op jit(solution)/shard_map/all_to_all | solution.py:82
  172.2 1.5 broadcast_in_dim.55
  173.7 3.6 %all-to-all-start.7 = ((f32[176,2,8,128]{3,1,0,2:T(2,128)}), f32[176,2,8,128]{3,1,0,2:T(2,128)S(1)}, u32[]{:S(2)}, u32[]{:S(2)}) async-start(f32[176,2,8,128]{3,1,0,2:T(2,128)} %broadcast_in_dim.55), calls=%async_computation.7 | async-start | bytes 2883584 | tf_op jit(solution)/shard_map/all_to_all | solution.py:41
  177.3 2.0 slice.64
  179.3 2.6 reshape.54
  181.9 7.7 %fusion.24 = f32[8,256,704]{1,2,0:T(8,128)} fusion(f32[8,256,256]{2,1,0:T(8,128)S(1)} %bitcast.79, f32[704,256,1]{1,0,2:T(8,128)} %reshape.54), kind=kOutput, calls=%fused_computation.44 | convolution fusion | flops 4429185024 | bytes 8585216 | tf_op jit(solution)/shard_map/dot_general | solution.py:14
  189.5 1.7 reduce_sum.18
  191.4 7.8 %all-to-all-start.6 = ((f32[8,256,704]{1,2,0:T(8,128)}), f32[8,256,704]{1,2,0:T(8,128)}, u32[]{:S(2)}, u32[]{:S(2)}) async-start(f32[8,256,704]{1,2,0:T(8,128)} %fusion.24), calls=%async_computation.6 | async-start | bytes 11534336 | tf_op jit(solution)/shard_map/all_to_all | solution.py:91
  199.3 0.7 all-gather.8.cloned.1.call-update
  200.0 0.8 copy.16
  200.8 0.5 copy.38
  201.4 78.8 %all-gather.8.cloned.1.call-done = f32[2048,256]{1,0:T(8,128)} async-done(((f32[64,256]{1,0:T(8,128)}), f32[2048,256]{1,0:T(8,128)}) %all-gather.8.cloned.1.call-update) | async-done | bytes 2097168 | tf_op jit(solution)/shard_map/all_gather | solution.py:84
  280.1 8.0 %fusion = f32[704,256]{1,0:T(8,128)} fusion(f32[2048,256]{1,0:T(8,128)} %all-gather.8.cloned.1.call-done, f32[176,2048]{1,0:T(8,128)S(1)} %bitcast.91, f32[176,2048]{1,0:T(8,128)} %get-tuple-element.18, f32[176,2048]{1,0:T(8,128)} %get-tuple-element.17, f32[176,2048]{1,0:T(8,128)S(1)} %bitcast.90), kind=kOutput, calls=%fused_computation | convolution fusion | flops 4433510400 | bytes 8585216 | tf_op jit(solution)/shard_map/dot_general | solution.py:10
  288.1 3.2 %reduce_sum.19 = f32[256,704]{0,1:T(8,128)S(1)} reduce(f32[8,256,704]{1,2,0:T(8,128)} %all-to-all-done.6, f32[]{:T(128)} %constant.13.clone.1), dimensions={0}, to_apply=%region_1.2 | reduce | flops 1261568 | bytes 6488068 | tf_op jit(solution)/shard_map/reduce_sum | solution.py:92
  291.4 0.7 copy-done.8
  292.2 1.3 reshape.49
  (36 shorter events, 0.8 us)
Async XLA Ops:
  6.5 1.6 slice-start.1
  6.5 63.5 %all-gather.10.cloned.1.call-start = ((), (), s32[]{:S(2)}) async-start(), calls=%async_computation.10 | async-start | bytes 2162688 | tf_op jit(solution)/shard_map/all_gather | solution.py:32
  8.8 7.9 %copy-start.7 = (f32[1,64,2,128]{3,1,2,0:T(8,128)S(1)}, f32[1,64,2,128]{3,1,2,0:T(8,128)}, u32[]{:S(2)}) copy-start(f32[1,64,2,128]{3,1,2,0:T(8,128)} %copy.17) | copy-start | bytes 196612
  10.3 46.1 %all-to-all-start = ((f32[176,2,8,128]{3,1,0,2:T(2,128)}), f32[176,2,8,128]{3,1,0,2:T(2,128)S(1)}, u32[]{:S(2)}, u32[]{:S(2)}) async-start(f32[176,2,8,128]{3,1,0,2:T(2,128)} %broadcast_in_dim.46), calls=%async_computation | async-start | bytes 2883584 | tf_op jit(solution)/shard_map/all_to_all | solution.py:41
  56.4 13.6 %copy-start.2 = (f32[1,64,2,1024]{3,1,2,0:T(8,128)}, f32[1,64,2,1024]{3,1,2,0:T(8,128)S(1)}, u32[]{:S(2)}) copy-start(f32[1,64,2,1024]{3,1,2,0:T(8,128)S(1)} %all-gather.1) | copy-start | bytes 1572868
  57.3 18.4 %slice-start.2 = ((f32[12,64,2,128]{3,2,1,0:T(2,128)}), f32[1,64,2,128]{3,2,1,0:T(2,128)S(1)}, s32[]{:S(2)}) async-start(f32[12,64,2,128]{3,2,1,0:T(2,128)} %param.2), calls=%async_computation.13 | async-start | bytes 131072 | tf_op jit(solution)/shard_map/slice | solution.py:62
  72.2 9.5 %all-to-all-start.3 = ((f32[64,8,128]{2,0,1:T(8,128)}), f32[64,8,128]{2,0,1:T(8,128)S(1)}, u32[]{:S(2)}, u32[]{:S(2)}) async-start(f32[64,8,128]{2,0,1:T(8,128)} %broadcast_in_dim.51), calls=%async_computation.3 | async-start | bytes 524288 | tf_op jit(solution)/shard_map/all_to_all | solution.py:56
  75.7 75.9 %all-gather.6.cloned.1.call-start = ((), (), s32[]{:S(2)}) async-start(), calls=%async_computation.8 | async-start | bytes 3244032 | tf_op jit(solution)/shard_map/all_gather | solution.py:63
  111.1 31.9 %all-to-all-start.1 = ((f32[176,2,8,128]{3,1,0,2:T(2,128)}), f32[176,2,8,128]{3,1,0,2:T(2,128)S(1)}, u32[]{:S(2)}, u32[]{:S(2)}) async-start(f32[176,2,8,128]{3,1,0,2:T(2,128)} %broadcast_in_dim.48), calls=%async_computation.1 | async-start | bytes 2883584 | tf_op jit(solution)/shard_map/all_to_all | solution.py:41
  116.7 27.2 %copy-start = (f32[176,2,8,128]{3,2,1,0:T(8,128)S(1)}, f32[176,2,8,128]{3,2,1,0:T(8,128)}, u32[]{:S(2)}) copy-start(f32[176,2,8,128]{3,2,1,0:T(8,128)} %copy.12) | copy-start | bytes 4325380
  143.9 2.9 copy-start.1
  147.5 10.1 %all-to-all-start.4 = ((f32[64,8,128]{2,0,1:T(8,128)}), f32[64,8,128]{2,0,1:T(8,128)S(1)}, u32[]{:S(2)}, u32[]{:S(2)}) async-start(f32[64,8,128]{2,0,1:T(8,128)} %broadcast_in_dim.52), calls=%async_computation.4 | async-start | bytes 524288 | tf_op jit(solution)/shard_map/all_to_all | solution.py:60
  152.8 1.6 slice-start
  152.8 1.7 copy-start.3
  159.5 12.7 %copy-start.5 = (f32[176,2,128]{2,1,0:T(2,128)S(1)}, f32[176,2,128]{2,1,0:T(2,128)}, u32[]{:S(2)}) copy-start(f32[176,2,128]{2,1,0:T(2,128)} %get-tuple-element.21) | copy-start | bytes 540676
  173.7 17.7 %all-to-all-start.7 = ((f32[176,2,8,128]{3,1,0,2:T(2,128)}), f32[176,2,8,128]{3,1,0,2:T(2,128)S(1)}, u32[]{:S(2)}, u32[]{:S(2)}) async-start(f32[176,2,8,128]{3,1,0,2:T(2,128)} %broadcast_in_dim.55), calls=%async_computation.7 | async-start | bytes 2883584 | tf_op jit(solution)/shard_map/all_to_all | solution.py:41
  191.4 96.7 %all-to-all-start.6 = ((f32[8,256,704]{1,2,0:T(8,128)}), f32[8,256,704]{1,2,0:T(8,128)}, u32[]{:S(2)}, u32[]{:S(2)}) async-start(f32[8,256,704]{1,2,0:T(8,128)} %fusion.24), calls=%async_computation.6 | async-start | bytes 11534336 | tf_op jit(solution)/shard_map/all_to_all | solution.py:91
  199.2 80.9 %all-gather.8.cloned.1.call-start = ((), (), s32[]{:S(2)}) async-start(), calls=%async_computation.9 | async-start | bytes 2162688 | tf_op jit(solution)/shard_map/all_gather | solution.py:84
  200.8 79.3 %copy-start.4 = (f32[22,8,16,128]{3,1,2,0:T(8,128)S(1)}, f32[22,8,16,128]{3,1,2,0:T(8,128)}, u32[]{:S(2)}) copy-start(f32[22,8,16,128]{3,1,2,0:T(8,128)} %copy.39) | copy-start | bytes 4325380
  288.1 3.2 %copy-start.6 = (f32[704,256]{1,0:T(8,128)S(1)}, f32[704,256]{1,0:T(8,128)}, u32[]{:S(2)}) copy-start(f32[704,256]{1,0:T(8,128)} %fusion) | copy-start | bytes 2162692
  291.3 0.8 copy-start.8
Sparse Core Ops, SparseCore 0:
  10.0 60.0 all-gather.9
  84.0 58.9 all-gather.5
  202.6 77.4 all-gather.7

commit v16 on v15

--- a/solution.py
+++ b/solution.py
@@ -59,9 +59,10 @@
     chained_copies = jnp.broadcast_to(chained_piece[:, None, :], (strip_width, row_count, row_run))
     chained = lax.all_to_all(chained_copies, "row", split_axis=1, concat_axis=1, tiled=True)
     chained = chained.reshape(strip_width, block_size)
+    left_chunks[1], chained = lax.optimization_barrier((left_chunks[1], chained))
     joined = jnp.concatenate([strip[0].reshape(strip_width, 2 * row_run), chained_piece], axis=1)
     joined = lax.all_gather(joined, "col", axis=0, tiled=True)
-    left_chunks[1:3], joined = lax.optimization_barrier((left_chunks[1:3], joined))
+    left_chunks[2:], joined = lax.optimization_barrier((left_chunks[2:], joined))
     strip_lead = joined[:, : 2 * row_run]
     chained_cols = joined[block_size:, 2 * row_run :]
 

time: 301 us -> 288 us (0.957); the launches traced: 300 us -> 283 us
  blocking collectives: 75.6 us -> 49 us
  starting transfers between devices: 28.8 us -> 33.4 us
    all_to_all x3 -> x4, waiting for transfers between devices: 26.5 us -> 56.7 us  [local(): lax.all_to_all(copies, 'row', split_axis=2, concat_axis=2, tiled=True)]
    all_to_all x2 -> x1, blocking collectives: 35.9 us -> 9.33 us  [local(): lax.all_to_all(cross_copies, 'row', split_axis=1, concat_axis=1, tiled=True)]
    all_gather x1, waiting for transfers between devices: 78.8 us -> 61 us  [local(): everything = lax.all_gather(solved_lead, 'col', axis=0, tiled=True)]
    all_to_all x1, waiting for transfers between devices: 5.99 us -> 0.06 us  [local(): lax.all_to_all(lead_parts, 'row', split_axis=0, concat_axis=0, tiled=True)]
    all_to_all x3 -> x4, starting transfers between devices: 13.5 us -> 18.2 us  [local(): lax.all_to_all(copies, 'row', split_axis=2, concat_axis=2, tiled=True)]
    slice x2 -> x3, local copies, waits for them, and re-layouts: 4.62 us -> 0.59 us  [local(): trail_parts = times_rows_turned(inverse_cols, strip_rows[strip_width:])]
  transfers between devices with their start and end apart: 9 -> 10, of which waited for: 6 -> 6; matrix products, arithmetic and copies ran while one was open for 13% -> 13% of each run, Pallas kernels for 0% -> 0%
where the time goes in v16:
time: 288 us; the launch traced here: 283 us
  waiting for transfers between devices  129 us (45%)
  blocking collectives  49 us (17%)
  starting transfers between devices  33.4 us (12%)
  local copies, waits for them, and re-layouts  29.1 us (10%)
  matrix products  22.2 us (8%)
  between operations  13.3 us (5%)
  other arithmetic  6.94 us (2%)
    all_gather x1, waiting for transfers between devices, local(): everything = lax.all_gather(solved_lead, 'col', axis=0, tiled=True)  61 us
    all_to_all x4, waiting for transfers between devices, local(): lax.all_to_all(copies, 'row', split_axis=2, concat_axis=2, tiled=True)  56.7 us
    all_gather x1, blocking collectives, local(): own_rows = lax.all_gather(lower[0], 'row', axis=2, tiled=True)  39.7 us
    all_to_all x4, starting transfers between devices, local(): lax.all_to_all(copies, 'row', split_axis=2, concat_axis=2, tiled=True)  18.2 us
    dot_general x5, matrix products, times_rows(): jnp.dot(coeff, right_side, precision=highest, preferred_element_type=jnp....  12.7 us
    all_gather x1, waiting for transfers between devices, local(): gathered = lax.all_gather(lower[0], 'col', axis=0, tiled=True)  11.1 us
    dot_general x2, matrix products, times_rows_turned(): lax.dot_general(coeff, right_turned, (((1,), (1,)), ((), ())), precision=...  9.53 us
    all_to_all x1, blocking collectives, local(): lax.all_to_all(cross_copies, 'row', split_axis=1, concat_axis=1, tiled=True)  9.33 us
  transfers between devices with their start and end apart: 10, of which 6 were waited for; matrix products, arithmetic and copies ran while one was open for 13% of the time, Pallas kernels for 0%

profile of v16, /device:TPU:1, one launch (start us, length us, event | category | flops | bytes accessed | tf_op | source)
XLA Modules:
  0.0 283.4 jit_solution(14516827210014265808)
XLA Ops:
  6.5 0.9 slice.55
  7.5 0.6 copy.17
  8.1 0.7 slice_bitcast_fusion.4
  8.8 1.5 broadcast_in_dim.46
  10.3 6.4 %all-to-all-start = ((f32[176,2,8,128]{3,1,0,2:T(2,128)}), f32[176,2,8,128]{3,1,0,2:T(2,128)S(1)}, u32[]{:S(2)}, u32[]{:S(2)}) async-start(f32[176,2,8,128]{3,1,0,2:T(2,128)} %broadcast_in_dim.46), calls=%async_computation | async-start | bytes 2883584 | tf_op jit(solution)/shard_map/all_to_all | solution.py:41
  16.7 39.7 %all-gather.1 = f32[1,64,2,1024]{3,1,2,0:T(8,128)S(1)} all-gather(f32[1,64,2,128]{3,1,2,0:T(8,128)S(1)} %copy-done.6), channel_id=3, replica_groups=mesh['row'=8,'col'=32] {'row'}, dimensions={3}, use_global_device_ids=true | all-gather | bytes 589824 | tf_op jit(solution)/shard_map/all_gather | solution.py:50
  56.4 0.8 copy.9
  57.3 1.6 copy.36
  58.9 11.1 %all-gather.10.cloned.1.call-done = f32[1,2048,2,128]{3,1,2,0:T(8,128)} async-done(((f32[1,64,2,128]{3,1,2,0:T(8,128)}), f32[1,2048,2,128]{3,1,2,0:T(8,128)}) %all-gather.10.cloned.1.call-update) | async-done | bytes 2097168 | tf_op jit(solution)/shard_map/all_gather | solution.py:32
  70.0 1.5 convolution_bitcast_fusion
  71.5 9.3 %all_to_all.40 = f32[64,8,128]{2,0,1:T(8,128)S(1)} all-to-all(f32[64,8,128]{2,0,1:T(8,128)S(1)} %broadcast_in_dim.51), channel_id=1, replica_groups=mesh['row'=8,'col'=32] {'row'}, dimensions={1} | all-to-all | bytes 524288 | tf_op jit(solution)/shard_map/all_to_all | solution.py:56
  80.8 1.5 broadcast_in_dim.50
  82.3 3.8 %all-to-all-start.2 = ((f32[176,2,8,128]{3,1,0,2:T(2,128)}), f32[176,2,8,128]{3,1,0,2:T(2,128)S(1)}, u32[]{:S(2)}, u32[]{:S(2)}) async-start(f32[176,2,8,128]{3,1,0,2:T(2,128)} %broadcast_in_dim.50), calls=%async_computation.2 | async-start | bytes 2883584 | tf_op jit(solution)/shard_map/all_to_all | solution.py:41
  86.1 1.5 fusion.15
  87.6 17.6 %all-to-all-done.2 = f32[176,2,8,128]{3,1,0,2:T(2,128)S(1)} async-done(((f32[176,2,8,128]{3,1,0,2:T(2,128)}), f32[176,2,8,128]{3,1,0,2:T(2,128)S(1)}, u32[]{:S(2)}, u32[]{:S(2)}) %all-to-all-start.2) | async-done | bytes 1441824 | tf_op jit(solution)/shard_map/all_to_all | solution.py:41
  105.2 1.5 broadcast_in_dim.48
  106.8 3.7 %all-to-all-start.1 = ((f32[176,2,8,128]{3,1,0,2:T(2,128)}), f32[176,2,8,128]{3,1,0,2:T(2,128)S(1)}, u32[]{:S(2)}, u32[]{:S(2)}) async-start(f32[176,2,8,128]{3,1,0,2:T(2,128)} %broadcast_in_dim.48), calls=%async_computation.1 | async-start | bytes 2883584 | tf_op jit(solution)/shard_map/all_to_all | solution.py:41
  110.5 0.6 pad_maximum_fusion.1
  111.2 18.4 %all-to-all-done.1 = f32[176,2,8,128]{3,1,0,2:T(2,128)S(1)} async-done(((f32[176,2,8,128]{3,1,0,2:T(2,128)}), f32[176,2,8,128]{3,1,0,2:T(2,128)S(1)}, u32[]{:S(2)}, u32[]{:S(2)}) %all-to-all-start.1) | async-done | bytes 1441824 | tf_op jit(solution)/shard_map/all_to_all | solution.py:41
  129.6 2.4 broadcast_in_dim.53
  132.1 4.3 %all-to-all-start.4 = ((f32[176,2,8,128]{3,1,0,2:T(2,128)}), f32[176,2,8,128]{3,1,0,2:T(2,128)}, u32[]{:S(2)}, u32[]{:S(2)}) async-start(f32[176,2,8,128]{3,1,0,2:T(2,128)} %broadcast_in_dim.53), calls=%async_computation.4 | async-start | bytes 2883584 | tf_op jit(solution)/shard_map/all_to_all | solution.py:41
  136.4 1.9 copy.12
  138.3 2.0 copy.11
  140.3 20.6 %all-to-all-done.4 = f32[176,2,8,128]{3,1,0,2:T(2,128)} async-done(((f32[176,2,8,128]{3,1,0,2:T(2,128)}), f32[176,2,8,128]{3,1,0,2:T(2,128)}, u32[]{:S(2)}, u32[]{:S(2)}) %all-to-all-start.4) | async-done | bytes 1441824 | tf_op jit(solution)/shard_map/all_to_all | solution.py:41
  161.0 0.7 broadcast_in_dim.54
  161.7 4.5 %all-to-all-start.5 = ((f32[64,8,128]{2,0,1:T(8,128)}), f32[64,8,128]{2,0,1:T(8,128)S(1)}, u32[]{:S(2)}, u32[]{:S(2)}) async-start(f32[64,8,128]{2,0,1:T(8,128)} %broadcast_in_dim.54), calls=%async_computation.5 | async-start | bytes 524288 | tf_op jit(solution)/shard_map/all_to_all | solution.py:60
  166.2 4.2 %copy_bitcast_fusion.1 = (f32[176,2048]{1,0:T(8,128)}, f32[176,2048]{1,0:T(8,128)}) fusion(f32[22,8,16,128]{3,2,1,0:T(8,128)S(1)} %bitcast.82, f32[22,8,16,128]{3,2,1,0:T(8,128)} %bitcast.83), kind=kLoop, calls=%fused_computation.11 | loop fusion | bytes 5767168 | tf_op jit(solution)/shard_map/reshape | solution.py:42
  170.4 2.2 copy.15
  172.6 1.7 copy.35
  174.5 1.1 slice_negate_fusion
  175.6 0.2 select_maximum_fusion
  176.0 1.4 slice-done
  177.4 0.6 fusion.11
  178.0 0.3 copy-done.1
  178.3 0.6 fusion.9
  179.0 3.0 %fusion.23 = f32[8,256,64]{1,2,0:T(8,128)} fusion(f32[8,256,256]{2,1,0:T(8,128)S(1)} %bitcast.77, f32[64,256,1]{1,0,2:T(8,128)S(1)} %fusion.9), kind=kOutput, calls=%fused_computation.44 | convolution fusion | flops 402653184 | bytes 2686976 | tf_op jit(solution)/shard_map/dot_general | solution.py:14
  181.9 5.1 %all-to-all-start.6 = ((f32[8,256,64]{1,2,0:T(8,128)}), f32[8,256,64]{1,2,0:T(8,128)}, u32[]{:S(2)}, u32[]{:S(2)}) async-start(f32[8,256,64]{1,2,0:T(8,128)} %fusion.23), calls=%async_computation.6 | async-start | bytes 1048576 | tf_op jit(solution)/shard_map/all_to_all | solution.py:83
  187.1 0.6 reshape.54
  187.7 6.6 %fusion.22 = f32[8,256,704]{1,2,0:T(8,128)} fusion(f32[8,256,256]{2,1,0:T(8,128)S(1)} %bitcast.78, f32[704,256,1]{1,0,2:T(8,128)S(1)} %reshape.54), kind=kOutput, calls=%fused_computation.43 | convolution fusion | flops 4429185024 | bytes 8585216 | tf_op jit(solution)/shard_map/dot_general | solution.py:14
  194.3 1.7 reduce_sum.18
  196.0 5.3 %all-to-all-start.7 = ((f32[8,256,704]{1,2,0:T(8,128)}), f32[8,256,704]{1,2,0:T(8,128)}, u32[]{:S(2)}, u32[]{:S(2)}) async-start(f32[8,256,704]{1,2,0:T(8,128)} %fusion.22), calls=%async_computation.7 | async-start | bytes 11534336 | tf_op jit(solution)/shard_map/all_to_all | solution.py:92
  201.4 0.3 all-gather.8.cloned.1.call-start
  201.6 0.5 all-gather.8.cloned.1.call-update
  202.1 61.0 %all-gather.8.cloned.1.call-done = f32[2048,256]{1,0:T(8,128)} async-done(((f32[64,256]{1,0:T(8,128)}), f32[2048,256]{1,0:T(8,128)}) %all-gather.8.cloned.1.call-update) | async-done | bytes 2097168 | tf_op jit(solution)/shard_map/all_gather | solution.py:85
  263.1 8.5 %fusion = f32[704,256]{1,0:T(8,128)} fusion(f32[2048,256]{1,0:T(8,128)} %all-gather.8.cloned.1.call-done, f32[176,2048]{1,0:T(8,128)} %get-tuple-element.22, f32[176,2048]{1,0:T(8,128)} %get-tuple-element.21, f32[176,2048]{1,0:T(8,128)S(1)} %bitcast.91, f32[176,2048]{1,0:T(8,128)S(1)} %bitcast.90), kind=kOutput, calls=%fused_computation | convolution fusion | flops 4433510400 | bytes 8585216 | tf_op jit(solution)/shard_map/dot_general | solution.py:10
  271.5 3.2 %reduce_sum.19 = f32[256,704]{0,1:T(8,128)S(1)} reduce(f32[8,256,704]{1,2,0:T(8,128)} %all-to-all-done.7, f32[]{:T(128)} %constant.13.clone.1), dimensions={0}, to_apply=%region_1.2 | reduce | flops 1261568 | bytes 6488068 | tf_op jit(solution)/shard_map/reduce_sum | solution.py:93
  274.8 0.7 copy-done.7
  275.6 1.3 reshape.49
  (37 shorter events, 0.7 us)
Async XLA Ops:
  6.5 1.6 slice-start.1
  6.5 63.5 %all-gather.10.cloned.1.call-start = ((), (), s32[]{:S(2)}) async-start(), calls=%async_computation.10 | async-start | bytes 2162688 | tf_op jit(solution)/shard_map/all_gather | solution.py:32
  8.8 7.9 %copy-start.6 = (f32[1,64,2,128]{3,1,2,0:T(8,128)S(1)}, f32[1,64,2,128]{3,1,2,0:T(8,128)}, u32[]{:S(2)}) copy-start(f32[1,64,2,128]{3,1,2,0:T(8,128)} %copy.17) | copy-start | bytes 196612
  10.3 46.1 %all-to-all-start = ((f32[176,2,8,128]{3,1,0,2:T(2,128)}), f32[176,2,8,128]{3,1,0,2:T(2,128)S(1)}, u32[]{:S(2)}, u32[]{:S(2)}) async-start(f32[176,2,8,128]{3,1,0,2:T(2,128)} %broadcast_in_dim.46), calls=%async_computation | async-start | bytes 2883584 | tf_op jit(solution)/shard_map/all_to_all | solution.py:41
  80.8 5.3 %slice-start.2 = ((f32[12,64,2,128]{3,2,1,0:T(2,128)}), f32[1,64,2,128]{3,2,1,0:T(2,128)S(1)}, s32[]{:S(2)}) async-start(f32[12,64,2,128]{3,2,1,0:T(2,128)} %param.2), calls=%async_computation.13 | async-start | bytes 131072 | tf_op jit(solution)/shard_map/slice | solution.py:63
  82.3 22.9 %all-to-all-start.2 = ((f32[176,2,8,128]{3,1,0,2:T(2,128)}), f32[176,2,8,128]{3,1,0,2:T(2,128)S(1)}, u32[]{:S(2)}, u32[]{:S(2)}) async-start(f32[176,2,8,128]{3,1,0,2:T(2,128)} %broadcast_in_dim.50), calls=%async_computation.2 | async-start | bytes 2883584 | tf_op jit(solution)/shard_map/all_to_all | solution.py:41
  106.8 22.9 %all-to-all-start.1 = ((f32[176,2,8,128]{3,1,0,2:T(2,128)}), f32[176,2,8,128]{3,1,0,2:T(2,128)S(1)}, u32[]{:S(2)}, u32[]{:S(2)}) async-start(f32[176,2,8,128]{3,1,0,2:T(2,128)} %broadcast_in_dim.48), calls=%async_computation.1 | async-start | bytes 2883584 | tf_op jit(solution)/shard_map/all_to_all | solution.py:41
  110.5 64.0 %all-gather.6.cloned.1.call-start = ((), (), s32[]{:S(2)}) async-start(), calls=%async_computation.8 | async-start | bytes 3244032 | tf_op jit(solution)/shard_map/all_gather | solution.py:64
  132.1 28.9 %all-to-all-start.4 = ((f32[176,2,8,128]{3,1,0,2:T(2,128)}), f32[176,2,8,128]{3,1,0,2:T(2,128)}, u32[]{:S(2)}, u32[]{:S(2)}) async-start(f32[176,2,8,128]{3,1,0,2:T(2,128)} %broadcast_in_dim.53), calls=%async_computation.4 | async-start | bytes 2883584 | tf_op jit(solution)/shard_map/all_to_all | solution.py:41
  138.3 27.9 %copy-start = (f32[176,2,8,128]{3,2,1,0:T(8,128)S(1)}, f32[176,2,8,128]{3,2,1,0:T(8,128)}, u32[]{:S(2)}) copy-start(f32[176,2,8,128]{3,2,1,0:T(8,128)} %copy.12) | copy-start | bytes 4325380
  161.7 12.8 %all-to-all-start.5 = ((f32[64,8,128]{2,0,1:T(8,128)}), f32[64,8,128]{2,0,1:T(8,128)S(1)}, u32[]{:S(2)}, u32[]{:S(2)}) async-start(f32[64,8,128]{2,0,1:T(8,128)} %broadcast_in_dim.54), calls=%async_computation.5 | async-start | bytes 524288 | tf_op jit(solution)/shard_map/all_to_all | solution.py:60
  172.6 1.8 copy-start.2
  175.8 1.6 slice-start
  175.8 2.5 copy-start.1
  179.0 8.1 %slice-start.3 = ((f32[12,64,2,128]{3,2,1,0:T(2,128)}), f32[11,64,2,128]{3,2,1,0:T(2,128)S(1)}, s32[]{:S(2)}) async-start(f32[12,64,2,128]{3,2,1,0:T(2,128)} %param.2), calls=%async_computation.14 | async-start | bytes 1441792 | tf_op jit(solution)/shard_map/slice | solution.py:89
  181.9 12.4 %all-to-all-start.6 = ((f32[8,256,64]{1,2,0:T(8,128)}), f32[8,256,64]{1,2,0:T(8,128)}, u32[]{:S(2)}, u32[]{:S(2)}) async-start(f32[8,256,64]{1,2,0:T(8,128)} %fusion.23), calls=%async_computation.6 | async-start | bytes 1048576 | tf_op jit(solution)/shard_map/all_to_all | solution.py:83
  196.0 67.0 %copy-start.3 = (f32[22,8,16,128]{3,1,2,0:T(8,128)S(1)}, f32[22,8,16,128]{3,1,2,0:T(8,128)}, u32[]{:S(2)}) copy-start(f32[22,8,16,128]{3,1,2,0:T(8,128)} %copy.36) | copy-start | bytes 4325380
  196.0 67.0 %copy-start.4 = (f32[22,8,16,128]{3,1,2,0:T(8,128)S(1)}, f32[22,8,16,128]{3,1,2,0:T(8,128)}, u32[]{:S(2)}) copy-start(f32[22,8,16,128]{3,1,2,0:T(8,128)} %copy.35) | copy-start | bytes 4325380
  196.0 75.5 %all-to-all-start.7 = ((f32[8,256,704]{1,2,0:T(8,128)}), f32[8,256,704]{1,2,0:T(8,128)}, u32[]{:S(2)}, u32[]{:S(2)}) async-start(f32[8,256,704]{1,2,0:T(8,128)} %fusion.22), calls=%async_computation.7 | async-start | bytes 11534336 | tf_op jit(solution)/shard_map/all_to_all | solution.py:92
  201.4 61.7 %all-gather.8.cloned.1.call-start = ((), (), s32[]{:S(2)}) async-start(), calls=%async_computation.9 | async-start | bytes 2162688 | tf_op jit(solution)/shard_map/all_gather | solution.py:85
  271.5 3.2 %copy-start.5 = (f32[704,256]{1,0:T(8,128)S(1)}, f32[704,256]{1,0:T(8,128)}, u32[]{:S(2)}) copy-start(f32[704,256]{1,0:T(8,128)} %fusion) | copy-start | bytes 2162692
  274.7 0.8 copy-start.7
Sparse Core Ops, SparseCore 0:
  10.0 59.9 all-gather.9
  113.9 56.8 all-gather.5
  204.8 58.2 all-gather.7

commit v17 on v14

--- a/solution.py
+++ b/solution.py
@@ -84,7 +84,10 @@
     everything = lax.all_gather(solved_lead, "col", axis=0, tiled=True)
 
     full_left = jnp.concatenate(left_chunks, axis=0)
-    left_update = lax.optimization_barrier(times_rows(full_left, everything))
+    left_update = jnp.dot(
+        full_left, everything, precision=lax.Precision.HIGH, preferred_element_type=jnp.float32
+    )
+    left_update = lax.optimization_barrier(left_update)
     trail_parts = times_rows_turned(inverse_cols, strip_rows[strip_width:])
     trail_parts = trail_parts.reshape(row_count, 2 * row_run, trail_count)
     trail_parts, solved_lead = lax.optimization_barrier((trail_parts, solved_lead))

time: 282 us -> 282 us (level)
  waiting for transfers between devices: 113 us -> 116 us
    dot_general x5 -> x4, matrix products: 13.9 us -> 5.45 us  [times_rows(): jnp.dot(coeff, right_side, precision=highest, preferred_element_type=jnp....]
    dot_general x0 -> x1, matrix products: none -> 5.75 us  [local(): jnp.dot(full_left, everything, precision=lax.Precision.HIGH, preferred_el...]
  transfers between devices with their start and end apart: 9 -> 9, of which waited for: 6 -> 6; matrix products, arithmetic and copies ran while one was open for 12% -> 11% of each run, Pallas kernels for 0% -> 0%
where the time goes in v17:
time: 282 us; the launch traced here: 278 us
  waiting for transfers between devices  116 us (41%)
  blocking collectives  71.8 us (25%)
  starting transfers between devices  28.5 us (10%)
  local copies, waits for them, and re-layouts  21 us (7%)
  matrix products  20.7 us (7%)
  between operations  13.4 us (5%)
  other arithmetic  6.87 us (2%)
    all_gather x1, waiting for transfers between devices, local(): everything = lax.all_gather(solved_lead, 'col', axis=0, tiled=True)  61.8 us
    all_gather x1, blocking collectives, local(): own_rows = lax.all_gather(lower[0], 'row', axis=2, tiled=True)  39 us
    all_to_all x3, waiting for transfers between devices, local(): lax.all_to_all(copies, 'row', split_axis=2, concat_axis=2, tiled=True)  34.9 us
    all_to_all x1, blocking collectives, local(): lax.all_to_all(copies, 'row', split_axis=2, concat_axis=2, tiled=True)  23.8 us
    all_to_all x3, starting transfers between devices, local(): lax.all_to_all(copies, 'row', split_axis=2, concat_axis=2, tiled=True)  13.7 us
    all_gather x1, waiting for transfers between devices, local(): gathered = lax.all_gather(lower[0], 'col', axis=0, tiled=True)  12.4 us
    dot_general x2, matrix products, times_rows_turned(): lax.dot_general(coeff, right_turned, (((1,), (1,)), ((), ())), precision=...  9.53 us
    all_to_all x1, blocking collectives, local(): lax.all_to_all(cross_copies, 'row', split_axis=1, concat_axis=1, tiled=True)  9.05 us
  transfers between devices with their start and end apart: 9, of which 6 were waited for; matrix products, arithmetic and copies ran while one was open for 11% of the time, Pallas kernels for 0%

profile of v17, /device:TPU:1, one launch (start us, length us, event | category | flops | bytes accessed | tf_op | source)
XLA Modules:
  0.0 277.8 jit_solution(10926732874889420538)
XLA Ops:
  6.5 0.9 slice.55
  7.5 0.6 copy.17
  8.2 1.5 broadcast_in_dim.46
  9.7 6.4 %all-to-all-start = ((f32[176,2,8,128]{3,1,0,2:T(2,128)}), f32[176,2,8,128]{3,1,0,2:T(2,128)S(1)}, u32[]{:S(2)}, u32[]{:S(2)}) async-start(f32[176,2,8,128]{3,1,0,2:T(2,128)} %broadcast_in_dim.46), calls=%async_computation | async-start | bytes 2883584 | tf_op jit(solution)/shard_map/all_to_all | solution.py:41
  16.1 39.0 %all-gather.1 = f32[1,64,2,1024]{3,1,2,0:T(8,128)S(1)} all-gather(f32[1,64,2,128]{3,1,2,0:T(8,128)S(1)} %copy-done.5), channel_id=3, replica_groups=mesh['row'=8,'col'=32] {'row'}, dimensions={3}, use_global_device_ids=true | all-gather | bytes 589824 | tf_op jit(solution)/shard_map/all_gather | solution.py:50
  55.1 0.8 copy.9
  55.9 1.6 copy.39
  57.6 12.4 %all-gather.10.cloned.1.call-done = f32[1,2048,2,128]{3,1,2,0:T(8,128)} async-done(((f32[1,64,2,128]{3,1,2,0:T(8,128)}), f32[1,2048,2,128]{3,1,2,0:T(8,128)}) %all-gather.10.cloned.1.call-update) | async-done | bytes 2097168 | tf_op jit(solution)/shard_map/all_gather | solution.py:32
  69.9 1.5 convolution_bitcast_fusion
  71.5 9.0 %all_to_all.40 = f32[64,8,128]{2,0,1:T(8,128)S(1)} all-to-all(f32[64,8,128]{2,0,1:T(8,128)S(1)} %broadcast_in_dim.53), channel_id=1, replica_groups=mesh['row'=8,'col'=32] {'row'}, dimensions={1} | all-to-all | bytes 524288 | tf_op jit(solution)/shard_map/all_to_all | solution.py:56
  80.5 1.5 broadcast_in_dim.48
  82.0 3.8 %all-to-all-start.1 = ((f32[176,2,8,128]{3,1,0,2:T(2,128)}), f32[176,2,8,128]{3,1,0,2:T(2,128)S(1)}, u32[]{:S(2)}, u32[]{:S(2)}) async-start(f32[176,2,8,128]{3,1,0,2:T(2,128)} %broadcast_in_dim.48), calls=%async_computation.1 | async-start | bytes 2883584 | tf_op jit(solution)/shard_map/all_to_all | solution.py:41
  85.9 1.5 fusion.17
  87.3 0.6 pad_maximum_fusion.1
  88.0 16.9 %all-to-all-done.1 = f32[176,2,8,128]{3,1,0,2:T(2,128)S(1)} async-done(((f32[176,2,8,128]{3,1,0,2:T(2,128)}), f32[176,2,8,128]{3,1,0,2:T(2,128)S(1)}, u32[]{:S(2)}, u32[]{:S(2)}) %all-to-all-start.1) | async-done | bytes 1441824 | tf_op jit(solution)/shard_map/all_to_all | solution.py:41
  104.9 0.4 broadcast_in_dim.52
  105.3 23.8 %all_to_all.41 = f32[176,2,8,128]{3,1,0,2:T(2,128)} all-to-all(f32[176,2,8,128]{3,1,0,2:T(2,128)S(1)} %broadcast_in_dim.52), channel_id=1, replica_groups=mesh['row'=8,'col'=32] {'row'}, dimensions={2} | all-to-all | bytes 2883584 | tf_op jit(solution)/shard_map/all_to_all | solution.py:41
  129.1 1.5 broadcast_in_dim.50
  130.6 3.6 %all-to-all-start.2 = ((f32[176,2,8,128]{3,1,0,2:T(2,128)}), f32[176,2,8,128]{3,1,0,2:T(2,128)S(1)}, u32[]{:S(2)}, u32[]{:S(2)}) async-start(f32[176,2,8,128]{3,1,0,2:T(2,128)} %broadcast_in_dim.50), calls=%async_computation.2 | async-start | bytes 2883584 | tf_op jit(solution)/shard_map/all_to_all | solution.py:41
  134.2 0.8 copy.11
  135.1 1.6 copy.38
  136.7 0.8 copy.13
  137.5 18.0 %all-to-all-done.2 = f32[176,2,8,128]{3,1,0,2:T(2,128)S(1)} async-done(((f32[176,2,8,128]{3,1,0,2:T(2,128)}), f32[176,2,8,128]{3,1,0,2:T(2,128)S(1)}, u32[]{:S(2)}, u32[]{:S(2)}) %all-to-all-start.2) | async-done | bytes 1441824 | tf_op jit(solution)/shard_map/all_to_all | solution.py:41
  155.5 0.8 copy.12
  156.4 2.9 %copy_bitcast_fusion = (f32[176,2048]{1,0:T(8,128)}, f32[176,2048]{1,0:T(8,128)}) fusion(f32[22,8,16,128]{3,2,1,0:T(8,128)S(1)} %bitcast.83, f32[22,8,16,128]{3,2,1,0:T(8,128)S(1)} %bitcast.84), kind=kLoop, calls=%fused_computation.10 | loop fusion | bytes 5767168 | tf_op jit(solution)/shard_map/reshape | solution.py:42
  159.3 0.7 broadcast_in_dim.54
  160.0 5.2 %all-to-all-start.5 = ((f32[64,8,128]{2,0,1:T(8,128)}), f32[64,8,128]{2,0,1:T(8,128)S(1)}, u32[]{:S(2)}, u32[]{:S(2)}) async-start(f32[64,8,128]{2,0,1:T(8,128)} %broadcast_in_dim.54), calls=%async_computation.5 | async-start | bytes 524288 | tf_op jit(solution)/shard_map/all_to_all | solution.py:60
  165.3 1.1 slice_negate_fusion
  166.4 0.2 select_maximum_fusion
  166.6 0.1 copy.15
  166.8 1.4 slice-done
  168.2 0.6 fusion.11
  168.8 2.5 all-to-all-done.5
  171.4 1.9 fusion.9
  173.2 3.0 %fusion.25 = f32[8,256,64]{1,2,0:T(8,128)} fusion(f32[8,256,256]{2,1,0:T(8,128)S(1)} %bitcast.78, f32[64,256,1]{1,0,2:T(8,128)S(1)} %fusion.9), kind=kOutput, calls=%fused_computation.45 | convolution fusion | flops 402653184 | bytes 2686976 | tf_op jit(solution)/shard_map/dot_general | solution.py:14
  176.2 4.1 %all-to-all-start.6 = ((f32[8,256,64]{1,2,0:T(8,128)}), f32[8,256,64]{1,2,0:T(8,128)}, u32[]{:S(2)}, u32[]{:S(2)}) async-start(f32[8,256,64]{1,2,0:T(8,128)} %fusion.25), calls=%async_computation.6 | async-start | bytes 1048576 | tf_op jit(solution)/shard_map/all_to_all | solution.py:82
  180.4 0.6 reshape.54
  180.9 6.6 %fusion.24 = f32[8,256,704]{1,2,0:T(8,128)} fusion(f32[8,256,256]{2,1,0:T(8,128)S(1)} %bitcast.79, f32[704,256,1]{1,0,2:T(8,128)S(1)} %reshape.54), kind=kOutput, calls=%fused_computation.44 | convolution fusion | flops 4429185024 | bytes 8585216 | tf_op jit(solution)/shard_map/dot_general | solution.py:14
  187.5 1.7 reduce_sum.18
  189.2 5.3 %all-to-all-start.7 = ((f32[8,256,704]{1,2,0:T(8,128)}), f32[8,256,704]{1,2,0:T(8,128)}, u32[]{:S(2)}, u32[]{:S(2)}) async-start(f32[8,256,704]{1,2,0:T(8,128)} %fusion.24), calls=%async_computation.7 | async-start | bytes 11534336 | tf_op jit(solution)/shard_map/all_to_all | solution.py:94
  194.6 0.7 all-gather.8.cloned.1.call-update
  195.3 61.8 %all-gather.8.cloned.1.call-done = f32[2048,256]{1,0:T(8,128)} async-done(((f32[64,256]{1,0:T(8,128)}), f32[2048,256]{1,0:T(8,128)}) %all-gather.8.cloned.1.call-update) | async-done | bytes 2097168 | tf_op jit(solution)/shard_map/all_gather | solution.py:84
  257.1 5.8 %fusion = f32[704,256]{1,0:T(8,128)} fusion(f32[2048,256]{1,0:T(8,128)} %all-gather.8.cloned.1.call-done, f32[176,2048]{1,0:T(8,128)} %get-tuple-element.20, f32[176,2048]{1,0:T(8,128)} %get-tuple-element.19, f32[176,2048]{1,0:T(8,128)S(1)} %bitcast.92, f32[176,2048]{1,0:T(8,128)S(1)} %bitcast.91), kind=kOutput, calls=%fused_computation | convolution fusion | flops 2218917888 | bytes 8585216 | tf_op jit(solution)/shard_map/dot_general | solution.py:87
  262.8 3.2 %all-to-all-done.7 = f32[8,256,704]{1,2,0:T(8,128)} async-done(((f32[8,256,704]{1,2,0:T(8,128)}), f32[8,256,704]{1,2,0:T(8,128)}, u32[]{:S(2)}, u32[]{:S(2)}) %all-to-all-start.7) | async-done | bytes 5767200 | tf_op jit(solution)/shard_map/all_to_all | solution.py:94
  266.0 3.1 %reduce_sum.19 = f32[256,704]{0,1:T(8,128)S(1)} reduce(f32[8,256,704]{1,2,0:T(8,128)} %all-to-all-done.7, f32[]{:T(128)} %constant.13.clone.1), dimensions={0}, to_apply=%region_1.2 | reduce | flops 1261568 | bytes 6488068 | tf_op jit(solution)/shard_map/reduce_sum | solution.py:95
  269.2 0.1 bitcast_subtract_fusion
  269.3 0.7 copy-done.6
  270.1 1.3 reshape.49
  (33 shorter events, 0.4 us)
Async XLA Ops:
  6.5 1.6 slice-start.1
  6.5 63.4 %all-gather.10.cloned.1.call-start = ((), (), s32[]{:S(2)}) async-start(), calls=%async_computation.10 | async-start | bytes 2162688 | tf_op jit(solution)/shard_map/all_gather | solution.py:32
  8.2 7.9 %copy-start.5 = (f32[1,64,2,128]{3,1,2,0:T(8,128)S(1)}, f32[1,64,2,128]{3,1,2,0:T(8,128)}, u32[]{:S(2)}) copy-start(f32[1,64,2,128]{3,1,2,0:T(8,128)} %copy.17) | copy-start | bytes 196612
  9.7 45.4 %all-to-all-start = ((f32[176,2,8,128]{3,1,0,2:T(2,128)}), f32[176,2,8,128]{3,1,0,2:T(2,128)S(1)}, u32[]{:S(2)}, u32[]{:S(2)}) async-start(f32[176,2,8,128]{3,1,0,2:T(2,128)} %broadcast_in_dim.46), calls=%async_computation | async-start | bytes 2883584 | tf_op jit(solution)/shard_map/all_to_all | solution.py:41
  80.5 5.3 %slice-start.2 = ((f32[12,64,2,128]{3,2,1,0:T(2,128)}), f32[1,64,2,128]{3,2,1,0:T(2,128)S(1)}, s32[]{:S(2)}) async-start(f32[12,64,2,128]{3,2,1,0:T(2,128)} %param.2), calls=%async_computation.13 | async-start | bytes 131072 | tf_op jit(solution)/shard_map/slice | solution.py:62
  82.0 22.9 %all-to-all-start.1 = ((f32[176,2,8,128]{3,1,0,2:T(2,128)}), f32[176,2,8,128]{3,1,0,2:T(2,128)S(1)}, u32[]{:S(2)}, u32[]{:S(2)}) async-start(f32[176,2,8,128]{3,1,0,2:T(2,128)} %broadcast_in_dim.48), calls=%async_computation.1 | async-start | bytes 2883584 | tf_op jit(solution)/shard_map/all_to_all | solution.py:41
  85.8 79.5 %all-gather.6.cloned.1.call-start = ((), (), s32[]{:S(2)}) async-start(), calls=%async_computation.8 | async-start | bytes 3244032 | tf_op jit(solution)/shard_map/all_gather | solution.py:63
  130.6 24.9 %all-to-all-start.2 = ((f32[176,2,8,128]{3,1,0,2:T(2,128)}), f32[176,2,8,128]{3,1,0,2:T(2,128)S(1)}, u32[]{:S(2)}, u32[]{:S(2)}) async-start(f32[176,2,8,128]{3,1,0,2:T(2,128)} %broadcast_in_dim.50), calls=%async_computation.2 | async-start | bytes 2883584 | tf_op jit(solution)/shard_map/all_to_all | solution.py:41
  135.0 1.7 copy-start
  156.4 2.9 %copy-start.1 = (f32[1,2048,2,128]{3,1,2,0:T(8,128)S(1)}, f32[1,2048,2,128]{3,1,2,0:T(8,128)}, u32[]{:S(2)}) copy-start(f32[1,2048,2,128]{3,1,2,0:T(8,128)} %all-gather.10.cloned.1.call-done) | copy-start | bytes 6291460
  160.0 11.3 %all-to-all-start.5 = ((f32[64,8,128]{2,0,1:T(8,128)}), f32[64,8,128]{2,0,1:T(8,128)S(1)}, u32[]{:S(2)}, u32[]{:S(2)}) async-start(f32[64,8,128]{2,0,1:T(8,128)} %broadcast_in_dim.54), calls=%async_computation.5 | async-start | bytes 524288 | tf_op jit(solution)/shard_map/all_to_all | solution.py:60
  166.6 1.6 slice-start
  173.2 7.1 %slice-start.3 = ((f32[12,64,2,128]{3,2,1,0:T(2,128)}), f32[11,64,2,128]{3,2,1,0:T(2,128)S(1)}, s32[]{:S(2)}) async-start(f32[12,64,2,128]{3,2,1,0:T(2,128)} %param.2), calls=%async_computation.14 | async-start | bytes 1441792 | tf_op jit(solution)/shard_map/slice | solution.py:91
  176.2 11.3 %all-to-all-start.6 = ((f32[8,256,64]{1,2,0:T(8,128)}), f32[8,256,64]{1,2,0:T(8,128)}, u32[]{:S(2)}, u32[]{:S(2)}) async-start(f32[8,256,64]{1,2,0:T(8,128)} %fusion.25), calls=%async_computation.6 | async-start | bytes 1048576 | tf_op jit(solution)/shard_map/all_to_all | solution.py:82
  189.2 67.9 %copy-start.2 = (f32[22,8,16,128]{3,1,2,0:T(8,128)S(1)}, f32[22,8,16,128]{3,1,2,0:T(8,128)}, u32[]{:S(2)}) copy-start(f32[22,8,16,128]{3,1,2,0:T(8,128)} %copy.39) | copy-start | bytes 4325380
  189.2 67.9 %copy-start.3 = (f32[22,8,16,128]{3,1,2,0:T(8,128)S(1)}, f32[22,8,16,128]{3,1,2,0:T(8,128)}, u32[]{:S(2)}) copy-start(f32[22,8,16,128]{3,1,2,0:T(8,128)} %copy.38) | copy-start | bytes 4325380
  189.2 76.8 %all-to-all-start.7 = ((f32[8,256,704]{1,2,0:T(8,128)}), f32[8,256,704]{1,2,0:T(8,128)}, u32[]{:S(2)}, u32[]{:S(2)}) async-start(f32[8,256,704]{1,2,0:T(8,128)} %fusion.24), calls=%async_computation.7 | async-start | bytes 11534336 | tf_op jit(solution)/shard_map/all_to_all | solution.py:94
  194.5 62.6 %all-gather.8.cloned.1.call-start = ((), (), s32[]{:S(2)}) async-start(), calls=%async_computation.9 | async-start | bytes 2162688 | tf_op jit(solution)/shard_map/all_gather | solution.py:84
  262.8 6.3 %copy-start.4 = (f32[704,256]{1,0:T(8,128)S(1)}, f32[704,256]{1,0:T(8,128)}, u32[]{:S(2)}) copy-start(f32[704,256]{1,0:T(8,128)} %fusion) | copy-start | bytes 2162692
  269.2 0.8 copy-start.6
Sparse Core Ops, SparseCore 0:
  10.0 59.9 all-gather.9
  89.2 58.8 all-gather.5
  197.9 59.1 all-gather.7

commit v18 on v16

--- a/solution.py
+++ b/solution.py
@@ -40,14 +40,16 @@
         copies = jnp.broadcast_to(trail_part, (hi - lo, 2, row_count, row_run))
         moved = lax.all_to_all(copies, "row", split_axis=2, concat_axis=2, tiled=True)
         left_chunks.append(moved.reshape(hi - lo, 2 * block_size))
-    left_chunks[0], gathered = lax.optimization_barrier((left_chunks[0], gathered))
+    left_chunks[:2], gathered = lax.optimization_barrier((left_chunks[:2], gathered))
     first_cols = gathered[:block_size, 0, :]
     cross_cols = gathered[block_size:, 0, :]
     second_cols = gathered[block_size:, 1, :]
 
     col_position = lax.axis_index("col")
     lower_half = col_position * strip_width // block_size
-    own_rows = lax.all_gather(lower[0], "row", axis=2, tiled=True)
+    own_copies = jnp.broadcast_to(lower[0][:, :, None, :], (strip_width, 2, row_count, row_run))
+    own_rows = lax.all_to_all(own_copies, "row", split_axis=2, concat_axis=2, tiled=True)
+    own_rows = own_rows.reshape(strip_width, 2, block_size)
     diag_rows = lax.dynamic_index_in_dim(own_rows, lower_half, 1, keepdims=False)
     below = lower_half == 1
 
@@ -59,7 +61,6 @@
     chained_copies = jnp.broadcast_to(chained_piece[:, None, :], (strip_width, row_count, row_run))
     chained = lax.all_to_all(chained_copies, "row", split_axis=1, concat_axis=1, tiled=True)
     chained = chained.reshape(strip_width, block_size)
-    left_chunks[1], chained = lax.optimization_barrier((left_chunks[1], chained))
     joined = jnp.concatenate([strip[0].reshape(strip_width, 2 * row_run), chained_piece], axis=1)
     joined = lax.all_gather(joined, "col", axis=0, tiled=True)
     left_chunks[2:], joined = lax.optimization_barrier((left_chunks[2:], joined))

time: 288 us -> 293 us (1.017)
  blocking collectives: 49 us -> 25.2 us
  waiting for transfers between devices: 129 us -> 150 us
  local copies, waits for them, and re-layouts: 29.1 us -> 34.5 us
  starting transfers between devices: 33.4 us -> 36.8 us
    all_gather x1 -> x0, blocking collectives: 39.7 us -> none  [local(): own_rows = lax.all_gather(lower[0], 'row', axis=2, tiled=True)]
    all_to_all x1, blocking collectives: 9.33 us -> 25.2 us  [local(): lax.all_to_all(copies, 'row', split_axis=2, concat_axis=2, tiled=True)]
    all_to_all x0 -> x2, waiting for transfers between devices: none -> 11.4 us  [the longest x1 7 us: local(): lax.all_to_all(own_copies, 'row', split_axis=2, concat_axis=2, tiled=True)]
    all_to_all x0 -> x2, starting transfers between devices: none -> 10.4 us  [the longest x1 6.37 us: local(): lax.all_to_all(own_copies, 'row', split_axis=2, concat_axis=2, tiled=True)]
    all_to_all x4 -> x3, starting transfers between devices: 18.2 us -> 12.7 us  [local(): lax.all_to_all(copies, 'row', split_axis=2, concat_axis=2, tiled=True)]
    all_gather x1, waiting for transfers between devices: 11.1 us -> 14.4 us  [local(): gathered = lax.all_gather(lower[0], 'col', axis=0, tiled=True)]
    unnamed x20 -> x21, local copies, waits for them, and re-layouts: 5.06 us -> 1.81 us
    all_to_all x4 -> x3, waiting for transfers between devices: 56.7 us -> 59.9 us  [local(): lax.all_to_all(copies, 'row', split_axis=2, concat_axis=2, tiled=True)]
  transfers between devices with their start and end apart: 10 -> 11, of which waited for: 6 -> 8; matrix products, arithmetic and copies ran while one was open for 13% -> 13% of each run, Pallas kernels for 0% -> 0%
where the time goes in v18:
time: 293 us; the launch traced here: 289 us
  waiting for transfers between devices  150 us (51%)
  starting transfers between devices  36.8 us (13%)
  local copies, waits for them, and re-layouts  34.5 us (12%)
  blocking collectives  25.2 us (9%)
  matrix products  21.4 us (7%)
  between operations  13.4 us (5%)
  other arithmetic  6.93 us (2%)
    all_gather x1, waiting for transfers between devices, local(): everything = lax.all_gather(solved_lead, 'col', axis=0, tiled=True)  62.2 us
    all_to_all x3, waiting for transfers between devices, local(): lax.all_to_all(copies, 'row', split_axis=2, concat_axis=2, tiled=True)  59.9 us
    all_to_all x1, blocking collectives, local(): lax.all_to_all(copies, 'row', split_axis=2, concat_axis=2, tiled=True)  25.2 us
    all_gather x1, waiting for transfers between devices, local(): gathered = lax.all_gather(lower[0], 'col', axis=0, tiled=True)  14.4 us
    all_to_all x3, starting transfers between devices, local(): lax.all_to_all(copies, 'row', split_axis=2, concat_axis=2, tiled=True)  12.7 us
    dot_general x5, matrix products, times_rows(): jnp.dot(coeff, right_side, precision=highest, preferred_element_type=jnp....  11.8 us
    dot_general x2, matrix products, times_rows_turned(): lax.dot_general(coeff, right_turned, (((1,), (1,)), ((), ())), precision=...  9.54 us
    all_to_all x1, waiting for transfers between devices, local(): lax.all_to_all(own_copies, 'row', split_axis=2, concat_axis=2, tiled=True)  7 us
  transfers between devices with their start and end apart: 11, of which 8 were waited for; matrix products, arithmetic and copies ran while one was open for 13% of the time, Pallas kernels for 0%

profile of v18, /device:TPU:1, one launch (start us, length us, event | category | flops | bytes accessed | tf_op | source)
XLA Modules:
  0.0 288.7 jit_solution(4447776344249649250)
XLA Ops:
  6.5 1.6 slice_bitcast_fusion.7
  8.1 0.9 broadcast_in_dim.58
  9.0 6.4 %all-to-all-start.4 = ((f32[64,2,8,128]{3,1,0,2:T(2,128)}), f32[64,2,8,128]{3,1,0,2:T(2,128)S(1)}, u32[]{:S(2)}, u32[]{:S(2)}) async-start(f32[64,2,8,128]{3,1,0,2:T(2,128)} %broadcast_in_dim.58), calls=%async_computation.4 | async-start | bytes 1048576 | tf_op jit(solution)/shard_map/all_to_all | solution.py:51
  15.4 0.8 slice_bitcast_fusion.3
  16.2 7.0 %all-to-all-done.4 = f32[64,2,8,128]{3,1,0,2:T(2,128)S(1)} async-done(((f32[64,2,8,128]{3,1,0,2:T(2,128)}), f32[64,2,8,128]{3,1,0,2:T(2,128)S(1)}, u32[]{:S(2)}, u32[]{:S(2)}) %all-to-all-start.4) | async-done | bytes 524320 | tf_op jit(solution)/shard_map/all_to_all | solution.py:51
  23.2 1.5 broadcast_in_dim.53
  24.7 5.2 %all-to-all-start.1 = ((f32[176,2,8,128]{3,1,0,2:T(2,128)}), f32[176,2,8,128]{3,1,0,2:T(2,128)S(1)}, u32[]{:S(2)}, u32[]{:S(2)}) async-start(f32[176,2,8,128]{3,1,0,2:T(2,128)} %broadcast_in_dim.53), calls=%async_computation.1 | async-start | bytes 2883584 | tf_op jit(solution)/shard_map/all_to_all | solution.py:41
  29.9 0.7 all-gather.9.cloned.1.call-update
  30.6 18.4 %all-to-all-done.1 = f32[176,2,8,128]{3,1,0,2:T(2,128)S(1)} async-done(((f32[176,2,8,128]{3,1,0,2:T(2,128)}), f32[176,2,8,128]{3,1,0,2:T(2,128)S(1)}, u32[]{:S(2)}, u32[]{:S(2)}) %all-to-all-start.1) | async-done | bytes 1441824 | tf_op jit(solution)/shard_map/all_to_all | solution.py:41
  49.0 1.5 broadcast_in_dim.51
  50.5 3.7 %all-to-all-start = ((f32[176,2,8,128]{3,1,0,2:T(2,128)}), f32[176,2,8,128]{3,1,0,2:T(2,128)S(1)}, u32[]{:S(2)}, u32[]{:S(2)}) async-start(f32[176,2,8,128]{3,1,0,2:T(2,128)} %broadcast_in_dim.51), calls=%async_computation | async-start | bytes 2883584 | tf_op jit(solution)/shard_map/all_to_all | solution.py:41
  54.2 1.1 copy.14
  55.3 1.1 reshape.50
  56.4 2.0 copy.9
  58.4 15.0 %all-to-all-done = f32[176,2,8,128]{3,1,0,2:T(2,128)S(1)} async-done(((f32[176,2,8,128]{3,1,0,2:T(2,128)}), f32[176,2,8,128]{3,1,0,2:T(2,128)S(1)}, u32[]{:S(2)}, u32[]{:S(2)}) %all-to-all-start) | async-done | bytes 1441824 | tf_op jit(solution)/shard_map/all_to_all | solution.py:41
  73.4 0.8 copy.8
  74.2 2.8 copy_bitcast_fusion.2
  77.0 14.4 %all-gather.9.cloned.1.call-done = f32[1,2048,2,128]{3,2,0,1:T(2,128)} async-done(((f32[1,64,2,128]{3,2,0,1:T(2,128)}), f32[1,2048,2,128]{3,2,0,1:T(2,128)}) %all-gather.9.cloned.1.call-update) | async-done | bytes 2097168 | tf_op jit(solution)/shard_map/all_gather | solution.py:32
  91.4 3.2 %fusion.22 = (f32[1024,1,128]{2,1,0:T(1,128)S(1)}, f32[1024,1,128]{2,1,0:T(1,128)}) fusion(f32[2048,2,128]{2,1,0:T(2,128)} %bitcast.89), kind=kLoop, calls=%fused_computation.43 | loop fusion | bytes 2097152 | tf_op jit(solution)/shard_map/slice | solution.py:45
  95.1 0.7 broadcast_in_dim.59
  95.8 4.0 %all-to-all-start.5 = ((f32[64,8,128]{2,0,1:T(8,128)}), f32[64,8,128]{2,0,1:T(8,128)S(1)}, u32[]{:S(2)}, u32[]{:S(2)}) async-start(f32[64,8,128]{2,0,1:T(8,128)} %broadcast_in_dim.59), calls=%async_computation.5 | async-start | bytes 524288 | tf_op jit(solution)/shard_map/all_to_all | solution.py:58
  99.9 1.8 copy.11
  101.7 4.4 %all-to-all-done.5 = f32[64,8,128]{2,0,1:T(8,128)S(1)} async-done(((f32[64,8,128]{2,0,1:T(8,128)}), f32[64,8,128]{2,0,1:T(8,128)S(1)}, u32[]{:S(2)}, u32[]{:S(2)}) %all-to-all-start.5) | async-done | bytes 262176 | tf_op jit(solution)/shard_map/all_to_all | solution.py:58
  107.5 25.2 %all_to_all.45 = f32[176,2,8,128]{3,1,0,2:T(2,128)S(1)} all-to-all(f32[176,2,8,128]{3,1,0,2:T(2,128)S(1)} %broadcast_in_dim.57), channel_id=1, replica_groups=mesh['row'=8,'col'=32] {'row'}, dimensions={2} | all-to-all | bytes 2883584 | tf_op jit(solution)/shard_map/all_to_all | solution.py:41
  132.8 1.6 broadcast_in_dim.55
  134.4 3.8 %all-to-all-start.2 = ((f32[176,2,8,128]{3,1,0,2:T(2,128)}), f32[176,2,8,128]{3,1,0,2:T(2,128)S(1)}, u32[]{:S(2)}, u32[]{:S(2)}) async-start(f32[176,2,8,128]{3,1,0,2:T(2,128)} %broadcast_in_dim.55), calls=%async_computation.2 | async-start | bytes 2883584 | tf_op jit(solution)/shard_map/all_to_all | solution.py:41
  138.1 2.0 copy.13
  140.1 26.6 %all-to-all-done.2 = f32[176,2,8,128]{3,1,0,2:T(2,128)S(1)} async-done(((f32[176,2,8,128]{3,1,0,2:T(2,128)}), f32[176,2,8,128]{3,1,0,2:T(2,128)S(1)}, u32[]{:S(2)}, u32[]{:S(2)}) %all-to-all-start.2) | async-done | bytes 1441824 | tf_op jit(solution)/shard_map/all_to_all | solution.py:41
  166.7 0.8 copy.12
  167.5 2.8 copy_bitcast_fusion
  170.4 1.1 slice_bitcast_fusion
  171.4 0.7 broadcast_in_dim.60
  172.2 4.0 %all-to-all-start.6 = ((f32[64,8,128]{2,0,1:T(8,128)}), f32[64,8,128]{2,0,1:T(8,128)S(1)}, u32[]{:S(2)}, u32[]{:S(2)}) async-start(f32[64,8,128]{2,0,1:T(8,128)} %broadcast_in_dim.60), calls=%async_computation.6 | async-start | bytes 524288 | tf_op jit(solution)/shard_map/all_to_all | solution.py:62
  176.1 1.1 slice_negate_fusion
  177.2 1.0 copy-done.3
  178.6 1.4 slice-done
  180.7 1.5 all-to-all-done.6
  182.2 1.9 fusion.9
  184.1 3.0 %fusion.24 = f32[8,256,64]{1,2,0:T(8,128)} fusion(f32[8,256,256]{2,1,0:T(8,128)S(1)} %bitcast.82, f32[64,256,1]{1,0,2:T(8,128)S(1)} %fusion.9), kind=kOutput, calls=%fused_computation.45 | convolution fusion | flops 402653184 | bytes 2686976 | tf_op jit(solution)/shard_map/dot_general | solution.py:14
  187.0 4.2 %all-to-all-start.7 = ((f32[8,256,64]{1,2,0:T(8,128)}), f32[8,256,64]{1,2,0:T(8,128)}, u32[]{:S(2)}, u32[]{:S(2)}) async-start(f32[8,256,64]{1,2,0:T(8,128)} %fusion.24), calls=%async_computation.7 | async-start | bytes 1048576 | tf_op jit(solution)/shard_map/all_to_all | solution.py:84
  191.8 6.6 %fusion.23 = f32[8,256,704]{1,2,0:T(8,128)} fusion(f32[8,256,256]{2,1,0:T(8,128)S(1)} %bitcast.83, f32[704,256,1]{1,0,2:T(8,128)S(1)} %reshape.56), kind=kOutput, calls=%fused_computation.44 | convolution fusion | flops 4429185024 | bytes 8585216 | tf_op jit(solution)/shard_map/dot_general | solution.py:14
  198.4 1.7 reduce_sum.18
  200.1 5.3 %all-to-all-start.8 = ((f32[8,256,704]{1,2,0:T(8,128)}), f32[8,256,704]{1,2,0:T(8,128)}, u32[]{:S(2)}, u32[]{:S(2)}) async-start(f32[8,256,704]{1,2,0:T(8,128)} %fusion.23), calls=%async_computation.8 | async-start | bytes 11534336 | tf_op jit(solution)/shard_map/all_to_all | solution.py:93
  206.1 62.2 %all-gather.7.cloned.1.call-done = f32[2048,256]{1,0:T(8,128)} async-done(((f32[64,256]{1,0:T(8,128)}), f32[2048,256]{1,0:T(8,128)}) %all-gather.7.cloned.1.call-update) | async-done | bytes 2097168 | tf_op jit(solution)/shard_map/all_gather | solution.py:86
  268.3 8.5 %fusion = f32[704,256]{1,0:T(8,128)} fusion(f32[2048,256]{1,0:T(8,128)} %all-gather.7.cloned.1.call-done, f32[176,2048]{1,0:T(8,128)} %get-tuple-element.20, f32[176,2048]{1,0:T(8,128)} %get-tuple-element.19, f32[176,2048]{1,0:T(8,128)S(1)} %copy-done.4, f32[176,2048]{1,0:T(8,128)S(1)} %copy-done.5), kind=kOutput, calls=%fused_computation | convolution fusion | flops 4433510400 | bytes 8585216 | tf_op jit(solution)/shard_map/dot_general | solution.py:10
  276.8 3.2 %reduce_sum.19 = f32[256,704]{0,1:T(8,128)S(1)} reduce(f32[8,256,704]{1,2,0:T(8,128)} %all-to-all-done.8, f32[]{:T(128)} %constant.13.clone.1), dimensions={0}, to_apply=%region_1.2 | reduce | flops 1261568 | bytes 6488068 | tf_op jit(solution)/shard_map/reduce_sum | solution.py:94
  280.1 0.7 copy-done.9
  280.9 1.3 reshape.54
  (44 shorter events, 4.5 us)
Async XLA Ops:
  6.5 8.9 %slice-start.1 = ((f32[12,64,2,128]{3,2,1,0:T(2,128)}), f32[11,64,2,128]{3,2,1,0:T(2,128)S(1)}, s32[]{:S(2)}) async-start(f32[12,64,2,128]{3,2,1,0:T(2,128)} %param.3), calls=%async_computation.13 | async-start | bytes 1441792 | tf_op jit(solution)/shard_map/slice | solution.py:39
  9.0 14.2 %all-to-all-start.4 = ((f32[64,2,8,128]{3,1,0,2:T(2,128)}), f32[64,2,8,128]{3,1,0,2:T(2,128)S(1)}, u32[]{:S(2)}, u32[]{:S(2)}) async-start(f32[64,2,8,128]{3,1,0,2:T(2,128)} %broadcast_in_dim.58), calls=%async_computation.4 | async-start | bytes 1048576 | tf_op jit(solution)/shard_map/all_to_all | solution.py:51
  24.7 24.3 %all-to-all-start.1 = ((f32[176,2,8,128]{3,1,0,2:T(2,128)}), f32[176,2,8,128]{3,1,0,2:T(2,128)S(1)}, u32[]{:S(2)}, u32[]{:S(2)}) async-start(f32[176,2,8,128]{3,1,0,2:T(2,128)} %broadcast_in_dim.53), calls=%async_computation.1 | async-start | bytes 2883584 | tf_op jit(solution)/shard_map/all_to_all | solution.py:41
  29.9 61.5 %all-gather.9.cloned.1.call-start = ((), (), s32[]{:S(2)}) async-start(), calls=%async_computation.11 | async-start | bytes 2162688 | tf_op jit(solution)/shard_map/all_gather | solution.py:32
  50.5 22.9 %all-to-all-start = ((f32[176,2,8,128]{3,1,0,2:T(2,128)}), f32[176,2,8,128]{3,1,0,2:T(2,128)S(1)}, u32[]{:S(2)}, u32[]{:S(2)}) async-start(f32[176,2,8,128]{3,1,0,2:T(2,128)} %broadcast_in_dim.51), calls=%async_computation | async-start | bytes 2883584 | tf_op jit(solution)/shard_map/all_to_all | solution.py:41
  58.4 15.8 %copy-start = (f32[176,2,8,128]{3,2,1,0:T(8,128)S(1)}, f32[176,2,8,128]{3,2,1,0:T(8,128)}, u32[]{:S(2)}) copy-start(f32[176,2,8,128]{3,2,1,0:T(8,128)} %copy.9) | copy-start | bytes 4325380
  77.0 22.8 %slice-start.2 = ((f32[12,64,2,128]{3,2,1,0:T(2,128)}), f32[1,64,2,128]{3,2,1,0:T(2,128)S(1)}, s32[]{:S(2)}) async-start(f32[12,64,2,128]{3,2,1,0:T(2,128)} %param.2), calls=%async_computation.14 | async-start | bytes 131072 | tf_op jit(solution)/shard_map/slice | solution.py:64
  95.8 10.2 %all-to-all-start.5 = ((f32[64,8,128]{2,0,1:T(8,128)}), f32[64,8,128]{2,0,1:T(8,128)S(1)}, u32[]{:S(2)}, u32[]{:S(2)}) async-start(f32[64,8,128]{2,0,1:T(8,128)} %broadcast_in_dim.59), calls=%async_computation.5 | async-start | bytes 524288 | tf_op jit(solution)/shard_map/all_to_all | solution.py:58
  99.8 76.3 %all-gather.5.cloned.1.call-start = ((), (), s32[]{:S(2)}) async-start(), calls=%async_computation.9 | async-start | bytes 3244032 | tf_op jit(solution)/shard_map/all_gather | solution.py:65
  99.9 7.3 %copy-start.7 = (f32[176,2,128]{2,1,0:T(2,128)S(1)}, f32[176,2,128]{2,1,0:T(2,128)}, u32[]{:S(2)}) copy-start(f32[176,2,128]{2,1,0:T(2,128)} %get-tuple-element.25) | copy-start | bytes 540676
  101.7 5.5 %copy-start.2 = (f32[2048,2,128]{2,0,1:T(8,128)}, f32[2048,2,128]{2,0,1:T(8,128)S(1)}, u32[]{:S(2)}) copy-start(f32[2048,2,128]{2,0,1:T(8,128)S(1)} %copy.11) | copy-start | bytes 6291460
  107.2 25.6 %copy-start.6 = (f32[176,2,128]{2,1,0:T(2,128)S(1)}, f32[176,2,128]{2,1,0:T(2,128)}, u32[]{:S(2)}) copy-start(f32[176,2,128]{2,1,0:T(2,128)} %get-tuple-element.26) | copy-start | bytes 540676
  134.4 32.3 %all-to-all-start.2 = ((f32[176,2,8,128]{3,1,0,2:T(2,128)}), f32[176,2,8,128]{3,1,0,2:T(2,128)S(1)}, u32[]{:S(2)}, u32[]{:S(2)}) async-start(f32[176,2,8,128]{3,1,0,2:T(2,128)} %broadcast_in_dim.55), calls=%async_computation.2 | async-start | bytes 2883584 | tf_op jit(solution)/shard_map/all_to_all | solution.py:41
  140.1 27.4 %copy-start.1 = (f32[176,2,8,128]{3,2,1,0:T(8,128)S(1)}, f32[176,2,8,128]{3,2,1,0:T(8,128)}, u32[]{:S(2)}) copy-start(f32[176,2,8,128]{3,2,1,0:T(8,128)} %copy.13) | copy-start | bytes 4325380
  172.2 10.0 %all-to-all-start.6 = ((f32[64,8,128]{2,0,1:T(8,128)}), f32[64,8,128]{2,0,1:T(8,128)S(1)}, u32[]{:S(2)}, u32[]{:S(2)}) async-start(f32[64,8,128]{2,0,1:T(8,128)} %broadcast_in_dim.60), calls=%async_computation.6 | async-start | bytes 524288 | tf_op jit(solution)/shard_map/all_to_all | solution.py:62
  177.2 1.0 copy-start.3
  178.5 1.6 slice-start
  184.1 7.1 %slice-start.3 = ((f32[12,64,2,128]{3,2,1,0:T(2,128)}), f32[11,64,2,128]{3,2,1,0:T(2,128)S(1)}, s32[]{:S(2)}) async-start(f32[12,64,2,128]{3,2,1,0:T(2,128)} %param.2), calls=%async_computation.15 | async-start | bytes 1441792 | tf_op jit(solution)/shard_map/slice | solution.py:90
  187.0 11.4 %all-to-all-start.7 = ((f32[8,256,64]{1,2,0:T(8,128)}), f32[8,256,64]{1,2,0:T(8,128)}, u32[]{:S(2)}, u32[]{:S(2)}) async-start(f32[8,256,64]{1,2,0:T(8,128)} %fusion.24), calls=%async_computation.7 | async-start | bytes 1048576 | tf_op jit(solution)/shard_map/all_to_all | solution.py:84
  200.1 68.2 %copy-start.4 = (f32[176,2048]{1,0:T(8,128)S(1)}, f32[176,2048]{1,0:T(8,128)}, u32[]{:S(2)}) copy-start(f32[176,2048]{1,0:T(8,128)} %get-tuple-element.18) | copy-start | bytes 4325380
  200.1 68.2 %copy-start.5 = (f32[176,2048]{1,0:T(8,128)S(1)}, f32[176,2048]{1,0:T(8,128)}, u32[]{:S(2)}) copy-start(f32[176,2048]{1,0:T(8,128)} %get-tuple-element.17) | copy-start | bytes 4325380
  200.1 76.7 %all-to-all-start.8 = ((f32[8,256,704]{1,2,0:T(8,128)}), f32[8,256,704]{1,2,0:T(8,128)}, u32[]{:S(2)}, u32[]{:S(2)}) async-start(f32[8,256,704]{1,2,0:T(8,128)} %fusion.23), calls=%async_computation.8 | async-start | bytes 11534336 | tf_op jit(solution)/shard_map/all_to_all | solution.py:93
  205.4 62.9 %all-gather.7.cloned.1.call-start = ((), (), s32[]{:S(2)}) async-start(), calls=%async_computation.10 | async-start | bytes 2162688 | tf_op jit(solution)/shard_map/all_gather | solution.py:86
  276.8 3.2 %copy-start.8 = (f32[704,256]{1,0:T(8,128)S(1)}, f32[704,256]{1,0:T(8,128)}, u32[]{:S(2)}) copy-start(f32[704,256]{1,0:T(8,128)} %fusion) | copy-start | bytes 2162692
  280.0 0.8 copy-start.9
Sparse Core Ops, SparseCore 0:
  33.3 58.0 all-gather.8
  107.3 59.3 all-gather.4
  208.8 59.5 all-gather.6

commit v19 on v14

--- a/solution.py
+++ b/solution.py
@@ -33,7 +33,7 @@
 
     trail_count = cols_here - strip_width
     chunk = trail_count // 4
-    bounds = [0, chunk, 2 * chunk, 3 * chunk, trail_count]
+    bounds = [0, chunk, trail_count]
     left_chunks = []
     for lo, hi in zip(bounds[:-1], bounds[1:]):
         trail_part = lower[1:].reshape(trail_count, 2, 1, row_run)[lo:hi]

time: 282 us -> 289 us (1.025)
  blocking collectives: 71.8 us -> 40 us
  waiting for transfers between devices: 113 us -> 139 us
  local copies, waits for them, and re-layouts: 21 us -> 32.4 us
    all_to_all x2 -> x0, blocking collectives: 32.8 us -> none  [the longest x1 23.8 us: local(): lax.all_to_all(copies, 'row', split_axis=2, concat_axis=2, tiled=True)]
    all_to_all x3 -> x2, waiting for transfers between devices: 34.9 us -> 58.1 us  [local(): lax.all_to_all(copies, 'row', split_axis=2, concat_axis=2, tiled=True)]
    all_to_all x0 -> x1, waiting for transfers between devices: none -> 6.03 us  [local(): lax.all_to_all(cross_copies, 'row', split_axis=1, concat_axis=1, tiled=True)]
    slice x3 -> x2, local copies, waits for them, and re-layouts: 0.58 us -> 4.57 us  [local(): trail_parts = times_rows_turned(inverse_cols, strip_rows[strip_width:])]
    unnamed x18 -> x22, local copies, waits for them, and re-layouts: 4.69 us -> 8.53 us
    all_to_all x0 -> x1, starting transfers between devices: none -> 3.41 us  [local(): lax.all_to_all(cross_copies, 'row', split_axis=1, concat_axis=1, tiled=True)]
    all_to_all x3 -> x2, starting transfers between devices: 13.7 us -> 11.1 us  [local(): lax.all_to_all(copies, 'row', split_axis=2, concat_axis=2, tiled=True)]
  transfers between devices with their start and end apart: 9 -> 9, of which waited for: 6 -> 5; matrix products, arithmetic and copies ran while one was open for 12% -> 14% of each run, Pallas kernels for 0% -> 0%
where the time goes in v19:
time: 289 us; the launch traced here: 285 us
  waiting for transfers between devices  139 us (48%)
  blocking collectives  40 us (14%)
  local copies, waits for them, and re-layouts  32.4 us (11%)
  starting transfers between devices  29.1 us (10%)
  matrix products  24 us (8%)
  between operations  13.3 us (5%)
  other arithmetic  6.81 us (2%)
    all_gather x1, waiting for transfers between devices, local(): everything = lax.all_gather(solved_lead, 'col', axis=0, tiled=True)  60.9 us
    all_to_all x2, waiting for transfers between devices, local(): lax.all_to_all(copies, 'row', split_axis=2, concat_axis=2, tiled=True)  58.1 us
    all_gather x1, blocking collectives, local(): own_rows = lax.all_gather(lower[0], 'row', axis=2, tiled=True)  40 us
    dot_general x5, matrix products, times_rows(): jnp.dot(coeff, right_side, precision=highest, preferred_element_type=jnp....  13.3 us
    all_gather x1, waiting for transfers between devices, local(): gathered = lax.all_gather(lower[0], 'col', axis=0, tiled=True)  11.7 us
    all_to_all x2, starting transfers between devices, local(): lax.all_to_all(copies, 'row', split_axis=2, concat_axis=2, tiled=True)  11.1 us
    dot_general x2, matrix products, times_rows_turned(): lax.dot_general(coeff, right_turned, (((1,), (1,)), ((), ())), precision=...  10.7 us
    unnamed x22, local copies, waits for them, and re-layouts  8.53 us
  transfers between devices with their start and end apart: 9, of which 5 were waited for; matrix products, arithmetic and copies ran while one was open for 14% of the time, Pallas kernels for 0%

profile of v19, /device:TPU:1, one launch (start us, length us, event | category | flops | bytes accessed | tf_op | source)
XLA Modules:
  0.0 284.7 jit_solution(9656354886405646118)
XLA Ops:
  6.5 0.8 slice.47
  7.4 0.6 copy.15
  8.0 1.2 slice.45
  9.2 1.5 broadcast_in_dim.32
  10.8 6.4 %all-to-all-start = ((f32[176,2,8,128]{3,1,0,2:T(2,128)}), f32[176,2,8,128]{3,1,0,2:T(2,128)S(1)}, u32[]{:S(2)}, u32[]{:S(2)}) async-start(f32[176,2,8,128]{3,1,0,2:T(2,128)} %broadcast_in_dim.32), calls=%async_computation | async-start | bytes 2883584 | tf_op jit(solution)/shard_map/all_to_all | solution.py:41
  17.1 40.0 %all-gather.1 = f32[1,64,2,1024]{3,1,2,0:T(8,128)S(1)} all-gather(f32[1,64,2,128]{3,1,2,0:T(8,128)S(1)} %copy-done.6), channel_id=3, replica_groups=mesh['row'=8,'col'=32] {'row'}, dimensions={3}, use_global_device_ids=true | all-gather | bytes 589824 | tf_op jit(solution)/shard_map/all_gather | solution.py:50
  57.1 0.8 copy.9
  58.0 0.5 copy.33
  58.5 11.7 %all-gather.10.cloned.1.call-done = f32[1,2048,2,128]{3,1,2,0:T(8,128)} async-done(((f32[1,64,2,128]{3,1,2,0:T(8,128)}), f32[1,2048,2,128]{3,1,2,0:T(8,128)}) %all-gather.10.cloned.1.call-update) | async-done | bytes 2097168 | tf_op jit(solution)/shard_map/all_gather | solution.py:32
  70.2 1.5 convolution_bitcast_fusion
  71.7 0.7 broadcast_in_dim.35
  72.4 3.4 %all-to-all-start.2 = ((f32[64,8,128]{2,0,1:T(8,128)}), f32[64,8,128]{2,0,1:T(8,128)S(1)}, u32[]{:S(2)}, u32[]{:S(2)}) async-start(f32[64,8,128]{2,0,1:T(8,128)} %broadcast_in_dim.35), calls=%async_computation.2 | async-start | bytes 524288 | tf_op jit(solution)/shard_map/all_to_all | solution.py:56
  75.9 6.0 %all-to-all-done.2 = f32[64,8,128]{2,0,1:T(8,128)S(1)} async-done(((f32[64,8,128]{2,0,1:T(8,128)}), f32[64,8,128]{2,0,1:T(8,128)S(1)}, u32[]{:S(2)}, u32[]{:S(2)}) %all-to-all-start.2) | async-done | bytes 262176 | tf_op jit(solution)/shard_map/all_to_all | solution.py:56
  81.9 0.7 copy-done.5
  82.6 3.2 %broadcast_in_dim.34 = f32[528,2,8,128]{3,1,0,2:T(2,128)} broadcast(f32[528,2,128]{2,1,0:T(2,128)S(1)} %slice_bitcast_fusion), dimensions={0,1,3} | broadcast | bytes 4866048 | tf_op jit(solution)/shard_map/broadcast_in_dim | solution.py:40
  85.8 4.7 %all-to-all-start.1 = ((f32[528,2,8,128]{3,1,0,2:T(2,128)}), f32[528,2,8,128]{3,1,0,2:T(2,128)}, u32[]{:S(2)}, u32[]{:S(2)}) async-start(f32[528,2,8,128]{3,1,0,2:T(2,128)} %broadcast_in_dim.34), calls=%async_computation.1 | async-start | bytes 8650752 | tf_op jit(solution)/shard_map/all_to_all | solution.py:41
  90.6 0.8 slice.50
  91.5 1.4 fusion.13
  92.9 0.6 copy-done.8
  93.5 0.6 pad_maximum_fusion.1
  94.2 1.1 slice_bitcast_fusion.1
  95.3 58.1 %all-to-all-done.1 = f32[528,2,8,128]{3,1,0,2:T(2,128)} async-done(((f32[528,2,8,128]{3,1,0,2:T(2,128)}), f32[528,2,8,128]{3,1,0,2:T(2,128)}, u32[]{:S(2)}, u32[]{:S(2)}) %all-to-all-start.1) | async-done | bytes 4325408 | tf_op jit(solution)/shard_map/all_to_all | solution.py:41
  153.4 1.5 broadcast_in_dim.36
  154.8 4.2 %all-to-all-start.3 = ((f32[64,8,128]{2,0,1:T(8,128)}), f32[64,8,128]{2,0,1:T(8,128)}, u32[]{:S(2)}, u32[]{:S(2)}) async-start(f32[64,8,128]{2,0,1:T(8,128)} %broadcast_in_dim.36), calls=%async_computation.3 | async-start | bytes 524288 | tf_op jit(solution)/shard_map/all_to_all | solution.py:60
  159.1 4.7 %copy.11 = f32[528,2,8,128]{3,2,1,0:T(8,128)S(1)} copy(f32[528,2,8,128]{3,1,0,2:T(2,128)} %all-to-all-done.1) | data formatting | bytes 8650752 | tf_op jit(solution)/shard_map/all_to_all | solution.py:41
  163.8 4.0 %copy.32 = f32[66,8,16,128]{3,1,2,0:T(8,128)} copy(f32[66,8,16,128]{3,2,1,0:T(8,128)S(1)} %bitcast.69) | data formatting | bytes 8650752
  167.8 1.1 slice_negate_fusion
  168.9 1.0 copy-done.3
  170.0 0.2 copy-done.4
  170.1 0.1 select_maximum_fusion
  170.4 1.4 slice-done
  171.9 1.3 fusion.7
  173.2 1.9 fusion.5
  175.1 3.0 %fusion.21 = f32[8,256,64]{1,2,0:T(8,128)} fusion(f32[8,256,256]{2,1,0:T(8,128)S(1)} %bitcast.66, f32[64,256,1]{1,0,2:T(8,128)S(1)} %fusion.5), kind=kOutput, calls=%fused_computation.37 | convolution fusion | flops 402653184 | bytes 2686976 | tf_op jit(solution)/shard_map/dot_general | solution.py:14
  178.1 4.9 %all-to-all-start.4 = ((f32[8,256,64]{1,2,0:T(8,128)}), f32[8,256,64]{1,2,0:T(8,128)}, u32[]{:S(2)}, u32[]{:S(2)}) async-start(f32[8,256,64]{1,2,0:T(8,128)} %fusion.21), calls=%async_computation.4 | async-start | bytes 1048576 | tf_op jit(solution)/shard_map/all_to_all | solution.py:82
  183.0 2.0 slice.55
  185.0 2.5 reshape.44
  187.5 7.7 %fusion.20 = f32[8,256,704]{1,2,0:T(8,128)} fusion(f32[8,256,256]{2,1,0:T(8,128)S(1)} %bitcast.67, f32[704,256,1]{1,0,2:T(8,128)} %reshape.44), kind=kOutput, calls=%fused_computation.36 | convolution fusion | flops 4429185024 | bytes 8585216 | tf_op jit(solution)/shard_map/dot_general | solution.py:14
  195.3 1.7 reduce_sum.18
  197.0 5.1 %all-to-all-start.5 = ((f32[8,256,704]{1,2,0:T(8,128)}), f32[8,256,704]{1,2,0:T(8,128)}, u32[]{:S(2)}, u32[]{:S(2)}) async-start(f32[8,256,704]{1,2,0:T(8,128)} %fusion.20), calls=%async_computation.5 | async-start | bytes 11534336 | tf_op jit(solution)/shard_map/all_to_all | solution.py:91
  202.1 0.3 all-gather.8.cloned.1.call-start
  202.4 0.5 all-gather.8.cloned.1.call-update
  202.9 60.9 %all-gather.8.cloned.1.call-done = f32[2048,256]{1,0:T(8,128)} async-done(((f32[64,256]{1,0:T(8,128)}), f32[2048,256]{1,0:T(8,128)}) %all-gather.8.cloned.1.call-update) | async-done | bytes 2097168 | tf_op jit(solution)/shard_map/all_gather | solution.py:84
  263.7 7.3 %fusion = f32[704,256]{1,0:T(8,128)S(1)} fusion(f32[2048,256]{1,0:T(8,128)} %all-gather.8.cloned.1.call-done, f32[528,2048]{1,0:T(8,128)} %bitcast.68, f32[176,2048]{1,0:T(8,128)S(1)} %bitcast.72), kind=kOutput, calls=%fused_computation | convolution fusion | flops 4430626816 | bytes 8585216 | tf_op jit(solution)/shard_map/dot_general | solution.py:10
  271.0 1.9 all-to-all-done.5
  272.9 3.1 %reduce_sum.19 = f32[256,704]{0,1:T(8,128)S(1)} reduce(f32[8,256,704]{1,2,0:T(8,128)} %all-to-all-done.5, f32[]{:T(128)} %constant.13.clone.1), dimensions={0}, to_apply=%region_1.2 | reduce | flops 1261568 | bytes 6488068 | tf_op jit(solution)/shard_map/reduce_sum | solution.py:92
  276.1 0.7 copy-done.7
  276.9 1.3 reshape.39
  (28 shorter events, 0.5 us)
Async XLA Ops:
  6.5 63.7 %all-gather.10.cloned.1.call-start = ((), (), s32[]{:S(2)}) async-start(), calls=%async_computation.8 | async-start | bytes 2162688 | tf_op jit(solution)/shard_map/all_gather | solution.py:32
  9.2 7.9 %copy-start.6 = (f32[1,64,2,128]{3,1,2,0:T(8,128)S(1)}, f32[1,64,2,128]{3,1,2,0:T(8,128)}, u32[]{:S(2)}) copy-start(f32[1,64,2,128]{3,1,2,0:T(8,128)} %copy.15) | copy-start | bytes 196612
  10.8 46.4 %all-to-all-start = ((f32[176,2,8,128]{3,1,0,2:T(2,128)}), f32[176,2,8,128]{3,1,0,2:T(2,128)S(1)}, u32[]{:S(2)}, u32[]{:S(2)}) async-start(f32[176,2,8,128]{3,1,0,2:T(2,128)} %broadcast_in_dim.32), calls=%async_computation | async-start | bytes 2883584 | tf_op jit(solution)/shard_map/all_to_all | solution.py:41
  57.1 13.1 %copy-start.1 = (f32[1,64,2,1024]{3,1,2,0:T(8,128)}, f32[1,64,2,1024]{3,1,2,0:T(8,128)S(1)}, u32[]{:S(2)}) copy-start(f32[1,64,2,1024]{3,1,2,0:T(8,128)S(1)} %all-gather.1) | copy-start | bytes 1572868
  72.4 9.5 %all-to-all-start.2 = ((f32[64,8,128]{2,0,1:T(8,128)}), f32[64,8,128]{2,0,1:T(8,128)S(1)}, u32[]{:S(2)}, u32[]{:S(2)}) async-start(f32[64,8,128]{2,0,1:T(8,128)} %broadcast_in_dim.35), calls=%async_computation.2 | async-start | bytes 524288 | tf_op jit(solution)/shard_map/all_to_all | solution.py:56
  81.9 0.7 copy-start.5
  85.8 5.6 %copy-start = (f32[1,2048,2,128]{3,1,2,0:T(8,128)S(1)}, f32[1,2048,2,128]{3,1,2,0:T(8,128)}, u32[]{:S(2)}) copy-start(f32[1,2048,2,128]{3,1,2,0:T(8,128)} %all-gather.10.cloned.1.call-done) | copy-start | bytes 6291460
  85.8 67.5 %all-to-all-start.1 = ((f32[528,2,8,128]{3,1,0,2:T(2,128)}), f32[528,2,8,128]{3,1,0,2:T(2,128)}, u32[]{:S(2)}, u32[]{:S(2)}) async-start(f32[528,2,8,128]{3,1,0,2:T(2,128)} %broadcast_in_dim.34), calls=%async_computation.1 | async-start | bytes 8650752 | tf_op jit(solution)/shard_map/all_to_all | solution.py:41
  90.6 77.3 %all-gather.6.cloned.1.call-start = ((), (), s32[]{:S(2)}) async-start(), calls=%async_computation.6 | async-start | bytes 3244032 | tf_op jit(solution)/shard_map/all_gather | solution.py:63
  92.9 0.6 copy-start.8
  154.8 18.4 %all-to-all-start.3 = ((f32[64,8,128]{2,0,1:T(8,128)}), f32[64,8,128]{2,0,1:T(8,128)}, u32[]{:S(2)}, u32[]{:S(2)}) async-start(f32[64,8,128]{2,0,1:T(8,128)} %broadcast_in_dim.36), calls=%async_computation.3 | async-start | bytes 524288 | tf_op jit(solution)/shard_map/all_to_all | solution.py:60
  168.9 1.0 copy-start.3
  168.9 1.2 copy-start.4
  170.3 1.6 slice-start
  170.3 1.7 copy-start.2
  178.1 17.2 %all-to-all-start.4 = ((f32[8,256,64]{1,2,0:T(8,128)}), f32[8,256,64]{1,2,0:T(8,128)}, u32[]{:S(2)}, u32[]{:S(2)}) async-start(f32[8,256,64]{1,2,0:T(8,128)} %fusion.21), calls=%async_computation.4 | async-start | bytes 1048576 | tf_op jit(solution)/shard_map/all_to_all | solution.py:82
  197.0 75.9 %all-to-all-start.5 = ((f32[8,256,704]{1,2,0:T(8,128)}), f32[8,256,704]{1,2,0:T(8,128)}, u32[]{:S(2)}, u32[]{:S(2)}) async-start(f32[8,256,704]{1,2,0:T(8,128)} %fusion.20), calls=%async_computation.5 | async-start | bytes 11534336 | tf_op jit(solution)/shard_map/all_to_all | solution.py:91
  202.1 61.6 %all-gather.8.cloned.1.call-start = ((), (), s32[]{:S(2)}) async-start(), calls=%async_computation.7 | async-start | bytes 2162688 | tf_op jit(solution)/shard_map/all_gather | solution.py:84
  276.0 0.8 copy-start.7
Sparse Core Ops, SparseCore 0:
  10.0 60.2 all-gather.9
  94.3 61.6 all-gather.5
  205.5 58.1 all-gather.7

commit v20 on v19

--- a/solution.py
+++ b/solution.py
@@ -32,8 +32,8 @@
     gathered = lax.all_gather(lower[0], "col", axis=0, tiled=True)
 
     trail_count = cols_here - strip_width
-    chunk = trail_count // 4
-    bounds = [0, chunk, trail_count]
+    chunk = trail_count // 8
+    bounds = [index * chunk for index in range(8)] + [trail_count]
     left_chunks = []
     for lo, hi in zip(bounds[:-1], bounds[1:]):
         trail_part = lower[1:].reshape(trail_count, 2, 1, row_run)[lo:hi]

time: 289 us -> 328 us (1.13)
  blocking collectives: 40 us -> 104 us
  waiting for transfers between devices: 139 us -> 109 us
  local copies, waits for them, and re-layouts: 32.4 us -> 37.5 us
    all_to_all x0 -> x5, blocking collectives: none -> 68.1 us  [the longest x4 58.4 us: local(): lax.all_to_all(copies, 'row', split_axis=2, concat_axis=2, tiled=True)]
    all_to_all x2 -> x4, waiting for transfers between devices: 58.1 us -> 17.9 us  [local(): lax.all_to_all(copies, 'row', split_axis=2, concat_axis=2, tiled=True)]
    all_gather x1, waiting for transfers between devices: 60.9 us -> 84.8 us  [local(): everything = lax.all_gather(solved_lead, 'col', axis=0, tiled=True)]
    all_gather x1, waiting for transfers between devices: 11.7 us -> 0.02 us  [local(): gathered = lax.all_gather(lower[0], 'col', axis=0, tiled=True)]
    all_to_all x2 -> x4, starting transfers between devices: 11.1 us -> 18.3 us  [local(): lax.all_to_all(copies, 'row', split_axis=2, concat_axis=2, tiled=True)]
    reshape x0 -> x3, local copies, waits for them, and re-layouts: none -> 6.1 us  [local(): left_chunks.append(moved.reshape(hi - lo, 2 * block_size))]
    all_to_all x1 -> x0, waiting for transfers between devices: 6.03 us -> none  [local(): lax.all_to_all(cross_copies, 'row', split_axis=1, concat_axis=1, tiled=True)]
    all_gather x1, waiting for transfers between devices: 0.01 us -> 5.13 us  [local(): joined = lax.all_gather(joined, 'col', axis=0, tiled=True)]
  transfers between devices with their start and end apart: 9 -> 10, of which waited for: 5 -> 5; matrix products, arithmetic and copies ran while one was open for 14% -> 16% of each run, Pallas kernels for 0% -> 0%
where the time goes in v20:
time: 328 us; the launch traced here: 327 us
  waiting for transfers between devices  109 us (33%)
  blocking collectives  104 us (32%)
  local copies, waits for them, and re-layouts  37.5 us (11%)
  starting transfers between devices  32 us (10%)
  matrix products  24.3 us (7%)
  between operations  13.5 us (4%)
  other arithmetic  6.87 us (2%)
    all_gather x1, waiting for transfers between devices, local(): everything = lax.all_gather(solved_lead, 'col', axis=0, tiled=True)  84.8 us
    all_to_all x4, blocking collectives, local(): lax.all_to_all(copies, 'row', split_axis=2, concat_axis=2, tiled=True)  58.4 us
    all_gather x1, blocking collectives, local(): own_rows = lax.all_gather(lower[0], 'row', axis=2, tiled=True)  35.8 us
    all_to_all x4, starting transfers between devices, local(): lax.all_to_all(copies, 'row', split_axis=2, concat_axis=2, tiled=True)  18.3 us
    all_to_all x4, waiting for transfers between devices, local(): lax.all_to_all(copies, 'row', split_axis=2, concat_axis=2, tiled=True)  17.9 us
    dot_general x5, matrix products, times_rows(): jnp.dot(coeff, right_side, precision=highest, preferred_element_type=jnp....  13.7 us
    dot_general x2, matrix products, times_rows_turned(): lax.dot_general(coeff, right_turned, (((1,), (1,)), ((), ())), precision=...  10.6 us
    all_to_all x1, blocking collectives, local(): lax.all_to_all(cross_copies, 'row', split_axis=1, concat_axis=1, tiled=True)  9.77 us
  transfers between devices with their start and end apart: 10, of which 5 were waited for; matrix products, arithmetic and copies ran while one was open for 16% of the time, Pallas kernels for 0%

profile of v20, /device:TPU:1, one launch (start us, length us, event | category | flops | bytes accessed | tf_op | source)
XLA Modules:
  0.0 326.5 jit_solution(3678142320538490279)
XLA Ops:
  6.5 1.2 slice.69
  8.5 1.0 broadcast_in_dim.74
  9.5 6.4 %all-to-all-start = ((f32[88,2,8,128]{3,1,0,2:T(2,128)}), f32[88,2,8,128]{3,1,0,2:T(2,128)S(1)}, u32[]{:S(2)}, u32[]{:S(2)}) async-start(f32[88,2,8,128]{3,1,0,2:T(2,128)} %broadcast_in_dim.74), calls=%async_computation | async-start | bytes 1441792 | tf_op jit(solution)/shard_map/all_to_all | solution.py:41
  16.6 9.4 %all-to-all-done = f32[88,2,8,128]{3,1,0,2:T(2,128)S(1)} async-done(((f32[88,2,8,128]{3,1,0,2:T(2,128)}), f32[88,2,8,128]{3,1,0,2:T(2,128)S(1)}, u32[]{:S(2)}, u32[]{:S(2)}) %all-to-all-start) | async-done | bytes 720928 | tf_op jit(solution)/shard_map/all_to_all | solution.py:41
  26.2 16.6 %all_to_all.60 = f32[88,2,8,128]{3,1,0,2:T(2,128)S(1)} all-to-all(f32[88,2,8,128]{3,1,0,2:T(2,128)S(1)} %broadcast_in_dim.86), channel_id=1, replica_groups=mesh['row'=8,'col'=32] {'row'}, dimensions={2} | all-to-all | bytes 1441792 | tf_op jit(solution)/shard_map/all_to_all | solution.py:41
  43.0 12.3 %all_to_all.61 = f32[88,2,8,128]{3,1,0,2:T(2,128)S(1)} all-to-all(f32[88,2,8,128]{3,1,0,2:T(2,128)S(1)} %broadcast_in_dim.88), channel_id=1, replica_groups=mesh['row'=8,'col'=32] {'row'}, dimensions={2} | all-to-all | bytes 1441792 | tf_op jit(solution)/shard_map/all_to_all | solution.py:41
  55.4 1.0 broadcast_in_dim.82
  56.4 3.5 %all-to-all-start.4 = ((f32[88,2,8,128]{3,1,0,2:T(2,128)}), f32[88,2,8,128]{3,1,0,2:T(2,128)S(1)}, u32[]{:S(2)}, u32[]{:S(2)}) async-start(f32[88,2,8,128]{3,1,0,2:T(2,128)} %broadcast_in_dim.82), calls=%async_computation.4 | async-start | bytes 1441792 | tf_op jit(solution)/shard_map/all_to_all | solution.py:41
  60.0 35.8 %all-gather.1 = f32[1,64,2,1024]{3,1,2,0:T(8,128)} all-gather(f32[1,64,2,128]{3,1,2,0:T(8,128)S(1)} %copy-done.12), channel_id=3, replica_groups=mesh['row'=8,'col'=32] {'row'}, dimensions={3}, use_global_device_ids=true | all-gather | bytes 589824 | tf_op jit(solution)/shard_map/all_gather | solution.py:50
  96.3 1.5 convolution_bitcast_fusion
  97.9 9.8 %all_to_all.62 = f32[64,8,128]{2,0,1:T(8,128)S(1)} all-to-all(f32[64,8,128]{2,0,1:T(8,128)S(1)} %broadcast_in_dim.89), channel_id=1, replica_groups=mesh['row'=8,'col'=32] {'row'}, dimensions={1} | all-to-all | bytes 524288 | tf_op jit(solution)/shard_map/all_to_all | solution.py:56
  107.6 2.0 broadcast_in_dim.84
  109.6 4.2 %all-to-all-start.5 = ((f32[88,2,8,128]{3,1,0,2:T(2,128)}), f32[88,2,8,128]{3,1,0,2:T(2,128)}, u32[]{:S(2)}, u32[]{:S(2)}) async-start(f32[88,2,8,128]{3,1,0,2:T(2,128)} %broadcast_in_dim.84), calls=%async_computation.5 | async-start | bytes 1441792 | tf_op jit(solution)/shard_map/all_to_all | solution.py:41
  113.9 1.5 fusion.9
  116.1 5.7 %all-to-all-done.5 = f32[88,2,8,128]{3,1,0,2:T(2,128)} async-done(((f32[88,2,8,128]{3,1,0,2:T(2,128)}), f32[88,2,8,128]{3,1,0,2:T(2,128)}, u32[]{:S(2)}, u32[]{:S(2)}) %all-to-all-start.5) | async-done | bytes 720928 | tf_op jit(solution)/shard_map/all_to_all | solution.py:41
  121.8 1.1 broadcast_in_dim.78
  122.9 12.5 %all_to_all.63 = f32[88,2,8,128]{3,1,0,2:T(2,128)} all-to-all(f32[88,2,8,128]{3,1,0,2:T(2,128)S(1)} %broadcast_in_dim.78), channel_id=1, replica_groups=mesh['row'=8,'col'=32] {'row'}, dimensions={2} | all-to-all | bytes 1441792 | tf_op jit(solution)/shard_map/all_to_all | solution.py:41
  135.6 16.9 %all_to_all.64 = f32[88,2,8,128]{3,1,0,2:T(2,128)} all-to-all(f32[88,2,8,128]{3,1,0,2:T(2,128)S(1)} %broadcast_in_dim.76), channel_id=1, replica_groups=mesh['row'=8,'col'=32] {'row'}, dimensions={2} | all-to-all | bytes 1441792 | tf_op jit(solution)/shard_map/all_to_all | solution.py:41
  152.5 1.0 broadcast_in_dim.80
  153.5 4.2 %all-to-all-start.3 = ((f32[88,2,8,128]{3,1,0,2:T(2,128)}), f32[88,2,8,128]{3,1,0,2:T(2,128)}, u32[]{:S(2)}, u32[]{:S(2)}) async-start(f32[88,2,8,128]{3,1,0,2:T(2,128)} %broadcast_in_dim.80), calls=%async_computation.3 | async-start | bytes 1441792 | tf_op jit(solution)/shard_map/all_to_all | solution.py:41
  157.8 1.3 copy.11
  159.1 1.1 copy.50
  160.2 1.1 copy.16
  161.3 1.2 copy.17
  162.7 2.5 copy.15
  165.4 2.8 all-to-all-done.3
  168.2 1.4 copy.13
  169.6 2.8 copy_bitcast_fusion
  172.4 1.7 copy_bitcast_fusion.2
  174.1 1.7 copy_bitcast_fusion.4
  176.5 4.2 %all-to-all-start.9 = ((f32[64,8,128]{2,0,1:T(8,128)}), f32[64,8,128]{2,0,1:T(8,128)}, u32[]{:S(2)}, u32[]{:S(2)}) async-start(f32[64,8,128]{2,0,1:T(8,128)} %broadcast_in_dim.90), calls=%async_computation.9 | async-start | bytes 524288 | tf_op jit(solution)/shard_map/all_to_all | solution.py:60
  180.8 5.1 %all-gather.6.cloned.1.call-done = f32[2048,384]{1,0:T(8,128)} async-done(((f32[64,384]{1,0:T(8,128)}), f32[2048,384]{1,0:T(8,128)}) %all-gather.6.cloned.1.call-update) | async-done | bytes 3145744 | tf_op jit(solution)/shard_map/all_gather | solution.py:63
  185.9 1.1 slice_negate_fusion
  187.4 1.2 slice-done
  188.6 1.3 fusion.3
  189.9 2.0 fusion.1
  191.9 3.0 fusion.16
  194.9 4.2 %all-to-all-start.10 = ((f32[8,256,64]{1,2,0:T(8,128)}), f32[8,256,64]{1,2,0:T(8,128)}, u32[]{:S(2)}, u32[]{:S(2)}) async-start(f32[8,256,64]{1,2,0:T(8,128)} %fusion.16), calls=%async_computation.10 | async-start | bytes 1048576 | tf_op jit(solution)/shard_map/all_to_all | solution.py:82
  199.0 1.5 reshape.74
  200.5 7.7 %fusion.15 = f32[8,256,704]{1,2,0:T(8,128)} fusion(f32[8,256,256]{2,1,0:T(8,128)S(1)} %bitcast.104, f32[704,256,1]{1,0,2:T(8,128)} %reshape.74), kind=kOutput, calls=%fused_computation.51 | convolution fusion | flops 4429185024 | bytes 8585216 | tf_op jit(solution)/shard_map/dot_general | solution.py:14
  208.1 1.7 reduce_sum.18
  209.8 5.2 %all-to-all-start.11 = ((f32[8,256,704]{1,2,0:T(8,128)}), f32[8,256,704]{1,2,0:T(8,128)}, u32[]{:S(2)}, u32[]{:S(2)}) async-start(f32[8,256,704]{1,2,0:T(8,128)} %fusion.15), calls=%async_computation.11 | async-start | bytes 11534336 | tf_op jit(solution)/shard_map/all_to_all | solution.py:91
  216.7 1.0 constant_dynamic-update-slice_fusion.6
  217.7 0.9 constant_dynamic-update-slice_fusion.5
  223.3 84.8 %all-gather.8.cloned.1.call-done = f32[2048,256]{1,0:T(8,128)} async-done(((f32[64,256]{1,0:T(8,128)}), f32[2048,256]{1,0:T(8,128)}) %all-gather.8.cloned.1.call-update) | async-done | bytes 2097168 | tf_op jit(solution)/shard_map/all_gather | solution.py:84
  308.0 7.4 %fusion.17 = f32[704,256]{1,0:T(8,128)S(1)} fusion(f32[704,2048]{1,0:T(8,128)} %constant_dynamic-update-slice_fusion, f32[2048,256]{1,0:T(8,128)} %all-gather.8.cloned.1.call-done), kind=kOutput, calls=%fused_computation.53 | convolution fusion | flops 4429185024 | bytes 8585216 | tf_op jit(solution)/shard_map/dot_general | solution.py:10
  315.5 3.1 reduce_sum.19
  318.7 1.3 reshape.69
  (74 shorter events, 11.4 us)
Async XLA Ops:
  6.5 9.4 %slice-start.3 = ((f32[12,64,2,128]{3,2,1,0:T(2,128)}), f32[1,64,2,128]{3,2,1,0:T(2,128)S(1)}, s32[]{:S(2)}) async-start(f32[12,64,2,128]{3,2,1,0:T(2,128)} %param.3), calls=%async_computation.18 | async-start | bytes 131072 | tf_op jit(solution)/shard_map/slice | solution.py:32
  9.5 16.5 %all-to-all-start = ((f32[88,2,8,128]{3,1,0,2:T(2,128)}), f32[88,2,8,128]{3,1,0,2:T(2,128)S(1)}, u32[]{:S(2)}, u32[]{:S(2)}) async-start(f32[88,2,8,128]{3,1,0,2:T(2,128)} %broadcast_in_dim.74), calls=%async_computation | async-start | bytes 1441792 | tf_op jit(solution)/shard_map/all_to_all | solution.py:41
  15.9 80.4 %all-gather.10.cloned.1.call-start = ((), (), s32[]{:S(2)}) async-start(), calls=%async_computation.14 | async-start | bytes 2162688 | tf_op jit(solution)/shard_map/all_gather | solution.py:32
  26.2 33.8 %copy-start.12 = (f32[1,64,2,128]{3,1,2,0:T(8,128)S(1)}, f32[1,64,2,128]{3,1,2,0:T(8,128)}, u32[]{:S(2)}) copy-start(f32[1,64,2,128]{3,1,2,0:T(8,128)} %copy.21) | copy-start | bytes 196612
  56.4 41.4 %all-to-all-start.4 = ((f32[88,2,8,128]{3,1,0,2:T(2,128)}), f32[88,2,8,128]{3,1,0,2:T(2,128)S(1)}, u32[]{:S(2)}, u32[]{:S(2)}) async-start(f32[88,2,8,128]{3,1,0,2:T(2,128)} %broadcast_in_dim.82), calls=%async_computation.4 | async-start | bytes 1441792 | tf_op jit(solution)/shard_map/all_to_all | solution.py:41
  96.0 17.9 %slice-start.1 = ((f32[12,64,2,128]{3,2,1,0:T(2,128)}), f32[1,64,2,128]{3,2,1,0:T(2,128)S(1)}, s32[]{:S(2)}) async-start(f32[12,64,2,128]{3,2,1,0:T(2,128)} %param.2), calls=%async_computation.16 | async-start | bytes 131072 | tf_op jit(solution)/shard_map/slice | solution.py:62
  107.6 27.8 %copy-start.15 = (f32[88,2,128]{2,1,0:T(2,128)S(1)}, f32[88,2,128]{2,1,0:T(2,128)}, u32[]{:S(2)}) copy-start(f32[88,2,128]{2,1,0:T(2,128)} %get-tuple-element.37) | copy-start | bytes 270340
  109.6 12.2 %all-to-all-start.5 = ((f32[88,2,8,128]{3,1,0,2:T(2,128)}), f32[88,2,8,128]{3,1,0,2:T(2,128)}, u32[]{:S(2)}, u32[]{:S(2)}) async-start(f32[88,2,8,128]{3,1,0,2:T(2,128)} %broadcast_in_dim.84), calls=%async_computation.5 | async-start | bytes 1441792 | tf_op jit(solution)/shard_map/all_to_all | solution.py:41
  113.8 38.6 %copy-start.14 = (f32[88,2,128]{2,1,0:T(2,128)S(1)}, f32[88,2,128]{2,1,0:T(2,128)}, u32[]{:S(2)}) copy-start(f32[88,2,128]{2,1,0:T(2,128)} %get-tuple-element.35) | copy-start | bytes 270340
  113.8 72.1 %all-gather.6.cloned.1.call-start = ((), (), s32[]{:S(2)}) async-start(), calls=%async_computation.12 | async-start | bytes 3244032 | tf_op jit(solution)/shard_map/all_gather | solution.py:63
  153.5 14.7 %all-to-all-start.3 = ((f32[88,2,8,128]{3,1,0,2:T(2,128)}), f32[88,2,8,128]{3,1,0,2:T(2,128)}, u32[]{:S(2)}, u32[]{:S(2)}) async-start(f32[88,2,8,128]{3,1,0,2:T(2,128)} %broadcast_in_dim.80), calls=%async_computation.3 | async-start | bytes 1441792 | tf_op jit(solution)/shard_map/all_to_all | solution.py:41
  160.2 5.0 %copy-start.1 = (f32[88,2,8,128]{3,1,0,2:T(2,128)S(1)}, f32[88,2,8,128]{3,1,0,2:T(2,128)}, u32[]{:S(2)}) copy-start(f32[88,2,8,128]{3,1,0,2:T(2,128)} %all_to_all.63) | copy-start | bytes 2162692
  162.7 6.9 %copy-start.8 = (f32[88,2,8,128]{3,2,1,0:T(8,128)S(1)}, f32[88,2,8,128]{3,2,1,0:T(8,128)}, u32[]{:S(2)}) copy-start(f32[88,2,8,128]{3,2,1,0:T(8,128)} %copy.16) | copy-start | bytes 2162692
  168.2 4.2 %copy-start.9 = (f32[88,2,8,128]{3,2,1,0:T(8,128)S(1)}, f32[88,2,8,128]{3,2,1,0:T(8,128)}, u32[]{:S(2)}) copy-start(f32[88,2,8,128]{3,2,1,0:T(8,128)} %copy.15) | copy-start | bytes 2162692
  172.4 3.3 %copy-start.10 = (f32[1,2048,2,128]{3,1,2,0:T(8,128)S(1)}, f32[1,2048,2,128]{3,1,2,0:T(8,128)}, u32[]{:S(2)}) copy-start(f32[1,2048,2,128]{3,1,2,0:T(8,128)} %all-gather.10.cloned.1.call-done) | copy-start | bytes 6291460
  176.5 13.4 %all-to-all-start.9 = ((f32[64,8,128]{2,0,1:T(8,128)}), f32[64,8,128]{2,0,1:T(8,128)}, u32[]{:S(2)}, u32[]{:S(2)}) async-start(f32[64,8,128]{2,0,1:T(8,128)} %broadcast_in_dim.90), calls=%async_computation.9 | async-start | bytes 524288 | tf_op jit(solution)/shard_map/all_to_all | solution.py:60
  187.0 1.6 slice-start
  187.0 1.7 copy-start.11
  189.9 9.1 %slice-start.2 = ((f32[12,64,2,128]{3,2,1,0:T(2,128)}), f32[11,64,2,128]{3,2,1,0:T(2,128)S(1)}, s32[]{:S(2)}) async-start(f32[12,64,2,128]{3,2,1,0:T(2,128)} %param.2), calls=%async_computation.17 | async-start | bytes 1441792 | tf_op jit(solution)/shard_map/slice | solution.py:88
  194.9 13.3 %all-to-all-start.10 = ((f32[8,256,64]{1,2,0:T(8,128)}), f32[8,256,64]{1,2,0:T(8,128)}, u32[]{:S(2)}, u32[]{:S(2)}) async-start(f32[8,256,64]{1,2,0:T(8,128)} %fusion.16), calls=%async_computation.10 | async-start | bytes 1048576 | tf_op jit(solution)/shard_map/all_to_all | solution.py:82
  209.8 6.9 %copy-start = (f32[11,8,16,128]{3,1,2,0:T(8,128)S(1)}, f32[11,8,16,128]{3,1,2,0:T(8,128)}, u32[]{:S(2)}) copy-start(f32[11,8,16,128]{3,1,2,0:T(8,128)} %copy.50) | copy-start | bytes 2162692
  209.8 105.6 %all-to-all-start.11 = ((f32[8,256,704]{1,2,0:T(8,128)}), f32[8,256,704]{1,2,0:T(8,128)}, u32[]{:S(2)}, u32[]{:S(2)}) async-start(f32[8,256,704]{1,2,0:T(8,128)} %fusion.15), calls=%async_computation.11 | async-start | bytes 11534336 | tf_op jit(solution)/shard_map/all_to_all | solution.py:91
  215.0 3.6 %copy-start.6 = (f32[88,2048]{1,0:T(8,128)S(1)}, f32[88,2048]{1,0:T(8,128)}, u32[]{:S(2)}) copy-start(f32[88,2048]{1,0:T(8,128)} %get-tuple-element.24) | copy-start | bytes 2162692
  215.0 4.5 %copy-start.5 = (f32[88,2048]{1,0:T(8,128)S(1)}, f32[88,2048]{1,0:T(8,128)}, u32[]{:S(2)}) copy-start(f32[88,2048]{1,0:T(8,128)} %get-tuple-element.25) | copy-start | bytes 2162692
  215.0 93.0 %all-gather.8.cloned.1.call-start = ((), (), s32[]{:S(2)}) async-start(), calls=%async_computation.13 | async-start | bytes 2162688 | tf_op jit(solution)/shard_map/all_gather | solution.py:84
  215.8 1.9 copy-start.7
  216.7 3.8 %copy-start.4 = (f32[88,2048]{1,0:T(8,128)S(1)}, f32[88,2048]{1,0:T(8,128)}, u32[]{:S(2)}) copy-start(f32[88,2048]{1,0:T(8,128)} %get-tuple-element.26) | copy-start | bytes 2162692
  217.7 3.7 %copy-start.3 = (f32[88,2048]{1,0:T(8,128)S(1)}, f32[88,2048]{1,0:T(8,128)}, u32[]{:S(2)}) copy-start(f32[88,2048]{1,0:T(8,128)} %get-tuple-element.27) | copy-start | bytes 2162692
  218.6 3.7 %copy-start.2 = (f32[88,2048]{1,0:T(8,128)S(1)}, f32[88,2048]{1,0:T(8,128)}, u32[]{:S(2)}) copy-start(f32[88,2048]{1,0:T(8,128)} %get-tuple-element.28) | copy-start | bytes 2162692
  315.4 3.2 copy-start.13
Sparse Core Ops, SparseCore 0:
  19.3 58.2 all-gather.9
  117.2 68.6 all-gather.5
  218.4 89.5 all-gather.7

commit v21 on v20

--- a/solution.py
+++ b/solution.py
@@ -33,7 +33,7 @@
 
     trail_count = cols_here - strip_width
     chunk = trail_count // 8
-    bounds = [index * chunk for index in range(8)] + [trail_count]
+    bounds = [0, 3 * chunk, 5 * chunk, 7 * chunk, trail_count]
     left_chunks = []
     for lo, hi in zip(bounds[:-1], bounds[1:]):
         trail_part = lower[1:].reshape(trail_count, 2, 1, row_run)[lo:hi]

time: 328 us -> 302 us (0.921)
  blocking collectives: 104 us -> 63.3 us
  waiting for transfers between devices: 109 us -> 138 us
  local copies, waits for them, and re-layouts: 37.5 us -> 25.3 us
    all_to_all x4 -> x1, blocking collectives: 58.4 us -> 15.5 us  [local(): lax.all_to_all(copies, 'row', split_axis=2, concat_axis=2, tiled=True)]
    all_gather x1, waiting for transfers between devices: 5.13 us -> 23.3 us  [local(): joined = lax.all_gather(joined, 'col', axis=0, tiled=True)]
    all_gather x1, blocking collectives: 35.8 us -> 47.8 us  [local(): own_rows = lax.all_gather(lower[0], 'row', axis=2, tiled=True)]
    all_to_all x1 -> x0, blocking collectives: 9.77 us -> none  [local(): lax.all_to_all(cross_copies, 'row', split_axis=1, concat_axis=1, tiled=True)]
    all_gather x1, waiting for transfers between devices: 84.8 us -> 91 us  [local(): everything = lax.all_gather(solved_lead, 'col', axis=0, tiled=True)]
    all_to_all x0 -> x1, waiting for transfers between devices: none -> 6.07 us  [local(): lax.all_to_all(cross_copies, 'row', split_axis=1, concat_axis=1, tiled=True)]
    all_to_all x4 -> x3, starting transfers between devices: 18.3 us -> 13.6 us  [local(): lax.all_to_all(copies, 'row', split_axis=2, concat_axis=2, tiled=True)]
    all_to_all x0 -> x1, starting transfers between devices: none -> 4 us  [local(): lax.all_to_all(cross_copies, 'row', split_axis=1, concat_axis=1, tiled=True)]
  transfers between devices with their start and end apart: 10 -> 10, of which waited for: 5 -> 7; matrix products, arithmetic and copies ran while one was open for 16% -> 12% of each run, Pallas kernels for 0% -> 0%
where the time goes in v21:
time: 302 us; the launch traced here: 301 us
  waiting for transfers between devices  138 us (46%)
  blocking collectives  63.3 us (21%)
  starting transfers between devices  30.8 us (10%)
  local copies, waits for them, and re-layouts  25.3 us (8%)
  matrix products  23 us (8%)
  between operations  13.4 us (4%)
  other arithmetic  6.93 us (2%)
    all_gather x1, waiting for transfers between devices, local(): everything = lax.all_gather(solved_lead, 'col', axis=0, tiled=True)  91 us
    all_gather x1, blocking collectives, local(): own_rows = lax.all_gather(lower[0], 'row', axis=2, tiled=True)  47.8 us
    all_gather x1, waiting for transfers between devices, local(): joined = lax.all_gather(joined, 'col', axis=0, tiled=True)  23.3 us
    all_to_all x1, blocking collectives, local(): lax.all_to_all(copies, 'row', split_axis=2, concat_axis=2, tiled=True)  15.5 us
    all_to_all x3, waiting for transfers between devices, local(): lax.all_to_all(copies, 'row', split_axis=2, concat_axis=2, tiled=True)  14.8 us
    all_to_all x3, starting transfers between devices, local(): lax.all_to_all(copies, 'row', split_axis=2, concat_axis=2, tiled=True)  13.6 us
    dot_general x5, matrix products, times_rows(): jnp.dot(coeff, right_side, precision=highest, preferred_element_type=jnp....  13.4 us
    dot_general x2, matrix products, times_rows_turned(): lax.dot_general(coeff, right_turned, (((1,), (1,)), ((), ())), precision=...  9.55 us
  transfers between devices with their start and end apart: 10, of which 7 were waited for; matrix products, arithmetic and copies ran while one was open for 12% of the time, Pallas kernels for 0%

profile of v21, /device:TPU:1, one launch (start us, length us, event | category | flops | bytes accessed | tf_op | source)
XLA Modules:
  0.0 300.8 jit_solution(9265260802030679530)
XLA Ops:
  6.5 0.8 slice.55
  7.4 0.6 copy.17
  8.0 1.2 slice.53
  9.2 1.9 broadcast_in_dim.46
  11.2 6.5 %all-to-all-start = ((f32[264,2,8,128]{3,1,0,2:T(2,128)}), f32[264,2,8,128]{3,1,0,2:T(2,128)S(1)}, u32[]{:S(2)}, u32[]{:S(2)}) async-start(f32[264,2,8,128]{3,1,0,2:T(2,128)} %broadcast_in_dim.46), calls=%async_computation | async-start | bytes 4325376 | tf_op jit(solution)/shard_map/all_to_all | solution.py:41
  17.7 47.8 %all-gather.1 = f32[1,64,2,1024]{3,1,2,0:T(8,128)S(1)} all-gather(f32[1,64,2,128]{3,1,2,0:T(8,128)S(1)} %copy-done.6), channel_id=3, replica_groups=mesh['row'=8,'col'=32] {'row'}, dimensions={3}, use_global_device_ids=true | all-gather | bytes 589824 | tf_op jit(solution)/shard_map/all_gather | solution.py:50
  65.5 0.7 copy.9
  66.2 2.3 copy.38
  68.6 1.0 all-gather.10.cloned.1.call-done
  69.6 1.5 convolution_bitcast_fusion
  71.1 0.7 broadcast_in_dim.53
  71.8 4.0 %all-to-all-start.4 = ((f32[64,8,128]{2,0,1:T(8,128)}), f32[64,8,128]{2,0,1:T(8,128)S(1)}, u32[]{:S(2)}, u32[]{:S(2)}) async-start(f32[64,8,128]{2,0,1:T(8,128)} %broadcast_in_dim.53), calls=%async_computation.4 | async-start | bytes 524288 | tf_op jit(solution)/shard_map/all_to_all | solution.py:56
  75.8 6.1 %all-to-all-done.4 = f32[64,8,128]{2,0,1:T(8,128)S(1)} async-done(((f32[64,8,128]{2,0,1:T(8,128)}), f32[64,8,128]{2,0,1:T(8,128)S(1)}, u32[]{:S(2)}, u32[]{:S(2)}) %all-to-all-start.4) | async-done | bytes 262176 | tf_op jit(solution)/shard_map/all_to_all | solution.py:56
  81.9 1.0 broadcast_in_dim.52
  82.9 3.5 %all-to-all-start.3 = ((f32[88,2,8,128]{3,1,0,2:T(2,128)}), f32[88,2,8,128]{3,1,0,2:T(2,128)S(1)}, u32[]{:S(2)}, u32[]{:S(2)}) async-start(f32[88,2,8,128]{3,1,0,2:T(2,128)} %broadcast_in_dim.52), calls=%async_computation.3 | async-start | bytes 1441792 | tf_op jit(solution)/shard_map/all_to_all | solution.py:41
  86.6 1.5 fusion.17
  88.0 0.6 pad_maximum_fusion.1
  88.7 5.6 %all-to-all-done.3 = f32[88,2,8,128]{3,1,0,2:T(2,128)S(1)} async-done(((f32[88,2,8,128]{3,1,0,2:T(2,128)}), f32[88,2,8,128]{3,1,0,2:T(2,128)S(1)}, u32[]{:S(2)}, u32[]{:S(2)}) %all-to-all-start.3) | async-done | bytes 720928 | tf_op jit(solution)/shard_map/all_to_all | solution.py:41
  94.4 0.9 copy-done.1
  95.6 15.5 %all_to_all.40 = f32[176,2,8,128]{3,1,0,2:T(2,128)S(1)} all-to-all(f32[176,2,8,128]{3,1,0,2:T(2,128)S(1)} %broadcast_in_dim.50), channel_id=1, replica_groups=mesh['row'=8,'col'=32] {'row'}, dimensions={2} | all-to-all | bytes 2883584 | tf_op jit(solution)/shard_map/all_to_all | solution.py:41
  111.1 1.5 broadcast_in_dim.48
  112.6 3.6 %all-to-all-start.1 = ((f32[176,2,8,128]{3,1,0,2:T(2,128)}), f32[176,2,8,128]{3,1,0,2:T(2,128)S(1)}, u32[]{:S(2)}, u32[]{:S(2)}) async-start(f32[176,2,8,128]{3,1,0,2:T(2,128)} %broadcast_in_dim.48), calls=%async_computation.1 | async-start | bytes 2883584 | tf_op jit(solution)/shard_map/all_to_all | solution.py:41
  116.2 1.3 copy.13
  117.6 1.1 copy.39
  118.7 2.0 copy.12
  120.6 9.1 %all-to-all-done.1 = f32[176,2,8,128]{3,1,0,2:T(2,128)S(1)} async-done(((f32[176,2,8,128]{3,1,0,2:T(2,128)}), f32[176,2,8,128]{3,1,0,2:T(2,128)S(1)}, u32[]{:S(2)}, u32[]{:S(2)}) %all-to-all-start.1) | async-done | bytes 1441824 | tf_op jit(solution)/shard_map/all_to_all | solution.py:41
  129.8 0.8 copy.11
  130.6 2.9 copy_bitcast_fusion.1
  133.6 0.7 broadcast_in_dim.54
  134.3 3.8 %all-to-all-start.5 = ((f32[64,8,128]{2,0,1:T(8,128)}), f32[64,8,128]{2,0,1:T(8,128)S(1)}, u32[]{:S(2)}, u32[]{:S(2)}) async-start(f32[64,8,128]{2,0,1:T(8,128)} %broadcast_in_dim.54), calls=%async_computation.5 | async-start | bytes 524288 | tf_op jit(solution)/shard_map/all_to_all | solution.py:60
  138.1 23.3 %all-gather.6.cloned.1.call-done = f32[2048,384]{1,0:T(8,128)} async-done(((f32[64,384]{1,0:T(8,128)}), f32[2048,384]{1,0:T(8,128)}) %all-gather.6.cloned.1.call-update) | async-done | bytes 3145744 | tf_op jit(solution)/shard_map/all_gather | solution.py:63
  161.4 1.1 slice_negate_fusion
  162.8 1.4 slice-done
  164.2 0.6 fusion.11
  164.9 1.9 fusion.9
  166.8 3.0 fusion.25
  169.7 4.1 %all-to-all-start.6 = ((f32[8,256,64]{1,2,0:T(8,128)}), f32[8,256,64]{1,2,0:T(8,128)}, u32[]{:S(2)}, u32[]{:S(2)}) async-start(f32[8,256,64]{1,2,0:T(8,128)} %fusion.25), calls=%async_computation.6 | async-start | bytes 1048576 | tf_op jit(solution)/shard_map/all_to_all | solution.py:82
  173.9 0.6 reshape.54
  174.5 6.6 %fusion.24 = f32[8,256,704]{1,2,0:T(8,128)} fusion(f32[8,256,256]{2,1,0:T(8,128)S(1)} %bitcast.79, f32[704,256,1]{1,0,2:T(8,128)S(1)} %reshape.54), kind=kOutput, calls=%fused_computation.44 | convolution fusion | flops 4429185024 | bytes 8585216 | tf_op jit(solution)/shard_map/dot_general | solution.py:14
  181.1 1.5 all-to-all-done.6
  182.5 1.7 reduce_sum.18
  184.2 5.0 %all-to-all-start.7 = ((f32[8,256,704]{1,2,0:T(8,128)}), f32[8,256,704]{1,2,0:T(8,128)}, u32[]{:S(2)}, u32[]{:S(2)}) async-start(f32[8,256,704]{1,2,0:T(8,128)} %fusion.24), calls=%async_computation.7 | async-start | bytes 11534336 | tf_op jit(solution)/shard_map/all_to_all | solution.py:91
  189.5 0.5 all-gather.8.cloned.1.call-update
  189.9 91.0 %all-gather.8.cloned.1.call-done = f32[2048,256]{1,0:T(8,128)} async-done(((f32[64,256]{1,0:T(8,128)}), f32[2048,256]{1,0:T(8,128)}) %all-gather.8.cloned.1.call-update) | async-done | bytes 2097168 | tf_op jit(solution)/shard_map/all_gather | solution.py:84
  281.0 8.0 %fusion = f32[704,256]{1,0:T(8,128)} fusion(f32[2048,256]{1,0:T(8,128)} %all-gather.8.cloned.1.call-done, f32[88,2048]{1,0:T(8,128)S(1)} %bitcast.94, f32[176,2048]{1,0:T(8,128)} %get-tuple-element.19, f32[176,2048]{1,0:T(8,128)} %get-tuple-element.18, f32[264,2048]{1,0:T(8,128)S(1)} %bitcast.89), kind=kOutput, calls=%fused_computation | convolution fusion | flops 4433510400 | bytes 8585216 | tf_op jit(solution)/shard_map/dot_general | solution.py:10
  288.9 3.2 %reduce_sum.19 = f32[256,704]{0,1:T(8,128)S(1)} reduce(f32[8,256,704]{1,2,0:T(8,128)} %all-to-all-done.7, f32[]{:T(128)} %constant.13.clone.1), dimensions={0}, to_apply=%region_1.2 | reduce | flops 1261568 | bytes 6488068 | tf_op jit(solution)/shard_map/reduce_sum | solution.py:92
  292.2 0.7 copy-done.7
  293.0 1.3 reshape.49
  (37 shorter events, 1.4 us)
Async XLA Ops:
  6.5 63.0 %all-gather.10.cloned.1.call-start = ((), (), s32[]{:S(2)}) async-start(), calls=%async_computation.10 | async-start | bytes 2162688 | tf_op jit(solution)/shard_map/all_gather | solution.py:32
  11.2 6.5 %copy-start.6 = (f32[1,64,2,128]{3,1,2,0:T(8,128)S(1)}, f32[1,64,2,128]{3,1,2,0:T(8,128)}, u32[]{:S(2)}) copy-start(f32[1,64,2,128]{3,1,2,0:T(8,128)} %copy.17) | copy-start | bytes 196612
  11.2 54.4 %all-to-all-start = ((f32[264,2,8,128]{3,1,0,2:T(2,128)}), f32[264,2,8,128]{3,1,0,2:T(2,128)S(1)}, u32[]{:S(2)}, u32[]{:S(2)}) async-start(f32[264,2,8,128]{3,1,0,2:T(2,128)} %broadcast_in_dim.46), calls=%async_computation | async-start | bytes 4325376 | tf_op jit(solution)/shard_map/all_to_all | solution.py:41
  69.6 17.0 %slice-start.1 = ((f32[12,64,2,128]{3,2,1,0:T(2,128)}), f32[1,64,2,128]{3,2,1,0:T(2,128)S(1)}, s32[]{:S(2)}) async-start(f32[12,64,2,128]{3,2,1,0:T(2,128)} %param.2), calls=%async_computation.12 | async-start | bytes 131072 | tf_op jit(solution)/shard_map/slice | solution.py:62
  71.8 10.1 %all-to-all-start.4 = ((f32[64,8,128]{2,0,1:T(8,128)}), f32[64,8,128]{2,0,1:T(8,128)S(1)}, u32[]{:S(2)}, u32[]{:S(2)}) async-start(f32[64,8,128]{2,0,1:T(8,128)} %broadcast_in_dim.53), calls=%async_computation.4 | async-start | bytes 524288 | tf_op jit(solution)/shard_map/all_to_all | solution.py:56
  82.9 11.4 %all-to-all-start.3 = ((f32[88,2,8,128]{3,1,0,2:T(2,128)}), f32[88,2,8,128]{3,1,0,2:T(2,128)S(1)}, u32[]{:S(2)}, u32[]{:S(2)}) async-start(f32[88,2,8,128]{3,1,0,2:T(2,128)} %broadcast_in_dim.52), calls=%async_computation.3 | async-start | bytes 1441792 | tf_op jit(solution)/shard_map/all_to_all | solution.py:41
  86.5 74.9 %all-gather.6.cloned.1.call-start = ((), (), s32[]{:S(2)}) async-start(), calls=%async_computation.8 | async-start | bytes 3244032 | tf_op jit(solution)/shard_map/all_gather | solution.py:63
  94.4 0.9 copy-start.1
  112.6 17.1 %all-to-all-start.1 = ((f32[176,2,8,128]{3,1,0,2:T(2,128)}), f32[176,2,8,128]{3,1,0,2:T(2,128)S(1)}, u32[]{:S(2)}, u32[]{:S(2)}) async-start(f32[176,2,8,128]{3,1,0,2:T(2,128)} %broadcast_in_dim.48), calls=%async_computation.1 | async-start | bytes 2883584 | tf_op jit(solution)/shard_map/all_to_all | solution.py:41
  120.6 10.0 %copy-start = (f32[176,2,8,128]{3,2,1,0:T(8,128)S(1)}, f32[176,2,8,128]{3,2,1,0:T(8,128)}, u32[]{:S(2)}) copy-start(f32[176,2,8,128]{3,2,1,0:T(8,128)} %copy.12) | copy-start | bytes 4325380
  130.6 2.9 copy-start.3
  134.3 30.6 %all-to-all-start.5 = ((f32[64,8,128]{2,0,1:T(8,128)}), f32[64,8,128]{2,0,1:T(8,128)S(1)}, u32[]{:S(2)}, u32[]{:S(2)}) async-start(f32[64,8,128]{2,0,1:T(8,128)} %broadcast_in_dim.54), calls=%async_computation.5 | async-start | bytes 524288 | tf_op jit(solution)/shard_map/all_to_all | solution.py:60
  162.7 1.6 slice-start
  166.8 7.1 %slice-start.2 = ((f32[12,64,2,128]{3,2,1,0:T(2,128)}), f32[11,64,2,128]{3,2,1,0:T(2,128)S(1)}, s32[]{:S(2)}) async-start(f32[12,64,2,128]{3,2,1,0:T(2,128)} %param.2), calls=%async_computation.13 | async-start | bytes 1441792 | tf_op jit(solution)/shard_map/slice | solution.py:88
  169.7 12.8 %all-to-all-start.6 = ((f32[8,256,64]{1,2,0:T(8,128)}), f32[8,256,64]{1,2,0:T(8,128)}, u32[]{:S(2)}, u32[]{:S(2)}) async-start(f32[8,256,64]{1,2,0:T(8,128)} %fusion.25), calls=%async_computation.6 | async-start | bytes 1048576 | tf_op jit(solution)/shard_map/all_to_all | solution.py:82
  184.2 96.7 %copy-start.2 = (f32[33,8,16,128]{3,1,2,0:T(8,128)S(1)}, f32[33,8,16,128]{3,1,2,0:T(8,128)}, u32[]{:S(2)}) copy-start(f32[33,8,16,128]{3,1,2,0:T(8,128)} %copy.38) | copy-start | bytes 6488068
  184.2 96.7 %copy-start.4 = (f32[11,8,16,128]{3,1,2,0:T(8,128)S(1)}, f32[11,8,16,128]{3,1,2,0:T(8,128)}, u32[]{:S(2)}) copy-start(f32[11,8,16,128]{3,1,2,0:T(8,128)} %copy.39) | copy-start | bytes 2162692
  184.2 104.7 %all-to-all-start.7 = ((f32[8,256,704]{1,2,0:T(8,128)}), f32[8,256,704]{1,2,0:T(8,128)}, u32[]{:S(2)}, u32[]{:S(2)}) async-start(f32[8,256,704]{1,2,0:T(8,128)} %fusion.24), calls=%async_computation.7 | async-start | bytes 11534336 | tf_op jit(solution)/shard_map/all_to_all | solution.py:91
  189.2 91.8 %all-gather.8.cloned.1.call-start = ((), (), s32[]{:S(2)}) async-start(), calls=%async_computation.9 | async-start | bytes 2162688 | tf_op jit(solution)/shard_map/all_gather | solution.py:84
  288.9 3.2 %copy-start.5 = (f32[704,256]{1,0:T(8,128)S(1)}, f32[704,256]{1,0:T(8,128)}, u32[]{:S(2)}) copy-start(f32[704,256]{1,0:T(8,128)} %fusion) | copy-start | bytes 2162692
  292.1 0.8 copy-start.7
Sparse Core Ops, SparseCore 0:
  10.0 59.5 all-gather.9
  89.9 71.4 all-gather.5
  192.6 88.3 all-gather.7
